TPU v7x, 512 devices: a whole 4x4x16 slice. The times are simulated.
512 devices in a mesh: rep: 4 (over y), exp: 128 (over x, z, core).
Axes of the slice: x: 4, y: 4, z: 16, core: 2. Of those that a mesh axis runs over, the one named last changes fastest.
Arguments:
- tokens: bfloat16 [16384, 2880], P('exp'), may hold values from -6 to 6
- expert_ids: int32 [16384, 4], P('exp'), may hold values from 0 to 63, all different within a row; in each aligned block of 128 rows (0 to 127, 128 to 255, ...) at most 12 rows name the same one
- gate_levels: int32 [16384, 4], P('exp'), may hold values from 1 to 255
- w_gate: bfloat16 [128, 768, 2880], P('exp', 'rep'), may hold values from -0.109375 to 0.109375
- w_up: bfloat16 [128, 768, 2880], P('exp', 'rep'), may hold values from -0.109375 to 0.109375
- w_down: bfloat16 [128, 1536, 1440], P('exp', None, 'rep'), may hold values from -0.15625 to 0.15625
Outputs:
- moe_out: bfloat16 [16384, 2, 1440], P('exp', None, 'rep')
Inputs may be any that keep to these rules, and one draw needn't show every extreme that they name: `expert_ids`: each row names 4 different experts. Within the rows of one device (aligned blocks of 128 tokens) no expert is named by more than 12 rows, a bound that some block reaches.
All inputs are finite; a program needn't handle non-finite values.
Results may differ from a plain program's by a relative error of at most 0.0057.
Values may be sent and summed in bfloat16 or wider, within the bound.
No kernel may reach another device: no remote copies, remote signals or barrier semaphores. Data moves between devices by JAX's collectives and lax.ppermute only.
A program may use at most 128 MiB of HBM per device.

v0:
```python
import jax
import jax.numpy as jnp
from jax import lax
from jax.sharding import PartitionSpec as P


def from_partner(value, axis, apart):
    mask = 2**apart
    pairs = [(source, source ^ mask) for source in range(lax.axis_size(axis))]
    return lax.ppermute(value, axis, pairs)


def on_device(tokens, expert_ids, gate_levels, w_gate, w_up, w_down):
    tok_rows = tokens.shape[0]
    model_width = tokens.shape[1]
    top_count = expert_ids.shape[1]
    n_shards = lax.axis_size("exp")
    expert_count = n_shards // 2
    capacity = min(tok_rows, max(4, (tok_rows * top_count * 3 // (2 * expert_count) + 3) // 4 * 4))
    flat_ids = expert_ids.reshape(-1)
    onehot = (flat_ids[:, None] == jnp.arange(expert_count, dtype=jnp.int32)[None, :]).astype(
        jnp.int32
    )
    rank_counts = jnp.cumsum(onehot, axis=0) - onehot
    slot_index = jnp.sum(rank_counts * onehot, axis=1)
    target = flat_ids * capacity + slot_index
    source_rows = jnp.arange(tok_rows * top_count, dtype=jnp.int32) // top_count
    packed = (
        jnp.zeros((expert_count * capacity, model_width), tokens.dtype)
        .at[target]
        .set(tokens[source_rows])
    )
    packed = packed.reshape(expert_count, capacity, model_width)
    gate_rows = w_gate[0]
    up_rows = w_up[0]
    down_rows = w_down[0]
    contract = (((1,), (1,)), ((), ()))
    outgoing = jnp.repeat(packed, 2, axis=0)
    arrived = lax.all_to_all(outgoing, "exp", split_axis=0, concat_axis=0, tiled=True)
    flat_rows = arrived.reshape(-1, model_width)
    gate_proj = lax.dot_general(flat_rows, gate_rows, contract, preferred_element_type=jnp.float32)
    up_proj = lax.dot_general(flat_rows, up_rows, contract, preferred_element_type=jnp.float32)
    hidden_part = ((up_proj + 1.0) * gate_proj * jax.nn.sigmoid(1.702 * gate_proj)).astype(
        jnp.bfloat16
    )
    hidden = hidden_part.reshape(arrived.shape[0], arrived.shape[1], gate_rows.shape[0])
    hidden = hidden.reshape(-1, hidden.shape[2])
    partner = from_partner(hidden, "exp", 0)
    half_index = lax.axis_index("exp") % 2
    half_units = down_rows.shape[0] // 2
    pieces = (
        lax.all_gather(hidden, "rep", axis=1, tiled=True),
        lax.all_gather(partner, "rep", axis=1, tiled=True),
    )
    span_rows = pieces[0].shape[1]
    own_weights = lax.dynamic_slice_in_dim(down_rows, half_index * half_units, span_rows, 0)
    other_weights = lax.dynamic_slice_in_dim(down_rows, (1 - half_index) * half_units, span_rows, 0)
    running = jnp.dot(pieces[0], own_weights, preferred_element_type=jnp.float32)
    projected = running + jnp.dot(pieces[1], other_weights, preferred_element_type=jnp.float32)
    expert_out = projected.astype(jnp.bfloat16).reshape(n_shards, capacity, down_rows.shape[1])
    returned = lax.all_to_all(expert_out, "exp", split_axis=0, concat_axis=0, tiled=True)
    returned = returned.reshape(n_shards * capacity, down_rows.shape[1])
    levels = gate_levels.astype(jnp.float32)
    mixing = (levels / jnp.sum(levels, axis=1, keepdims=True)).reshape(-1, 1)
    halves = []
    for half_pos in range(2):
        picked = returned[(2 * flat_ids + half_pos) * capacity + slot_index].astype(jnp.float32)
        weighted = (mixing * picked).reshape(tok_rows, top_count, down_rows.shape[1])
        halves.append(jnp.sum(weighted, axis=1))
    return jnp.stack(halves, axis=1).astype(jnp.bfloat16)


def solution(mesh):
    return jax.shard_map(
        on_device,
        mesh=mesh,
        in_specs=(
            P("exp", None),
            P("exp", None),
            P("exp", None),
            P("exp", "rep", None),
            P("exp", "rep", None),
            P("exp", None, "rep"),
        ),
        out_specs=P("exp", None, "rep"),
        check_vma=False,
    )
```

profile of v0, /device:TPU:6, one launch (start us, length us, event | category | flops | bytes accessed | tf_op | source)
XLA Modules:
  0.0 803.2 jit_solution(6614541302408794211)
XLA Ops:
  8.6 1.2 reduce-window.6
  10.5 1.5 copy.24
  12.1 16.8 %scatter_custom_fusion = bf16[768,2880]{1,0:T(8,128)(2,1)} fusion(s32[512]{0:T(512)S(1)} %bitcast.54, bf16[128,2880]{1,0:T(8,128)(2,1)S(1)} %copy.24, s32[1024]{0:T(1024)S(1)} %pad_clamp_fusion.2, bf16[]{:T(256)} %constant.49.clone.1), kind=kCustom, calls=%fused_computation.5 | custom fusion | bytes 4423682 | tf_op jit(solution)/shard_map/scatter | solution.py:31
  28.9 7.3 reshape.194
  36.2 4.5 broadcast_in_dim.5
  40.8 543.2 %all_to_all.10 = bf16[128,12,2880]{2,1,0:T(8,128)(2,1)} all-to-all(bf16[128,12,2880]{2,1,0:T(8,128)(2,1)S(1)} %bitcast.47), channel_id=1, replica_groups=mesh['rep'=4,'exp'=128] {'exp'}, dimensions={0} | all-to-all | bytes 17694720 | tf_op jit(solution)/shard_map/all_to_all | solution.py:39
  584.0 14.6 %reshape.196 = bf16[1536,2880]{1,0:T(8,128)(2,1)} reshape(bf16[128,12,2880]{2,1,0:T(8,128)(2,1)} %all_to_all.10) | data formatting | bytes 17694720 | tf_op jit(solution)/shard_map/reshape | solution.py:40
  598.6 6.8 fusion.7
  605.5 4.0 fusion.5
  609.5 2.1 collective-permute-start
  611.6 2.0 collective-permute-done
  613.6 0.8 copy-done.3
  614.5 31.6 %all-gather.3.cloned.1.call-done = bf16[1536,768]{0,1:T(8,128)(2,1)} async-done(((bf16[1536,192]{0,1:T(8,128)(2,1)}), bf16[1536,768]{0,1:T(8,128)(2,1)}) %all-gather.3.cloned.1.call-update) | async-done | bytes 2359312 | tf_op jit(solution)/shard_map/all_gather | solution.py:52
  646.1 4.1 fusion.11
  650.2 38.8 %all-gather.5.cloned.1.call-done = bf16[1536,768]{0,1:T(8,128)(2,1)} async-done(((bf16[1536,192]{0,1:T(8,128)(2,1)}), bf16[1536,768]{0,1:T(8,128)(2,1)}) %all-gather.5.cloned.1.call-update) | async-done | bytes 2359312 | tf_op jit(solution)/shard_map/all_gather | solution.py:53
  689.0 3.4 fusion.2
  693.1 1.3 reshape.197
  694.4 17.6 %all-to-all-start.1 = ((bf16[128,12,360]{2,1,0:T(8,128)(2,1)}), bf16[128,12,360]{2,1,0:T(8,128)(2,1)}, u32[]{:S(2)}, u32[]{:S(2)}) async-start(bf16[128,12,360]{2,1,0:T(8,128)(2,1)} %reshape.197), calls=%async_computation.1 | async-start | bytes 3145728 | tf_op jit(solution)/shard_map/all_to_all | solution.py:61
  712.8 74.7 %all-to-all-done.1 = bf16[128,12,360]{2,1,0:T(8,128)(2,1)} async-done(((bf16[128,12,360]{2,1,0:T(8,128)(2,1)}), bf16[128,12,360]{2,1,0:T(8,128)(2,1)}, u32[]{:S(2)}, u32[]{:S(2)}) %all-to-all-start.1) | async-done | bytes 1105952 | tf_op jit(solution)/shard_map/all_to_all | solution.py:61
  787.4 2.5 reshape.198
  789.9 1.9 gather_fusion
  792.1 2.2 gather_fusion.1
  794.5 1.0 multiply_reduce_fusion.1
  795.6 0.8 copy.28
  (44 shorter events, 4.9 us)
Async XLA Ops:
  6.5 592.1 %copy-start = (bf16[1,192,2880]{2,1,0:T(8,128)(2,1)S(1)}, bf16[1,192,2880]{2,1,0:T(8,128)(2,1)}, u32[]{:S(2)}) copy-start(bf16[1,192,2880]{2,1,0:T(8,128)(2,1)} %param.9) | copy-start | bytes 3317764
  6.5 639.6 %all-gather.3.cloned.1.call-start = ((), (), s32[]{:S(2)}) async-start(), calls=%async_computation.2 | async-start | bytes 2949120 | tf_op jit(solution)/shard_map/all_gather | solution.py:52
  598.6 6.8 copy-start.2
  598.6 6.8 copy-start.5
  605.4 40.7 %copy-start.6 = (bf16[1,1536,360]{1,2,0:T(8,128)(2,1)S(1)}, bf16[1,1536,360]{1,2,0:T(8,128)(2,1)}, u32[]{:S(2)}) copy-start(bf16[1,1536,360]{1,2,0:T(8,128)(2,1)} %param.11) | copy-start | bytes 3317764
  609.4 79.6 %all-gather.5.cloned.1.call-start = ((), (), s32[]{:S(2)}) async-start(), calls=%async_computation.3 | async-start | bytes 2949120 | tf_op jit(solution)/shard_map/all_gather | solution.py:53
  609.5 4.1 collective-permute-start
  613.6 0.8 copy-start.3
  694.4 17.6 %copy-start.4 = (s32[128,4]{0,1:T(4,128)S(1)}, s32[128,4]{0,1:T(4,128)}, u32[]{:S(2)}) copy-start(s32[128,4]{0,1:T(4,128)} %param.8) | copy-start | bytes 6148
  694.4 93.0 %all-to-all-start.1 = ((bf16[128,12,360]{2,1,0:T(8,128)(2,1)}), bf16[128,12,360]{2,1,0:T(8,128)(2,1)}, u32[]{:S(2)}, u32[]{:S(2)}) async-start(bf16[128,12,360]{2,1,0:T(8,128)(2,1)} %reshape.197), calls=%async_computation.1 | async-start | bytes 3145728 | tf_op jit(solution)/shard_map/all_to_all | solution.py:61
  792.1 4.3 copy-start.1
Sparse Core Ops, SparseCore 0:
  609.6 36.4 all-gather.2
  648.2 40.7 all-gather.4
where the time goes:
time: 806 us; the launch traced here: 803 us
  blocking collectives  543 us (67%)
  waiting for transfers between devices  147 us (18%)
  local copies, waits for them, and re-layouts  57.4 us (7%)
  starting transfers between devices  19.7 us (2%)
  matrix products  18.3 us (2%)
  between operations  13.6 us (2%)
    all_to_all x1, blocking collectives, on_device(): lax.all_to_all(outgoing, 'exp', split_axis=0, concat_axis=0, tiled=True)  543 us
    all_to_all x1, waiting for transfers between devices, on_device(): lax.all_to_all(expert_out, 'exp', split_axis=0, concat_axis=0, tiled=True)  74.7 us
    all_gather x1, waiting for transfers between devices, on_device(): lax.all_gather(partner, 'rep', axis=1, tiled=True)  38.8 us
    all_gather x1, waiting for transfers between devices, on_device(): lax.all_gather(hidden, 'rep', axis=1, tiled=True)  31.6 us
    all_to_all x1, starting transfers between devices, on_device(): lax.all_to_all(expert_out, 'exp', split_axis=0, concat_axis=0, tiled=True)  17.6 us
    scatter x1, local copies, waits for them, and re-layouts, on_device(): packed = jnp.zeros((expert_count * capacity, model_width), tokens.dtype)....  16.8 us
  transfers between devices with their start and end apart: 4, of which 4 were waited for; matrix products, arithmetic and copies ran while one was open for 1% of the time, Pallas kernels for 0%

commit v1 on v0

v1 whole, which is shorter than its diff:
```python
import jax
import jax.numpy as jnp
from jax import lax
from jax.sharding import Mesh
from jax.sharding import PartitionSpec as P

GROUP = "grp"
CORE = "core"
REP = "rep"


def on_device(tokens, expert_ids, gate_levels, w_gate, w_up, w_down):
    tok_rows = tokens.shape[0]
    model_width = tokens.shape[1]
    top_count = expert_ids.shape[1]
    n_rep = lax.axis_size(REP)
    expert_count = lax.axis_size(GROUP)
    capacity = min(
        tok_rows, max(4, (tok_rows * top_count * 3 // (2 * expert_count) + 3) // 4 * 4)
    )
    part = capacity // n_rep
    rep_index = lax.axis_index(REP)
    core_index = lax.axis_index(CORE)

    flat_ids = expert_ids.reshape(-1)
    onehot = (flat_ids[:, None] == jnp.arange(expert_count, dtype=jnp.int32)[None, :]).astype(
        jnp.int32
    )
    rank_counts = jnp.cumsum(onehot, axis=0) - onehot
    slot_index = jnp.sum(rank_counts * onehot, axis=1)
    source_rows = jnp.arange(tok_rows * top_count, dtype=jnp.int32) // top_count

    local_slot = slot_index - part * rep_index
    in_part = (local_slot >= 0) & (local_slot < part)
    send_slots = expert_count * part
    position = jnp.where(in_part, flat_ids * part + local_slot, send_slots)
    table = jnp.zeros((send_slots,), jnp.int32).at[position].set(source_rows, mode="drop")
    outgoing = tokens[table].reshape(expert_count, part, model_width)

    swap = [(0, 1), (1, 0)]
    other_gate, other_up, other_down = lax.ppermute((w_gate[0], w_up[0], w_down[0]), CORE, swap)

    arrived = lax.all_to_all(outgoing, GROUP, 0, 0, tiled=True)
    rows = lax.all_gather(arrived, REP, axis=0, tiled=False)
    rows = rows.reshape(-1, model_width)

    gate_units = jnp.concatenate([w_gate[0], other_gate], axis=0)
    up_units = jnp.concatenate([w_up[0], other_up], axis=0)
    contract = (((1,), (1,)), ((), ()))
    gate_proj = lax.dot_general(rows, gate_units, contract, preferred_element_type=jnp.float32)
    up_proj = lax.dot_general(rows, up_units, contract, preferred_element_type=jnp.float32)
    hidden = ((up_proj + 1.0) * gate_proj * jax.nn.sigmoid(1.702 * gate_proj)).astype(jnp.bfloat16)
    n_rows = rows.shape[0]
    quarter = w_gate.shape[1]
    hidden = hidden.reshape(n_rows, 2, quarter)
    hidden_all = lax.all_gather(hidden, REP, axis=0, tiled=False)

    down_cols = jnp.concatenate([w_down[0], other_down], axis=1)
    col_count = down_cols.shape[1]
    down_split = down_cols.reshape(2, n_rep, quarter, col_count)
    own_half = lax.dynamic_index_in_dim(down_split, core_index, 0, keepdims=False)
    other_half = lax.dynamic_index_in_dim(down_split, 1 - core_index, 0, keepdims=False)
    down_units = jnp.stack([own_half, other_half], axis=1)
    projected = jnp.einsum(
        "rnhk,rhkc->nc", hidden_all, down_units, preferred_element_type=jnp.float32
    )
    expert_out = projected.astype(jnp.bfloat16).reshape(n_rep, expert_count, part, col_count)

    returned = lax.all_to_all(expert_out, GROUP, 1, 1, tiled=True)
    returned = returned.reshape(-1, col_count)
    pick = ((slot_index // part) * expert_count + flat_ids) * part + slot_index % part
    picked = returned[pick].astype(jnp.float32)
    levels = gate_levels.astype(jnp.float32)
    mixing = (levels / jnp.sum(levels, axis=1, keepdims=True)).reshape(-1, 1)
    combined = jnp.sum((mixing * picked).reshape(tok_rows, top_count, col_count), axis=1)
    combined = combined.reshape(tok_rows, 2, col_count // 2)
    ordered = jnp.where(core_index == 0, combined, combined[:, ::-1, :])
    return ordered.astype(jnp.bfloat16)


def solution(mesh):
    n_rep = mesh.shape[REP]
    n_exp = mesh.shape["exp"]
    split = Mesh(mesh.devices.reshape(n_rep, n_exp // 2, 2), (REP, GROUP, CORE))
    shards = (GROUP, CORE)
    return jax.shard_map(
        on_device,
        mesh=split,
        in_specs=(
            P(shards, None),
            P(shards, None),
            P(shards, None),
            P(shards, REP, None),
            P(shards, REP, None),
            P(shards, None, REP),
        ),
        out_specs=P(shards, None, REP),
        check_vma=False,
    )
```

time: 806 us -> 324 us (0.40)
  blocking collectives: 543 us -> 92 us
  local copies, waits for them, and re-layouts: 57.4 us -> 37.1 us
    all_to_all x1, blocking collectives: 543 us -> 92 us  [on_device(): arrived = lax.all_to_all(outgoing, GROUP, 0, 0, tiled=True)]
    all_to_all x1, waiting for transfers between devices: 74.7 us -> 59.2 us  [on_device(): returned = lax.all_to_all(expert_out, GROUP, 1, 1, tiled=True)]
    scatter x1, local copies, waits for them, and re-layouts: 16.8 us -> 2.44 us  [on_device(): jnp.zeros((send_slots,), jnp.int32).at[position]]
    reshape x4 -> x6, local copies, waits for them, and re-layouts: 25.7 us -> 14.9 us  [the longest x1 10.1 us: on_device(): rows = rows.reshape(-1, model_width)]
    all_gather x2, waiting for transfers between devices: 70.4 us -> 79.3 us  [the longest x1 46.4 us: on_device(): rows = lax.all_gather(arrived, REP, axis=0, tiled=False)]
    all_gather x0 -> x1, local copies, waits for them, and re-layouts: none -> 8.72 us  [on_device(): rows = lax.all_gather(arrived, REP, axis=0, tiled=False)]
    dot_general x4 -> x3, matrix products: 18.3 us -> 12.7 us  [the longest x1 4.44 us: on_device(): lax.dot_general(rows, gate_units, contract, preferred_element_type=jnp.fl...]
  transfers between devices with their start and end apart: 4 -> 6, of which waited for: 4 -> 4; matrix products, arithmetic and copies ran while one was open for 1% -> 9% of each run, Pallas kernels for 0% -> 0%
where the time goes in v1:
time: 324 us; the launch traced here: 323 us
  waiting for transfers between devices  140 us (43%)
  blocking collectives  92 us (28%)
  local copies, waits for them, and re-layouts  37.1 us (11%)
  starting transfers between devices  22.5 us (7%)
  between operations  13.7 us (4%)
  matrix products  12.7 us (4%)
  other arithmetic  5.1 us (2%)
    all_to_all x1, blocking collectives, on_device(): arrived = lax.all_to_all(outgoing, GROUP, 0, 0, tiled=True)  92 us
    all_to_all x1, waiting for transfers between devices, on_device(): returned = lax.all_to_all(expert_out, GROUP, 1, 1, tiled=True)  59.2 us
    all_gather x1, waiting for transfers between devices, on_device(): rows = lax.all_gather(arrived, REP, axis=0, tiled=False)  46.4 us
    all_gather x1, waiting for transfers between devices, on_device(): hidden_all = lax.all_gather(hidden, REP, axis=0, tiled=False)  32.9 us
    all_to_all x1, starting transfers between devices, on_device(): returned = lax.all_to_all(expert_out, GROUP, 1, 1, tiled=True)  16 us
    reshape x1, local copies, waits for them, and re-layouts, on_device(): rows = rows.reshape(-1, model_width)  10.1 us
    all_gather x1, local copies, waits for them, and re-layouts, on_device(): rows = lax.all_gather(arrived, REP, axis=0, tiled=False)  8.72 us
  transfers between devices with their start and end apart: 6, of which 4 were waited for; matrix products, arithmetic and copies ran while one was open for 9% of the time, Pallas kernels for 0%

profile of v1, /device:TPU:6, one launch (start us, length us, event | category | flops | bytes accessed | tf_op | source)
XLA Modules:
  0.0 323.5 jit_solution(13368336528024642918)
XLA Ops:
  7.8 1.2 reduce-window.6
  9.4 2.4 scatter_custom_fusion
  12.3 1.4 gather_fusion
  14.2 92.0 %all_to_all.10 = bf16[64,3,2880]{2,1,0:T(4,128)(2,1)S(1)} all-to-all(bf16[64,3,2880]{2,1,0:T(4,128)(2,1)S(1)} %reshape.173), channel_id=1, replica_groups=mesh['rep'=4,'grp'=64,'core'=2] {'grp'}, dimensions={0} | all-to-all | bytes 2211840 | tf_op jit(solution)/shard_map/all_to_all | solution.py:43
  106.1 1.1 copy.45
  107.8 1.9 collective-permute-start.1
  109.7 2.4 collective-permute-start
  112.2 46.4 %all-gather.6.cloned.1.call-done = bf16[256,3,2880]{2,0,1:T(8,128)(2,1)} async-done(((bf16[64,3,2880]{2,0,1:T(8,128)(2,1)}), bf16[256,3,2880]{2,0,1:T(8,128)(2,1)}) %all-gather.6.cloned.1.call-update) | async-done | bytes 4423696 | tf_op jit(solution)/shard_map/all_gather | solution.py:44
  158.6 8.7 %copy.46 = bf16[256,3,2880]{2,1,0:T(4,128)(2,1)} copy(bf16[256,3,2880]{2,0,1:T(8,128)(2,1)} %all-gather.6.cloned.1.call-done) | data formatting | bytes 8847360 | tf_op jit(solution)/shard_map/all_gather | solution.py:44
  167.3 10.1 %reshape.174 = bf16[768,2880]{1,0:T(8,128)(2,1)} reshape(bf16[256,3,2880]{2,1,0:T(4,128)(2,1)} %copy.46) | data formatting | bytes 8847360 | tf_op jit(solution)/shard_map/reshape | solution.py:45
  177.4 4.4 %fusion.8 = f32[768,384]{0,1:T(8,128)S(1)} fusion(bf16[768,2880]{1,0:T(8,128)(2,1)} %reshape.174, bf16[192,2880]{1,0:T(8,128)(2,1)S(1)} %collective-permute-done.1, bf16[192,2880]{1,0:T(8,128)(2,1)S(1)} %bitcast.55), kind=kOutput, calls=%fused_computation.15 | convolution fusion | flops 1703116800 | bytes 7815168 | tf_op jit(solution)/shard_map/dot_general | solution.py:50
  181.9 4.3 %fusion.23 = bf16[768,384]{0,1:T(8,128)(2,1)} fusion(f32[768,384]{0,1:T(8,128)S(1)} %fusion.8, bf16[768,2880]{1,0:T(8,128)(2,1)S(1)} %copy-done, bf16[192,2880]{1,0:T(8,128)(2,1)} %collective-permute-done, bf16[192,2880]{1,0:T(8,128)(2,1)S(1)} %bitcast.57), kind=kOutput, calls=%fused_computation.24 | convolution fusion | flops 1705476096 | bytes 8404992 | tf_op jit(solution)/shard_map/dot_general | solution.py:51
  186.2 2.1 collective-permute-start.2
  189.0 1.9 collective-permute-done.2
  190.9 1.7 copy.49
  192.6 1.9 fusion.29
  194.5 32.9 %all-gather.4.cloned.1.call-done = bf16[4,768,2,192]{1,3,0,2:T(8,128)(2,1)} async-done(((bf16[1,768,2,192]{1,3,0,2:T(8,128)(2,1)}), bf16[4,768,2,192]{1,3,0,2:T(8,128)(2,1)}) %all-gather.4.cloned.1.call-update) | async-done | bytes 2359312 | tf_op jit(solution)/shard_map/all_gather | solution.py:56
  227.4 4.0 %bitcast_convert_fusion = bf16[768,720]{0,1:T(8,128)(2,1)S(1)} fusion(bf16[4,768,2,192]{1,3,0,2:T(8,128)(2,1)} %all-gather.4.cloned.1.call-done, bf16[4,1,192,720]{3,2,0,1:T(8,128)(2,1)} %get-tuple-element.6, bf16[4,1,192,720]{3,2,0,1:T(8,128)(2,1)S(1)} %get-tuple-element.5), kind=kOutput, calls=%fused_computation.19 | convolution fusion | flops 1700352000 | bytes 5677056 | tf_op jit(solution)/shard_map/rnhk,rhkc->nc/dot_general | solution.py:64
  232.7 2.5 copy.51
  235.2 16.0 %all-to-all-start.1 = ((bf16[4,64,3,720]{3,0,2,1:T(4,128)(2,1)}), bf16[4,64,3,720]{3,0,2,1:T(4,128)(2,1)S(1)}, u32[]{:S(2)}, u32[]{:S(2)}) async-start(bf16[4,64,3,720]{3,0,2,1:T(4,128)(2,1)} %copy.51), calls=%async_computation.1 | async-start | bytes 2359296 | tf_op jit(solution)/shard_map/all_to_all | solution.py:69
  251.4 59.2 %all-to-all-done.1 = bf16[4,64,3,720]{3,0,2,1:T(4,128)(2,1)S(1)} async-done(((bf16[4,64,3,720]{3,0,2,1:T(4,128)(2,1)}), bf16[4,64,3,720]{3,0,2,1:T(4,128)(2,1)S(1)}, u32[]{:S(2)}, u32[]{:S(2)}) %all-to-all-start.1) | async-done | bytes 1105952 | tf_op jit(solution)/shard_map/all_to_all | solution.py:69
  311.2 1.1 reshape.176
  312.3 2.0 gather_fusion.1
  314.7 1.0 multiply_reduce_fusion
  (46 shorter events, 7.1 us)
Async XLA Ops:
  6.5 5.4 %copy-start.2 = (bf16[128,2880]{0,1:T(8,128)(2,1)S(1)}, bf16[128,2880]{0,1:T(8,128)(2,1)}, u32[]{:S(2)}) copy-start(bf16[128,2880]{0,1:T(8,128)(2,1)} %param.6) | copy-start | bytes 2211844
  6.5 152.1 %all-gather.6.cloned.1.call-start = ((), (), s32[]{:S(2)}) async-start(), calls=%async_computation.3 | async-start | bytes 5652480 | tf_op jit(solution)/shard_map/all_gather | solution.py:44
  106.1 1.7 copy-start.4
  106.1 3.6 %copy-start.5 = (bf16[1,192,2880]{2,1,0:T(8,128)(2,1)S(1)}, bf16[1,192,2880]{2,1,0:T(8,128)(2,1)}, u32[]{:S(2)}) copy-start(bf16[1,192,2880]{2,1,0:T(8,128)(2,1)} %param.10) | copy-start | bytes 3317764
  107.3 120.1 %all-gather.4.cloned.1.call-start = ((), (), s32[]{:S(2)}) async-start(), calls=%async_computation.2 | async-start | bytes 2949120 | tf_op jit(solution)/shard_map/all_gather | solution.py:56
  107.8 69.6 %collective-permute-start.1 = (bf16[192,2880]{1,0:T(8,128)(2,1)S(1)}, bf16[192,2880]{1,0:T(8,128)(2,1)S(1)}, u32[]{:S(2)}, u32[]{:S(2)}) collective-permute-start(bf16[192,2880]{1,0:T(8,128)(2,1)S(1)} %bitcast.54), channel_id=1, source_target_pairs={{0,1},{1,0},{2,3},{3,2},{4,5},{5,4},{6,7},{7,6},{8,9},{9,8},{10,11... | collective-permute-start | bytes 3317768 | tf_op jit(solution)/shard_map/ppermute | solution.py:41
  109.7 72.1 %collective-permute-start = (bf16[192,2880]{1,0:T(8,128)(2,1)S(1)}, bf16[192,2880]{1,0:T(8,128)(2,1)}, u32[]{:S(2)}, u32[]{:S(2)}) collective-permute-start(bf16[192,2880]{1,0:T(8,128)(2,1)S(1)} %bitcast.56), channel_id=1, source_target_pairs={{0,1},{1,0},{2,3},{3,2},{4,5},{5,4},{6,7},{7,6},{8,9},{9,8},{10,11... | collective-permute-start | bytes 3317768 | tf_op jit(solution)/shard_map/ppermute | solution.py:41
  177.4 4.5 %copy-start = (bf16[768,2880]{1,0:T(8,128)(2,1)S(1)}, bf16[768,2880]{1,0:T(8,128)(2,1)}, u32[]{:S(2)}) copy-start(bf16[768,2880]{1,0:T(8,128)(2,1)} %reshape.174) | copy-start | bytes 13271044
  181.8 4.3 %copy-start.1 = (bf16[1,1536,360]{1,2,0:T(8,128)(2,1)S(1)}, bf16[1,1536,360]{1,2,0:T(8,128)(2,1)}, u32[]{:S(2)}) copy-start(bf16[1,1536,360]{1,2,0:T(8,128)(2,1)} %param.11) | copy-start | bytes 3317764
  186.2 4.8 %collective-permute-start.2 = (bf16[1536,360]{0,1:T(8,128)(2,1)S(1)}, bf16[1536,360]{0,1:T(8,128)(2,1)}, u32[]{:S(2)}, u32[]{:S(2)}) collective-permute-start(bf16[1536,360]{0,1:T(8,128)(2,1)S(1)} %bitcast.46), channel_id=1, source_target_pairs={{0,1},{1,0},{2,3},{3,2},{4,5},{5,4},{6,7},{7,6},{8,9},{9,8},{10,11... | collective-permute-start | bytes 3317768 | tf_op jit(solution)/shard_map/ppermute | solution.py:41
  235.2 16.1 %copy-start.3 = (s32[128,4]{0,1:T(4,128)S(1)}, s32[128,4]{0,1:T(4,128)}, u32[]{:S(2)}) copy-start(s32[128,4]{0,1:T(4,128)} %param.8) | copy-start | bytes 6148
  235.2 75.4 %all-to-all-start.1 = ((bf16[4,64,3,720]{3,0,2,1:T(4,128)(2,1)}), bf16[4,64,3,720]{3,0,2,1:T(4,128)(2,1)S(1)}, u32[]{:S(2)}, u32[]{:S(2)}) async-start(bf16[4,64,3,720]{3,0,2,1:T(4,128)(2,1)} %copy.51), calls=%async_computation.1 | async-start | bytes 2359296 | tf_op jit(solution)/shard_map/all_to_all | solution.py:69
Sparse Core Ops, SparseCore 0:
  107.4 51.1 all-gather.5
  186.3 41.0 all-gather.3

commit v2 on v1

--- a/solution.py
+++ b/solution.py
@@ -33,14 +33,14 @@
     local_slot = slot_index - part * rep_index
     in_part = (local_slot >= 0) & (local_slot < part)
     send_slots = expert_count * part
-    position = jnp.where(in_part, flat_ids * part + local_slot, send_slots)
+    position = jnp.where(in_part, local_slot * expert_count + flat_ids, send_slots)
     table = jnp.zeros((send_slots,), jnp.int32).at[position].set(source_rows, mode="drop")
-    outgoing = tokens[table].reshape(expert_count, part, model_width)
+    outgoing = tokens[table].reshape(part, expert_count, model_width)
 
     swap = [(0, 1), (1, 0)]
     other_gate, other_up, other_down = lax.ppermute((w_gate[0], w_up[0], w_down[0]), CORE, swap)
 
-    arrived = lax.all_to_all(outgoing, GROUP, 0, 0, tiled=True)
+    arrived = lax.all_to_all(outgoing, GROUP, 1, 1, tiled=True)
     rows = lax.all_gather(arrived, REP, axis=0, tiled=False)
     rows = rows.reshape(-1, model_width)
 
@@ -50,9 +50,7 @@
     gate_proj = lax.dot_general(rows, gate_units, contract, preferred_element_type=jnp.float32)
     up_proj = lax.dot_general(rows, up_units, contract, preferred_element_type=jnp.float32)
     hidden = ((up_proj + 1.0) * gate_proj * jax.nn.sigmoid(1.702 * gate_proj)).astype(jnp.bfloat16)
-    n_rows = rows.shape[0]
     quarter = w_gate.shape[1]
-    hidden = hidden.reshape(n_rows, 2, quarter)
     hidden_all = lax.all_gather(hidden, REP, axis=0, tiled=False)
 
     down_cols = jnp.concatenate([w_down[0], other_down], axis=1)
@@ -60,15 +58,15 @@
     down_split = down_cols.reshape(2, n_rep, quarter, col_count)
     own_half = lax.dynamic_index_in_dim(down_split, core_index, 0, keepdims=False)
     other_half = lax.dynamic_index_in_dim(down_split, 1 - core_index, 0, keepdims=False)
-    down_units = jnp.stack([own_half, other_half], axis=1)
+    down_units = jnp.stack([own_half, other_half], axis=1).reshape(n_rep, 2 * quarter, col_count)
     projected = jnp.einsum(
-        "rnhk,rhkc->nc", hidden_all, down_units, preferred_element_type=jnp.float32
+        "rnk,rkc->nc", hidden_all, down_units, preferred_element_type=jnp.float32
     )
-    expert_out = projected.astype(jnp.bfloat16).reshape(n_rep, expert_count, part, col_count)
+    expert_out = projected.astype(jnp.bfloat16).reshape(capacity, expert_count, col_count)
 
     returned = lax.all_to_all(expert_out, GROUP, 1, 1, tiled=True)
     returned = returned.reshape(-1, col_count)
-    pick = ((slot_index // part) * expert_count + flat_ids) * part + slot_index % part
+    pick = slot_index * expert_count + flat_ids
     picked = returned[pick].astype(jnp.float32)
     levels = gate_levels.astype(jnp.float32)
     mixing = (levels / jnp.sum(levels, axis=1, keepdims=True)).reshape(-1, 1)

time: 324 us -> 322 us (level)
  local copies, waits for them, and re-layouts: 37.1 us -> 17.3 us
  waiting for transfers between devices: 140 us -> 158 us
    all_to_all x1, waiting for transfers between devices: 59.2 us -> 75.2 us  [on_device(): returned = lax.all_to_all(expert_out, GROUP, 1, 1, tiled=True)]
    reshape x5 -> x2, local copies, waits for them, and re-layouts: 14.8 us -> 2.79 us  [the longest x1 1.82 us: on_device(): projected.astype(jnp.bfloat16).reshape(capacity, expert_count, col_count)]
    all_gather x1 -> x0, local copies, waits for them, and re-layouts: 8.72 us -> none  [on_device(): rows = lax.all_gather(arrived, REP, axis=0, tiled=False)]
  transfers between devices with their start and end apart: 6 -> 6, of which waited for: 4 -> 5; matrix products, arithmetic and copies ran while one was open for 9% -> 3% of each run, Pallas kernels for 0% -> 0%
where the time goes in v2:
time: 322 us; the launch traced here: 321 us
  waiting for transfers between devices  158 us (49%)
  blocking collectives  92 us (29%)
  starting transfers between devices  22.5 us (7%)
  local copies, waits for them, and re-layouts  17.3 us (5%)
  between operations  13.7 us (4%)
  matrix products  13.2 us (4%)
  other arithmetic  4.29 us (1%)
    all_to_all x1, blocking collectives, on_device(): arrived = lax.all_to_all(outgoing, GROUP, 1, 1, tiled=True)  92 us
    all_to_all x1, waiting for transfers between devices, on_device(): returned = lax.all_to_all(expert_out, GROUP, 1, 1, tiled=True)  75.2 us
    all_gather x1, waiting for transfers between devices, on_device(): rows = lax.all_gather(arrived, REP, axis=0, tiled=False)  46.1 us
    all_gather x1, waiting for transfers between devices, on_device(): hidden_all = lax.all_gather(hidden, REP, axis=0, tiled=False)  34.6 us
    all_to_all x1, starting transfers between devices, on_device(): returned = lax.all_to_all(expert_out, GROUP, 1, 1, tiled=True)  16 us
  transfers between devices with their start and end apart: 6, of which 5 were waited for; matrix products, arithmetic and copies ran while one was open for 3% of the time, Pallas kernels for 0%

profile of v2, /device:TPU:6, one launch (start us, length us, event | category | flops | bytes accessed | tf_op | source)
XLA Modules:
  0.0 321.0 jit_solution(11489619488270574034)
XLA Ops:
  6.5 0.8 copy.41
  7.6 1.2 reduce-window.6
  9.3 2.4 scatter_custom_fusion
  11.8 1.5 copy.45
  13.3 1.3 gather_fusion
  14.6 1.0 copy.46
  15.6 92.0 %all_to_all.10 = bf16[3,64,2880]{2,0,1:T(4,128)(2,1)S(1)} all-to-all(bf16[3,64,2880]{2,0,1:T(4,128)(2,1)S(1)} %copy.46), channel_id=1, replica_groups=mesh['rep'=4,'grp'=64,'core'=2] {'grp'}, dimensions={1} | all-to-all | bytes 2211840 | tf_op jit(solution)/shard_map/all_to_all | solution.py:43
  107.6 1.1 copy.47
  109.2 1.9 collective-permute-start.1
  111.2 2.4 collective-permute-start
  113.9 46.1 %all-gather.5.cloned.1.call-done = bf16[12,64,2880]{2,1,0:T(8,128)(2,1)} async-done(((bf16[3,64,2880]{2,1,0:T(8,128)(2,1)}), bf16[12,64,2880]{2,1,0:T(8,128)(2,1)}) %all-gather.5.cloned.1.call-update) | async-done | bytes 4423696 | tf_op jit(solution)/shard_map/all_gather | solution.py:44
  160.1 4.7 %fusion.4 = f32[768,384]{1,0:T(8,128)S(1)} fusion(bf16[768,2880]{1,0:T(8,128)(2,1)} %bitcast.57, bf16[192,2880]{1,0:T(8,128)(2,1)S(1)} %collective-permute-done.1, bf16[192,2880]{1,0:T(8,128)(2,1)S(1)} %bitcast.61), kind=kOutput, calls=%fused_computation.12 | convolution fusion | flops 1703116800 | bytes 7815168 | tf_op jit(solution)/shard_map/dot_general | solution.py:50
  164.8 4.9 %fusion.17 = bf16[768,384]{1,0:T(8,128)(2,1)} fusion(f32[768,384]{1,0:T(8,128)S(1)} %fusion.4, bf16[768,2880]{1,0:T(8,128)(2,1)S(1)} %bitcast.58, bf16[192,2880]{1,0:T(8,128)(2,1)} %collective-permute-done, bf16[192,2880]{1,0:T(8,128)(2,1)S(1)} %bitcast.63), kind=kOutput, calls=%fused_computation.21 | convolution fusion | flops 1705476096 | bytes 8404992 | tf_op jit(solution)/shard_map/dot_general | solution.py:51
  169.7 2.1 collective-permute-start.2
  172.5 1.8 collective-permute-done.2
  175.1 0.9 fusion.23
  176.3 34.6 %all-gather.7.cloned.1.call-done = bf16[3072,384]{1,0:T(8,128)(2,1)} async-done(((bf16[768,384]{1,0:T(8,128)(2,1)}), bf16[3072,384]{1,0:T(8,128)(2,1)}) %all-gather.7.cloned.1.call-update) | async-done | bytes 2359312 | tf_op jit(solution)/shard_map/all_gather | solution.py:54
  210.9 3.6 %bitcast_convert_fusion = bf16[768,720]{0,1:T(8,128)(2,1)S(1)} fusion(bf16[4,768,384]{2,1,0:T(8,128)(2,1)} %bitcast.59, bf16[4,384,720]{2,1,0:T(8,128)(2,1)S(1)} %bitcast.50), kind=kOutput, calls=%fused_computation.16 | convolution fusion | flops 1699246080 | bytes 5677056 | tf_op jit(solution)/shard_map/rnk,rkc->nc/dot_general | solution.py:62
  215.2 1.8 copy.53
  217.0 16.0 %all-to-all-start.1 = ((bf16[12,64,720]{2,0,1:T(8,128)(2,1)}), bf16[12,64,720]{2,0,1:T(8,128)(2,1)S(1)}, u32[]{:S(2)}, u32[]{:S(2)}) async-start(bf16[12,64,720]{2,0,1:T(8,128)(2,1)} %copy.53), calls=%async_computation.1 | async-start | bytes 3145728 | tf_op jit(solution)/shard_map/all_to_all | solution.py:67
  233.1 0.7 copy.40
  233.8 75.2 %all-to-all-done.1 = bf16[12,64,720]{2,0,1:T(8,128)(2,1)S(1)} async-done(((bf16[12,64,720]{2,0,1:T(8,128)(2,1)}), bf16[12,64,720]{2,0,1:T(8,128)(2,1)S(1)}, u32[]{:S(2)}, u32[]{:S(2)}) %all-to-all-start.1) | async-done | bytes 1105952 | tf_op jit(solution)/shard_map/all_to_all | solution.py:67
  309.4 2.0 gather_fusion.1
  312.3 1.0 multiply_reduce_fusion
  (44 shorter events, 6.2 us)
Async XLA Ops:
  6.5 153.5 %all-gather.5.cloned.1.call-start = ((), (), s32[]{:S(2)}) async-start(), calls=%async_computation.2 | async-start | bytes 5652480 | tf_op jit(solution)/shard_map/all_gather | solution.py:44
  107.6 1.7 copy-start.4
  107.6 3.6 %copy-start.5 = (bf16[1,192,2880]{2,1,0:T(8,128)(2,1)S(1)}, bf16[1,192,2880]{2,1,0:T(8,128)(2,1)}, u32[]{:S(2)}) copy-start(bf16[1,192,2880]{2,1,0:T(8,128)(2,1)} %param.10) | copy-start | bytes 3317764
  108.7 102.2 %all-gather.7.cloned.1.call-start = ((), (), s32[]{:S(2)}) async-start(), calls=%async_computation.3 | async-start | bytes 2949120 | tf_op jit(solution)/shard_map/all_gather | solution.py:54
  109.2 4.7 %collective-permute-start.1 = (bf16[192,2880]{1,0:T(8,128)(2,1)S(1)}, bf16[192,2880]{1,0:T(8,128)(2,1)S(1)}, u32[]{:S(2)}, u32[]{:S(2)}) collective-permute-start(bf16[192,2880]{1,0:T(8,128)(2,1)S(1)} %bitcast.60), channel_id=1, source_target_pairs={{0,1},{1,0},{2,3},{3,2},{4,5},{5,4},{6,7},{7,6},{8,9},{9,8},{10,11... | collective-permute-start | bytes 3317768 | tf_op jit(solution)/shard_map/ppermute | solution.py:41
  111.2 53.6 %collective-permute-start = (bf16[192,2880]{1,0:T(8,128)(2,1)S(1)}, bf16[192,2880]{1,0:T(8,128)(2,1)}, u32[]{:S(2)}, u32[]{:S(2)}) collective-permute-start(bf16[192,2880]{1,0:T(8,128)(2,1)S(1)} %bitcast.62), channel_id=1, source_target_pairs={{0,1},{1,0},{2,3},{3,2},{4,5},{5,4},{6,7},{7,6},{8,9},{9,8},{10,11... | collective-permute-start | bytes 3317768 | tf_op jit(solution)/shard_map/ppermute | solution.py:41
  160.1 4.7 %copy-start.3 = (bf16[12,64,2880]{2,1,0:T(8,128)(2,1)S(1)}, bf16[12,64,2880]{2,1,0:T(8,128)(2,1)}, u32[]{:S(2)}) copy-start(bf16[12,64,2880]{2,1,0:T(8,128)(2,1)} %all-gather.5.cloned.1.call-done) | copy-start | bytes 13271044
  164.8 4.9 %copy-start = (bf16[1,1536,360]{1,2,0:T(8,128)(2,1)S(1)}, bf16[1,1536,360]{1,2,0:T(8,128)(2,1)}, u32[]{:S(2)}) copy-start(bf16[1,1536,360]{1,2,0:T(8,128)(2,1)} %param.11) | copy-start | bytes 3317764
  169.7 4.6 %collective-permute-start.2 = (bf16[1536,360]{0,1:T(8,128)(2,1)S(1)}, bf16[1536,360]{0,1:T(8,128)(2,1)S(1)}, u32[]{:S(2)}, u32[]{:S(2)}) collective-permute-start(bf16[1536,360]{0,1:T(8,128)(2,1)S(1)} %bitcast.51), channel_id=1, source_target_pairs={{0,1},{1,0},{2,3},{3,2},{4,5},{5,4},{6,7},{7,6},{8,9},{9,8},{10,11... | collective-permute-start | bytes 3317768 | tf_op jit(solution)/shard_map/ppermute | solution.py:41
  217.0 16.1 %copy-start.2 = (s32[128,4]{0,1:T(4,128)S(1)}, s32[128,4]{0,1:T(4,128)}, u32[]{:S(2)}) copy-start(s32[128,4]{0,1:T(4,128)} %param.8) | copy-start | bytes 6148
  217.0 92.0 %all-to-all-start.1 = ((bf16[12,64,720]{2,0,1:T(8,128)(2,1)}), bf16[12,64,720]{2,0,1:T(8,128)(2,1)S(1)}, u32[]{:S(2)}, u32[]{:S(2)}) async-start(bf16[12,64,720]{2,0,1:T(8,128)(2,1)} %copy.53), calls=%async_computation.1 | async-start | bytes 3145728 | tf_op jit(solution)/shard_map/all_to_all | solution.py:67
  311.4 0.8 copy-start.1
Sparse Core Ops, SparseCore 0:
  108.9 51.1 all-gather.4
  169.8 41.0 all-gather.6

commit v3 on v2

--- a/solution.py
+++ b/solution.py
@@ -35,38 +35,39 @@
     send_slots = expert_count * part
     position = jnp.where(in_part, local_slot * expert_count + flat_ids, send_slots)
     table = jnp.zeros((send_slots,), jnp.int32).at[position].set(source_rows, mode="drop")
-    outgoing = tokens[table].reshape(part, expert_count, model_width)
+    outgoing = tokens[table].reshape(part, expert_count, 1, model_width)
 
     swap = [(0, 1), (1, 0)]
     other_gate, other_up, other_down = lax.ppermute((w_gate[0], w_up[0], w_down[0]), CORE, swap)
-
-    arrived = lax.all_to_all(outgoing, GROUP, 1, 1, tiled=True)
-    rows = lax.all_gather(arrived, REP, axis=0, tiled=False)
-    rows = rows.reshape(-1, model_width)
-
     gate_units = jnp.concatenate([w_gate[0], other_gate], axis=0)
     up_units = jnp.concatenate([w_up[0], other_up], axis=0)
-    contract = (((1,), (1,)), ((), ()))
-    gate_proj = lax.dot_general(rows, gate_units, contract, preferred_element_type=jnp.float32)
-    up_proj = lax.dot_general(rows, up_units, contract, preferred_element_type=jnp.float32)
-    hidden = ((up_proj + 1.0) * gate_proj * jax.nn.sigmoid(1.702 * gate_proj)).astype(jnp.bfloat16)
     quarter = w_gate.shape[1]
-    hidden_all = lax.all_gather(hidden, REP, axis=0, tiled=False)
-
     down_cols = jnp.concatenate([w_down[0], other_down], axis=1)
     col_count = down_cols.shape[1]
     down_split = down_cols.reshape(2, n_rep, quarter, col_count)
     own_half = lax.dynamic_index_in_dim(down_split, core_index, 0, keepdims=False)
     other_half = lax.dynamic_index_in_dim(down_split, 1 - core_index, 0, keepdims=False)
     down_units = jnp.stack([own_half, other_half], axis=1).reshape(n_rep, 2 * quarter, col_count)
-    projected = jnp.einsum(
-        "rnk,rkc->nc", hidden_all, down_units, preferred_element_type=jnp.float32
-    )
-    expert_out = projected.astype(jnp.bfloat16).reshape(capacity, expert_count, col_count)
+    contract = (((1,), (1,)), ((), ()))
 
-    returned = lax.all_to_all(expert_out, GROUP, 1, 1, tiled=True)
-    returned = returned.reshape(-1, col_count)
-    pick = slot_index * expert_count + flat_ids
+    chunks = []
+    for chunk in range(part):
+        arrived = lax.all_to_all(outgoing[chunk], GROUP, 0, 0, tiled=True)
+        rows = lax.all_gather(arrived, REP, axis=0, tiled=False).reshape(-1, model_width)
+        gate_proj = lax.dot_general(rows, gate_units, contract, preferred_element_type=jnp.float32)
+        up_proj = lax.dot_general(rows, up_units, contract, preferred_element_type=jnp.float32)
+        hidden = ((up_proj + 1.0) * gate_proj * jax.nn.sigmoid(1.702 * gate_proj)).astype(
+            jnp.bfloat16
+        )
+        hidden_all = lax.all_gather(hidden, REP, axis=0, tiled=False)
+        projected = jnp.einsum(
+            "rnk,rkc->nc", hidden_all, down_units, preferred_element_type=jnp.float32
+        )
+        expert_out = projected.astype(jnp.bfloat16).reshape(n_rep, expert_count, col_count)
+        chunks.append(lax.all_to_all(expert_out, GROUP, 1, 1, tiled=True))
+
+    returned = jnp.stack(chunks, axis=0).reshape(-1, col_count)
+    pick = ((slot_index % part) * n_rep + slot_index // part) * expert_count + flat_ids
     picked = returned[pick].astype(jnp.float32)
     levels = gate_levels.astype(jnp.float32)
     mixing = (levels / jnp.sum(levels, axis=1, keepdims=True)).reshape(-1, 1)

time: 322 us -> 268 us (0.83)
  waiting for transfers between devices: 158 us -> 34.2 us
  blocking collectives: 92 us -> 121 us
  starting transfers between devices: 22.5 us -> 50.2 us
  matrix products: 13.2 us -> 19.4 us
  local copies, waits for them, and re-layouts: 17.3 us -> 21.4 us
  other arithmetic: 4.29 us -> 7.89 us
    all_gather x2 -> x3, waiting for transfers between devices: 80.7 us -> 0.06 us  [on_device(): lax.all_gather(arrived, REP, axis=0, tiled=False).reshape(-1, model_width)]
    all_gather x0 -> x3, blocking collectives: none -> 43.7 us  [on_device(): hidden_all = lax.all_gather(hidden, REP, axis=0, tiled=False)]
    all_to_all x1 -> x4, waiting for transfers between devices: 75.2 us -> 34.1 us  [the longest x3 19 us: on_device(): chunks.append(lax.all_to_all(expert_out, GROUP, 1, 1, tiled=True))]
    all_to_all x1 -> x4, starting transfers between devices: 16 us -> 43.7 us  [the longest x3 36.9 us: on_device(): chunks.append(lax.all_to_all(expert_out, GROUP, 1, 1, tiled=True))]
    all_to_all x1 -> x2, blocking collectives: 92 us -> 76.9 us  [on_device(): arrived = lax.all_to_all(outgoing[chunk], GROUP, 0, 0, tiled=True)]
    dot_general x1 -> x3, matrix products: 4.7 us -> 9.48 us  [on_device(): lax.dot_general(rows, gate_units, contract, preferred_element_type=jnp.fl...]
    dot_general x1 -> x3, matrix products: 4.87 us -> 6.73 us  [on_device(): lax.dot_general(rows, up_units, contract, preferred_element_type=jnp.floa...]
  transfers between devices with their start and end apart: 6 -> 10, of which waited for: 5 -> 2; matrix products, arithmetic and copies ran while one was open for 3% -> 12% of each run, Pallas kernels for 0% -> 0%
where the time goes in v3:
time: 268 us; the launch traced here: 267 us
  blocking collectives  121 us (45%)
  starting transfers between devices  50.2 us (19%)
  waiting for transfers between devices  34.2 us (13%)
  local copies, waits for them, and re-layouts  21.4 us (8%)
  matrix products  19.4 us (7%)
  between operations  13.6 us (5%)
  other arithmetic  7.89 us (3%)
    all_to_all x2, blocking collectives, on_device(): arrived = lax.all_to_all(outgoing[chunk], GROUP, 0, 0, tiled=True)  76.9 us
    all_gather x3, blocking collectives, on_device(): hidden_all = lax.all_gather(hidden, REP, axis=0, tiled=False)  43.7 us
    all_to_all x3, starting transfers between devices, on_device(): chunks.append(lax.all_to_all(expert_out, GROUP, 1, 1, tiled=True))  36.9 us
    all_to_all x3, waiting for transfers between devices, on_device(): chunks.append(lax.all_to_all(expert_out, GROUP, 1, 1, tiled=True))  19 us
    all_to_all x1, waiting for transfers between devices, on_device(): arrived = lax.all_to_all(outgoing[chunk], GROUP, 0, 0, tiled=True)  15.1 us
    dot_general x3, matrix products, on_device(): lax.dot_general(rows, gate_units, contract, preferred_element_type=jnp.fl...  9.48 us
    all_to_all x1, starting transfers between devices, on_device(): arrived = lax.all_to_all(outgoing[chunk], GROUP, 0, 0, tiled=True)  6.78 us
    dot_general x3, matrix products, on_device(): lax.dot_general(rows, up_units, contract, preferred_element_type=jnp.floa...  6.73 us
  transfers between devices with their start and end apart: 10, of which 2 were waited for; matrix products, arithmetic and copies ran while one was open for 12% of the time, Pallas kernels for 0%

profile of v3, /device:TPU:6, one launch (start us, length us, event | category | flops | bytes accessed | tf_op | source)
XLA Modules:
  0.0 267.4 jit_solution(18212667437730728659)
XLA Ops:
  9.4 2.4 scatter_custom_fusion
  12.3 1.4 gather_fusion
  15.5 44.9 %all_to_all.30 = bf16[64,2,1440]{2,1,0:T(2,128)(2,1)S(1)} all-to-all(bf16[64,2,1440]{2,1,0:T(2,128)(2,1)S(1)} %reshape.253), channel_id=1, replica_groups=mesh['rep'=4,'grp'=64,'core'=2] {'grp'}, dimensions={0} | all-to-all | bytes 737280 | tf_op jit(solution)/shard_map/all_to_all | solution.py:55
  63.1 32.0 %all_to_all.31 = bf16[64,2,1440]{2,1,0:T(2,128)(2,1)S(1)} all-to-all(bf16[64,2,1440]{2,1,0:T(2,128)(2,1)S(1)} %reshape.251), channel_id=1, replica_groups=mesh['rep'=4,'grp'=64,'core'=2] {'grp'}, dimensions={0} | all-to-all | bytes 737280 | tf_op jit(solution)/shard_map/all_to_all | solution.py:55
  98.6 6.8 %all-to-all-start.4 = ((bf16[64,2,1440]{2,1,0:T(2,128)(2,1)}), bf16[64,2,1440]{2,1,0:T(2,128)(2,1)S(1)}, u32[]{:S(2)}, u32[]{:S(2)}) async-start(bf16[64,2,1440]{2,1,0:T(2,128)(2,1)} %reshape.249), calls=%async_computation.4 | async-start | bytes 786432 | tf_op jit(solution)/shard_map/all_to_all | solution.py:55
  105.5 1.9 collective-permute-start.2
  107.4 2.4 collective-permute-start.1
  109.8 2.1 collective-permute-start
  112.7 1.7 copy.87
  115.7 15.1 %all-to-all-done.4 = bf16[64,2,1440]{2,1,0:T(2,128)(2,1)S(1)} async-done(((bf16[64,2,1440]{2,1,0:T(2,128)(2,1)}), bf16[64,2,1440]{2,1,0:T(2,128)(2,1)S(1)}, u32[]{:S(2)}, u32[]{:S(2)}) %all-to-all-start.4) | async-done | bytes 368672 | tf_op jit(solution)/shard_map/all_to_all | solution.py:55
  132.2 3.2 %fusion.8 = f32[256,384]{1,0:T(8,128)S(1)} fusion(bf16[256,1,2880]{2,0,1:T(8,128)(2,1)} %all-gather.10.cloned.1.call-done, bf16[192,2880]{1,0:T(8,128)(2,1)} %collective-permute-done.1, bf16[192,2880]{1,0:T(8,128)(2,1)} %bitcast.138), kind=kOutput, calls=%fused_computation.19 | convolution fusion | flops 570654720 | bytes 4079616 | tf_op jit(solution)/shard_map/dot_general | solution.py:57
  135.4 2.2 fusion.52
  137.7 16.9 %all-gather.1 = bf16[1024,384]{1,0:T(8,128)(2,1)S(1)} all-gather(bf16[256,384]{1,0:T(8,128)(2,1)S(1)} %fusion.52), channel_id=3, replica_groups=mesh['rep'=4,'grp'=64,'core'=2] {'rep'}, dimensions={0}, use_global_device_ids=true | all-gather | bytes 983040 | tf_op jit(solution)/shard_map/all_gather | solution.py:62
  156.9 6.6 %all-to-all-start.1 = ((bf16[4,64,720]{2,0,1:T(4,128)(2,1)}), bf16[4,64,720]{2,0,1:T(4,128)(2,1)S(1)}, u32[]{:S(2)}, u32[]{:S(2)}) async-start(bf16[4,64,720]{2,0,1:T(4,128)(2,1)} %copy.91), calls=%async_computation.1 | async-start | bytes 786432 | tf_op jit(solution)/shard_map/all_to_all | solution.py:67
  163.6 3.2 %fusion.4 = f32[256,384]{1,0:T(8,128)S(1)} fusion(bf16[256,1,2880]{2,0,1:T(8,128)(2,1)} %all-gather.12.cloned.1.call-done, bf16[192,2880]{1,0:T(8,128)(2,1)} %collective-permute-done.1, bf16[192,2880]{1,0:T(8,128)(2,1)} %bitcast.139), kind=kOutput, calls=%fused_computation.15 | convolution fusion | flops 570654720 | bytes 4079616 | tf_op jit(solution)/shard_map/dot_general | solution.py:57
  166.8 2.2 fusion.49
  169.0 13.5 %all-gather.3 = bf16[1024,384]{1,0:T(8,128)(2,1)S(1)} all-gather(bf16[256,384]{1,0:T(8,128)(2,1)S(1)} %fusion.49), channel_id=5, replica_groups=mesh['rep'=4,'grp'=64,'core'=2] {'rep'}, dimensions={0}, use_global_device_ids=true | all-gather | bytes 983040 | tf_op jit(solution)/shard_map/all_gather | solution.py:62
  184.8 15.1 %all-to-all-start.3 = ((bf16[4,64,720]{2,0,1:T(4,128)(2,1)}), bf16[4,64,720]{2,0,1:T(4,128)(2,1)S(1)}, u32[]{:S(2)}, u32[]{:S(2)}) async-start(bf16[4,64,720]{2,0,1:T(4,128)(2,1)} %copy.97), calls=%async_computation.3 | async-start | bytes 786432 | tf_op jit(solution)/shard_map/all_to_all | solution.py:67
  200.0 3.2 %fusion = f32[256,384]{1,0:T(8,128)S(1)} fusion(bf16[256,1,2880]{2,0,1:T(8,128)(2,1)} %all-gather.14.cloned.1.call-done, bf16[192,2880]{1,0:T(8,128)(2,1)} %collective-permute-done.1, bf16[192,2880]{1,0:T(8,128)(2,1)} %bitcast.140), kind=kOutput, calls=%fused_computation.11 | convolution fusion | flops 570654720 | bytes 4079616 | tf_op jit(solution)/shard_map/dot_general | solution.py:57
  203.2 2.2 fusion.46
  205.5 13.3 %all-gather.5 = bf16[1024,384]{1,0:T(8,128)(2,1)S(1)} all-gather(bf16[256,384]{1,0:T(8,128)(2,1)S(1)} %fusion.46), channel_id=7, replica_groups=mesh['rep'=4,'grp'=64,'core'=2] {'rep'}, dimensions={0}, use_global_device_ids=true | all-gather | bytes 983040 | tf_op jit(solution)/shard_map/all_gather | solution.py:62
  221.1 15.1 %all-to-all-start.5 = ((bf16[4,64,720]{2,0,1:T(4,128)(2,1)}), bf16[4,64,720]{2,0,1:T(4,128)(2,1)S(1)}, u32[]{:S(2)}, u32[]{:S(2)}) async-start(bf16[4,64,720]{2,0,1:T(4,128)(2,1)} %copy.103), calls=%async_computation.5 | async-start | bytes 786432 | tf_op jit(solution)/shard_map/all_to_all | solution.py:67
  236.4 19.0 %all-to-all-done.5 = bf16[4,64,720]{2,0,1:T(4,128)(2,1)S(1)} async-done(((bf16[4,64,720]{2,0,1:T(4,128)(2,1)}), bf16[4,64,720]{2,0,1:T(4,128)(2,1)S(1)}, u32[]{:S(2)}, u32[]{:S(2)}) %all-to-all-start.5) | async-done | bytes 368672 | tf_op jit(solution)/shard_map/all_to_all | solution.py:67
  256.5 2.0 gather_fusion.1
  (86 shorter events, 25.1 us)
Async XLA Ops:
  6.5 5.4 %copy-start.1 = (bf16[128,2880]{0,1:T(8,128)(2,1)S(1)}, bf16[128,2880]{0,1:T(8,128)(2,1)}, u32[]{:S(2)}) copy-start(bf16[128,2880]{0,1:T(8,128)(2,1)} %param.6) | copy-start | bytes 2211844
  6.5 125.7 %all-gather.10.cloned.1.call-start = ((), (), s32[]{:S(2)}) async-start(), calls=%async_computation.6 | async-start | bytes 1884160 | tf_op jit(solution)/shard_map/all_gather | solution.py:56
  61.7 101.8 %all-gather.12.cloned.1.call-start = ((), (), s32[]{:S(2)}) async-start(), calls=%async_computation.7 | async-start | bytes 1884160 | tf_op jit(solution)/shard_map/all_gather | solution.py:56
  96.5 9.0 %copy-start = (bf16[1,1536,360]{1,2,0:T(8,128)(2,1)S(1)}, bf16[1,1536,360]{1,2,0:T(8,128)(2,1)}, u32[]{:S(2)}) copy-start(bf16[1,1536,360]{1,2,0:T(8,128)(2,1)} %param.11) | copy-start | bytes 3317764
  98.6 32.2 %all-to-all-start.4 = ((bf16[64,2,1440]{2,1,0:T(2,128)(2,1)}), bf16[64,2,1440]{2,1,0:T(2,128)(2,1)S(1)}, u32[]{:S(2)}, u32[]{:S(2)}) async-start(bf16[64,2,1440]{2,1,0:T(2,128)(2,1)} %reshape.249), calls=%async_computation.4 | async-start | bytes 786432 | tf_op jit(solution)/shard_map/all_to_all | solution.py:55
  105.4 94.6 %all-gather.14.cloned.1.call-start = ((), (), s32[]{:S(2)}) async-start(), calls=%async_computation.8 | async-start | bytes 1884160 | tf_op jit(solution)/shard_map/all_gather | solution.py:56
  105.5 7.2 %collective-permute-start.2 = (bf16[1536,360]{0,1:T(8,128)(2,1)S(1)}, bf16[1536,360]{0,1:T(8,128)(2,1)}, u32[]{:S(2)}, u32[]{:S(2)}) collective-permute-start(bf16[1536,360]{0,1:T(8,128)(2,1)S(1)} %bitcast.127), channel_id=1, source_target_pairs={{0,1},{1,0},{2,3},{3,2},{4,5},{5,4},{6,7},{7,6},{8,9},{9,8},{10,11... | collective-permute-start | bytes 3317768 | tf_op jit(solution)/shard_map/ppermute | solution.py:41
  107.4 24.8 %collective-permute-start.1 = (bf16[192,2880]{1,0:T(8,128)(2,1)}, bf16[192,2880]{1,0:T(8,128)(2,1)}, u32[]{:S(2)}, u32[]{:S(2)}) collective-permute-start(bf16[192,2880]{1,0:T(8,128)(2,1)} %bitcast.137), channel_id=1, source_target_pairs={{0,1},{1,0},{2,3},{3,2},{4,5},{5,4},{6,7},{7,6},{8,9},{9,8},{10,11... | collective-permute-start | bytes 3317768 | tf_op jit(solution)/shard_map/ppermute | solution.py:41
  109.8 25.6 %collective-permute-start = (bf16[192,2880]{1,0:T(8,128)(2,1)}, bf16[192,2880]{1,0:T(8,128)(2,1)}, u32[]{:S(2)}, u32[]{:S(2)}) collective-permute-start(bf16[192,2880]{1,0:T(8,128)(2,1)} %bitcast.141), channel_id=1, source_target_pairs={{0,1},{1,0},{2,3},{3,2},{4,5},{5,4},{6,7},{7,6},{8,9},{9,8},{10,11... | collective-permute-start | bytes 3317768 | tf_op jit(solution)/shard_map/ppermute | solution.py:41
  132.2 3.2 %copy-start.6 = (bf16[1,192,2880]{2,1,0:T(8,128)(2,1)S(1)}, bf16[1,192,2880]{2,1,0:T(8,128)(2,1)}, u32[]{:S(2)}) copy-start(bf16[1,192,2880]{2,1,0:T(8,128)(2,1)} %param.10) | copy-start | bytes 3317764
  132.2 3.2 %copy-start.4 = (bf16[256,1,2880]{2,0,1:T(8,128)(2,1)S(1)}, bf16[256,1,2880]{2,0,1:T(8,128)(2,1)}, u32[]{:S(2)}) copy-start(bf16[256,1,2880]{2,0,1:T(8,128)(2,1)} %all-gather.10.cloned.1.call-done) | copy-start | bytes 4423684
  156.9 27.9 %all-to-all-start.1 = ((bf16[4,64,720]{2,0,1:T(4,128)(2,1)}), bf16[4,64,720]{2,0,1:T(4,128)(2,1)S(1)}, u32[]{:S(2)}, u32[]{:S(2)}) async-start(bf16[4,64,720]{2,0,1:T(4,128)(2,1)} %copy.91), calls=%async_computation.1 | async-start | bytes 786432 | tf_op jit(solution)/shard_map/all_to_all | solution.py:67
  163.6 3.2 %copy-start.3 = (bf16[256,1,2880]{2,0,1:T(8,128)(2,1)S(1)}, bf16[256,1,2880]{2,0,1:T(8,128)(2,1)}, u32[]{:S(2)}) copy-start(bf16[256,1,2880]{2,0,1:T(8,128)(2,1)} %all-gather.12.cloned.1.call-done) | copy-start | bytes 4423684
  163.6 3.2 %copy-start.7 = (bf16[1,192,2880]{2,1,0:T(8,128)(2,1)S(1)}, bf16[1,192,2880]{2,1,0:T(8,128)(2,1)}, u32[]{:S(2)}) copy-start(bf16[1,192,2880]{2,1,0:T(8,128)(2,1)} %param.10) | copy-start | bytes 3317764
  184.8 36.3 %all-to-all-start.3 = ((bf16[4,64,720]{2,0,1:T(4,128)(2,1)}), bf16[4,64,720]{2,0,1:T(4,128)(2,1)S(1)}, u32[]{:S(2)}, u32[]{:S(2)}) async-start(bf16[4,64,720]{2,0,1:T(4,128)(2,1)} %copy.97), calls=%async_computation.3 | async-start | bytes 786432 | tf_op jit(solution)/shard_map/all_to_all | solution.py:67
  200.0 3.2 %copy-start.5 = (bf16[256,1,2880]{2,0,1:T(8,128)(2,1)S(1)}, bf16[256,1,2880]{2,0,1:T(8,128)(2,1)}, u32[]{:S(2)}) copy-start(bf16[256,1,2880]{2,0,1:T(8,128)(2,1)} %all-gather.14.cloned.1.call-done) | copy-start | bytes 4423684
  200.0 3.2 %copy-start.8 = (bf16[1,192,2880]{2,1,0:T(8,128)(2,1)S(1)}, bf16[1,192,2880]{2,1,0:T(8,128)(2,1)}, u32[]{:S(2)}) copy-start(bf16[1,192,2880]{2,1,0:T(8,128)(2,1)} %param.10) | copy-start | bytes 3317764
  219.8 16.4 %copy-start.2 = (s32[128,4]{0,1:T(4,128)S(1)}, s32[128,4]{0,1:T(4,128)}, u32[]{:S(2)}) copy-start(s32[128,4]{0,1:T(4,128)} %param.8) | copy-start | bytes 6148
  221.1 34.3 %all-to-all-start.5 = ((bf16[4,64,720]{2,0,1:T(4,128)(2,1)}), bf16[4,64,720]{2,0,1:T(4,128)(2,1)S(1)}, u32[]{:S(2)}, u32[]{:S(2)}) async-start(bf16[4,64,720]{2,0,1:T(4,128)(2,1)} %copy.103), calls=%async_computation.5 | async-start | bytes 786432 | tf_op jit(solution)/shard_map/all_to_all | solution.py:67
Sparse Core Ops, SparseCore 0:
  61.9 25.8 all-gather.9
  96.6 27.0 all-gather.11
  132.3 29.4 all-gather.13

commit v4 on v3

--- a/solution.py
+++ b/solution.py
@@ -7,6 +7,14 @@
 GROUP = "grp"
 CORE = "core"
 REP = "rep"
+
+
+def rep_shifts(value, n_rep):
+    pieces = [value]
+    for shift in range(1, n_rep):
+        pairs = [(source, (source + shift) % n_rep) for source in range(n_rep)]
+        pieces.append(lax.ppermute(value, REP, pairs))
+    return jnp.stack(pieces, axis=0)
 
 
 def on_device(tokens, expert_ids, gate_levels, w_gate, w_up, w_down):
@@ -48,18 +56,21 @@
     own_half = lax.dynamic_index_in_dim(down_split, core_index, 0, keepdims=False)
     other_half = lax.dynamic_index_in_dim(down_split, 1 - core_index, 0, keepdims=False)
     down_units = jnp.stack([own_half, other_half], axis=1).reshape(n_rep, 2 * quarter, col_count)
+    shift_source = (rep_index - jnp.arange(n_rep, dtype=jnp.int32)) % n_rep
+    down_units = jnp.take(down_units, shift_source, axis=0)
     contract = (((1,), (1,)), ((), ()))
 
     chunks = []
     for chunk in range(part):
         arrived = lax.all_to_all(outgoing[chunk], GROUP, 0, 0, tiled=True)
-        rows = lax.all_gather(arrived, REP, axis=0, tiled=False).reshape(-1, model_width)
+        rows = jnp.take(rep_shifts(arrived, n_rep), shift_source, axis=0)
+        rows = rows.reshape(-1, model_width)
         gate_proj = lax.dot_general(rows, gate_units, contract, preferred_element_type=jnp.float32)
         up_proj = lax.dot_general(rows, up_units, contract, preferred_element_type=jnp.float32)
         hidden = ((up_proj + 1.0) * gate_proj * jax.nn.sigmoid(1.702 * gate_proj)).astype(
             jnp.bfloat16
         )
-        hidden_all = lax.all_gather(hidden, REP, axis=0, tiled=False)
+        hidden_all = rep_shifts(hidden, n_rep)
         projected = jnp.einsum(
             "rnk,rkc->nc", hidden_all, down_units, preferred_element_type=jnp.float32
         )

time: 268 us -> 320 us (1.19)
  blocking collectives: 121 us -> 0 us
  starting transfers between devices: 50.2 us -> 147 us
  waiting for transfers between devices: 34.2 us -> 94.5 us
  local copies, waits for them, and re-layouts: 21.4 us -> 36.5 us
  between operations: 13.6 us -> 0.78 us
  other arithmetic: 7.89 us -> 19.8 us
    all_to_all x2 -> x0, blocking collectives: 76.9 us -> none  [on_device(): arrived = lax.all_to_all(outgoing[chunk], GROUP, 0, 0, tiled=True)]
    ppermute x0 -> x18, starting transfers between devices: none -> 66.8 us  [rep_shifts(): pieces.append(lax.ppermute(value, REP, pairs))]
    all_gather x3 -> x0, blocking collectives: 43.7 us -> none  [on_device(): hidden_all = lax.all_gather(hidden, REP, axis=0, tiled=False)]
    all_to_all x1 -> x3, waiting for transfers between devices: 15.1 us -> 48.1 us  [on_device(): arrived = lax.all_to_all(outgoing[chunk], GROUP, 0, 0, tiled=True)]
    all_to_all x1 -> x3, starting transfers between devices: 6.78 us -> 32.2 us  [on_device(): arrived = lax.all_to_all(outgoing[chunk], GROUP, 0, 0, tiled=True)]
    ppermute x0 -> x18, waiting for transfers between devices: none -> 18.6 us  [rep_shifts(): pieces.append(lax.ppermute(value, REP, pairs))]
    all_to_all x3, waiting for transfers between devices: 19 us -> 27.8 us  [on_device(): chunks.append(lax.all_to_all(expert_out, GROUP, 1, 1, tiled=True))]
    gather x0 -> x4, local copies, waits for them, and re-layouts: none -> 8.38 us  [the longest x3 6.1 us: on_device(): rows = jnp.take(rep_shifts(arrived, n_rep), shift_source, axis=0)]
  transfers between devices with their start and end apart: 10 -> 27, of which waited for: 2 -> 14; matrix products, arithmetic and copies ran while one was open for 12% -> 17% of each run, Pallas kernels for 0% -> 0%
where the time goes in v4:
time: 320 us; the launch traced here: 318 us
  starting transfers between devices  147 us (46%)
  waiting for transfers between devices  94.5 us (30%)
  local copies, waits for them, and re-layouts  36.5 us (11%)
  other arithmetic  19.8 us (6%)
  matrix products  19.2 us (6%)
    ppermute x18, starting transfers between devices, rep_shifts(): pieces.append(lax.ppermute(value, REP, pairs))  66.8 us
    all_to_all x3, waiting for transfers between devices, on_device(): arrived = lax.all_to_all(outgoing[chunk], GROUP, 0, 0, tiled=True)  48.1 us
    all_to_all x3, starting transfers between devices, on_device(): chunks.append(lax.all_to_all(expert_out, GROUP, 1, 1, tiled=True))  42 us
    all_to_all x3, starting transfers between devices, on_device(): arrived = lax.all_to_all(outgoing[chunk], GROUP, 0, 0, tiled=True)  32.2 us
    all_to_all x3, waiting for transfers between devices, on_device(): chunks.append(lax.all_to_all(expert_out, GROUP, 1, 1, tiled=True))  27.8 us
    ppermute x18, waiting for transfers between devices, rep_shifts(): pieces.append(lax.ppermute(value, REP, pairs))  18.6 us
    unnamed x41, local copies, waits for them, and re-layouts  11.3 us
    dot_general x3, matrix products, on_device(): lax.dot_general(rows, gate_units, contract, preferred_element_type=jnp.fl...  8.18 us
  transfers between devices with their start and end apart: 27, of which 14 were waited for; matrix products, arithmetic and copies ran while one was open for 17% of the time, Pallas kernels for 0%

profile of v4, /device:TPU:6, one launch (start us, length us, event | category | flops | bytes accessed | tf_op | source)
XLA Modules:
  0.0 318.0 jit_solution(4240722936531635019)
XLA Ops:
  9.7 18.8 %all-to-all-start = ((bf16[64,2,1440]{2,1,0:T(2,128)(2,1)}), bf16[64,2,1440]{2,1,0:T(2,128)(2,1)S(1)}, u32[]{:S(2)}, u32[]{:S(2)}) async-start(bf16[64,2,1440]{2,1,0:T(2,128)(2,1)} %reshape.364), calls=%async_computation | async-start | bytes 786432 | tf_op jit(solution)/shard_map/all_to_all | solution.py:65
  30.6 24.2 %all-to-all-done = bf16[64,2,1440]{2,1,0:T(2,128)(2,1)S(1)} async-done(((bf16[64,2,1440]{2,1,0:T(2,128)(2,1)}), bf16[64,2,1440]{2,1,0:T(2,128)(2,1)S(1)}, u32[]{:S(2)}, u32[]{:S(2)}) %all-to-all-start) | async-done | bytes 368672 | tf_op jit(solution)/shard_map/all_to_all | solution.py:65
  54.8 6.6 %all-to-all-start.2 = ((bf16[64,2,1440]{2,1,0:T(2,128)(2,1)}), bf16[64,2,1440]{2,1,0:T(2,128)(2,1)S(1)}, u32[]{:S(2)}, u32[]{:S(2)}) async-start(bf16[64,2,1440]{2,1,0:T(2,128)(2,1)} %reshape.362), calls=%async_computation.2 | async-start | bytes 786432 | tf_op jit(solution)/shard_map/all_to_all | solution.py:65
  63.5 23.5 %all-to-all-done.2 = bf16[64,2,1440]{2,1,0:T(2,128)(2,1)S(1)} async-done(((bf16[64,2,1440]{2,1,0:T(2,128)(2,1)}), bf16[64,2,1440]{2,1,0:T(2,128)(2,1)S(1)}, u32[]{:S(2)}, u32[]{:S(2)}) %all-to-all-start.2) | async-done | bytes 368672 | tf_op jit(solution)/shard_map/all_to_all | solution.py:65
  87.1 6.8 %all-to-all-start.4 = ((bf16[64,2,1440]{2,1,0:T(2,128)(2,1)}), bf16[64,2,1440]{2,1,0:T(2,128)(2,1)S(1)}, u32[]{:S(2)}, u32[]{:S(2)}) async-start(bf16[64,2,1440]{2,1,0:T(2,128)(2,1)} %reshape.360), calls=%async_computation.4 | async-start | bytes 786432 | tf_op jit(solution)/shard_map/all_to_all | solution.py:65
  99.6 5.1 %collective-permute-start.10 = (bf16[64,1,2880]{2,0,1:T(8,128)(2,1)}, bf16[64,1,2880]{2,0,1:T(8,128)(2,1)}, u32[]{:S(2)}, u32[]{:S(2)}) collective-permute-start(bf16[64,1,2880]{2,0,1:T(8,128)(2,1)} %copy.79), channel_id=1, source_target_pairs={{0,256},{128,384},{256,0},{384,128},{1,257},{129,385},{257,1},{385... | collective-permute-start | bytes 1105928 | tf_op jit(solution)/shard_map/ppermute | solution.py:16
  107.3 4.5 %collective-permute-start.11 = (bf16[64,1,2880]{2,0,1:T(8,128)(2,1)}, bf16[64,1,2880]{2,0,1:T(8,128)(2,1)}, u32[]{:S(2)}, u32[]{:S(2)}) collective-permute-start(bf16[64,1,2880]{2,0,1:T(8,128)(2,1)} %copy.79), channel_id=1, source_target_pairs={{0,384},{128,0},{256,128},{384,256},{1,385},{129,1},{257,129},{385... | collective-permute-start | bytes 1105928 | tf_op jit(solution)/shard_map/ppermute | solution.py:16
  121.4 5.1 %collective-permute-start.16 = (bf16[64,1,2880]{2,0,1:T(8,128)(2,1)}, bf16[64,1,2880]{2,0,1:T(8,128)(2,1)}, u32[]{:S(2)}, u32[]{:S(2)}) collective-permute-start(bf16[64,1,2880]{2,0,1:T(8,128)(2,1)} %copy.80), channel_id=1, source_target_pairs={{0,256},{128,384},{256,0},{384,128},{1,257},{129,385},{257,1},{385... | collective-permute-start | bytes 1105928 | tf_op jit(solution)/shard_map/ppermute | solution.py:16
  129.2 4.5 %collective-permute-start.17 = (bf16[64,1,2880]{2,0,1:T(8,128)(2,1)}, bf16[64,1,2880]{2,0,1:T(8,128)(2,1)}, u32[]{:S(2)}, u32[]{:S(2)}) collective-permute-start(bf16[64,1,2880]{2,0,1:T(8,128)(2,1)} %copy.80), channel_id=1, source_target_pairs={{0,384},{128,0},{256,128},{384,256},{1,385},{129,1},{257,129},{385... | collective-permute-start | bytes 1105928 | tf_op jit(solution)/shard_map/ppermute | solution.py:16
  136.8 5.0 %collective-permute-start.1 = (bf16[64,1,2880]{2,0,1:T(8,128)(2,1)}, bf16[64,1,2880]{2,0,1:T(8,128)(2,1)}, u32[]{:S(2)}, u32[]{:S(2)}) collective-permute-start(bf16[64,1,2880]{2,0,1:T(8,128)(2,1)} %copy.78), channel_id=1, source_target_pairs={{0,256},{128,384},{256,0},{384,128},{1,257},{129,385},{257,1},{385... | collective-permute-start | bytes 1105928 | tf_op jit(solution)/shard_map/ppermute | solution.py:16
  147.2 7.2 %collective-permute-start.2 = (bf16[64,1,2880]{2,0,1:T(8,128)(2,1)}, bf16[64,1,2880]{2,0,1:T(8,128)(2,1)}, u32[]{:S(2)}, u32[]{:S(2)}) collective-permute-start(bf16[64,1,2880]{2,0,1:T(8,128)(2,1)} %copy.78), channel_id=1, source_target_pairs={{0,384},{128,0},{256,128},{384,256},{1,385},{129,1},{257,129},{385... | collective-permute-start | bytes 1105928 | tf_op jit(solution)/shard_map/ppermute | solution.py:16
  162.9 3.2 %gather_fusion.3 = bf16[4,64,2880]{2,1,0:T(8,128)(2,1)} fusion(bf16[4,64,2880]{2,1,0:T(8,128)(2,1)} %maximum_bitcast_fusion, s32[1024]{0:T(1024)S(1)} %pad_clamp_fusion.2), kind=kCustom, calls=%fused_computation.clone | custom fusion | bytes 2949136 | tf_op jit(solution)/shard_map/jit(_take)/gather | solution.py:66
  166.2 3.6 %bitcast_select_fusion.2 = (bf16[4,64,1,2880]{3,1,0,2:T(8,128)(2,1)S(1)}, bf16[4,64,1,2880]{3,1,0,2:T(8,128)(2,1)}, bf16[4,64,1,2880]{3,1,0,2:T(8,128)(2,1)}) fusion(bf16[4,64,2880]{2,1,0:T(8,128)(2,1)} %gather_fusion.3, pred[4]{0:T(512)(128)(4,1)S(1)} %compare_and_fusion, bf16[4,64,2880]{2,1,0:T(8,128)(2,1)S(1)} %gather_fusion.4, ...), kind=kLoop, calls=%fused_computation.21 | loop fusion | flops 2211840 | bytes 8847364 | tf_op jit(solution)/shard_map/jit(_take)/select_n | solution.py:66
  174.5 5.3 %collective-permute-start.7 = (bf16[256,384]{1,0:T(8,128)(2,1)S(1)}, bf16[256,384]{1,0:T(8,128)(2,1)S(1)}, u32[]{:S(2)}, u32[]{:S(2)}) collective-permute-start(bf16[256,384]{1,0:T(8,128)(2,1)S(1)} %fusion.13), channel_id=1, source_target_pairs={{0,384},{128,0},{256,128},{384,256},{1,385},{129,1},{257,129},{385... | collective-permute-start | bytes 589832 | tf_op jit(solution)/shard_map/ppermute | solution.py:16
  187.1 3.0 copy.61
  196.1 15.4 %all-to-all-start.1 = ((bf16[4,64,720]{2,0,1:T(4,128)(2,1)}), bf16[4,64,720]{2,0,1:T(4,128)(2,1)S(1)}, u32[]{:S(2)}, u32[]{:S(2)}) async-start(bf16[4,64,720]{2,0,1:T(4,128)(2,1)} %copy.63), calls=%async_computation.1 | async-start | bytes 786432 | tf_op jit(solution)/shard_map/all_to_all | solution.py:78
  216.7 3.8 %collective-permute-start.20 = (bf16[256,384]{1,0:T(8,128)(2,1)S(1)}, bf16[256,384]{1,0:T(8,128)(2,1)S(1)}, u32[]{:S(2)}, u32[]{:S(2)}) collective-permute-start(bf16[256,384]{1,0:T(8,128)(2,1)S(1)} %fusion.15), channel_id=1, source_target_pairs={{0,384},{128,0},{256,128},{384,256},{1,385},{129,1},{257,129},{385... | collective-permute-start | bytes 589832 | tf_op jit(solution)/shard_map/ppermute | solution.py:16
  220.6 4.2 %collective-permute-start.19 = (bf16[256,384]{1,0:T(8,128)(2,1)S(1)}, bf16[256,384]{1,0:T(8,128)(2,1)S(1)}, u32[]{:S(2)}, u32[]{:S(2)}) collective-permute-start(bf16[256,384]{1,0:T(8,128)(2,1)S(1)} %fusion.15), channel_id=1, source_target_pairs={{0,256},{128,384},{256,0},{384,128},{1,257},{129,385},{257,1},{385... | collective-permute-start | bytes 589832 | tf_op jit(solution)/shard_map/ppermute | solution.py:16
  226.7 4.7 %collective-permute-done.19 = bf16[256,384]{1,0:T(8,128)(2,1)S(1)} collective-permute-done((bf16[256,384]{1,0:T(8,128)(2,1)S(1)}, bf16[256,384]{1,0:T(8,128)(2,1)S(1)}, u32[]{:S(2)}, u32[]{:S(2)}) %collective-permute-start.19) | collective-permute-done | bytes 196640 | tf_op jit(solution)/shard_map/ppermute | solution.py:16
  236.9 14.0 %all-to-all-start.5 = ((bf16[4,64,720]{2,0,1:T(4,128)(2,1)}), bf16[4,64,720]{2,0,1:T(4,128)(2,1)S(1)}, u32[]{:S(2)}, u32[]{:S(2)}) async-start(bf16[4,64,720]{2,0,1:T(4,128)(2,1)} %copy.75), calls=%async_computation.5 | async-start | bytes 786432 | tf_op jit(solution)/shard_map/all_to_all | solution.py:78
  250.9 3.2 fusion.38
  264.8 4.5 %collective-permute-done.13 = bf16[256,384]{1,0:T(8,128)(2,1)S(1)} collective-permute-done((bf16[256,384]{1,0:T(8,128)(2,1)S(1)}, bf16[256,384]{1,0:T(8,128)(2,1)S(1)}, u32[]{:S(2)}, u32[]{:S(2)}) %collective-permute-start.13) | collective-permute-done | bytes 196640 | tf_op jit(solution)/shard_map/ppermute | solution.py:16
  275.6 12.6 %all-to-all-start.3 = ((bf16[4,64,720]{2,0,1:T(4,128)(2,1)}), bf16[4,64,720]{2,0,1:T(4,128)(2,1)S(1)}, u32[]{:S(2)}, u32[]{:S(2)}) async-start(bf16[4,64,720]{2,0,1:T(4,128)(2,1)} %copy.69), calls=%async_computation.3 | async-start | bytes 786432 | tf_op jit(solution)/shard_map/all_to_all | solution.py:78
  288.4 24.2 %all-to-all-done.3 = bf16[4,64,720]{2,0,1:T(4,128)(2,1)S(1)} async-done(((bf16[4,64,720]{2,0,1:T(4,128)(2,1)}), bf16[4,64,720]{2,0,1:T(4,128)(2,1)S(1)}, u32[]{:S(2)}, u32[]{:S(2)}) %all-to-all-start.3) | async-done | bytes 368672 | tf_op jit(solution)/shard_map/all_to_all | solution.py:78
  (136 shorter events, 104.2 us)
Async XLA Ops:
  9.7 45.1 %all-to-all-start = ((bf16[64,2,1440]{2,1,0:T(2,128)(2,1)}), bf16[64,2,1440]{2,1,0:T(2,128)(2,1)S(1)}, u32[]{:S(2)}, u32[]{:S(2)}) async-start(bf16[64,2,1440]{2,1,0:T(2,128)(2,1)} %reshape.364), calls=%async_computation | async-start | bytes 786432 | tf_op jit(solution)/shard_map/all_to_all | solution.py:65
  54.8 32.2 %all-to-all-start.2 = ((bf16[64,2,1440]{2,1,0:T(2,128)(2,1)}), bf16[64,2,1440]{2,1,0:T(2,128)(2,1)S(1)}, u32[]{:S(2)}, u32[]{:S(2)}) async-start(bf16[64,2,1440]{2,1,0:T(2,128)(2,1)} %reshape.362), calls=%async_computation.2 | async-start | bytes 786432 | tf_op jit(solution)/shard_map/all_to_all | solution.py:65
  87.1 32.2 %all-to-all-start.4 = ((bf16[64,2,1440]{2,1,0:T(2,128)(2,1)}), bf16[64,2,1440]{2,1,0:T(2,128)(2,1)S(1)}, u32[]{:S(2)}, u32[]{:S(2)}) async-start(bf16[64,2,1440]{2,1,0:T(2,128)(2,1)} %reshape.360), calls=%async_computation.4 | async-start | bytes 786432 | tf_op jit(solution)/shard_map/all_to_all | solution.py:65
  93.9 19.4 %collective-permute-start.8 = (bf16[1536,360]{0,1:T(8,128)(2,1)S(1)}, bf16[1536,360]{0,1:T(8,128)(2,1)}, u32[]{:S(2)}, u32[]{:S(2)}) collective-permute-start(bf16[1536,360]{0,1:T(8,128)(2,1)S(1)} %bitcast.133), channel_id=1, source_target_pairs={{0,1},{1,0},{2,3},{3,2},{4,5},{5,4},{6,7},{7,6},{8,9},{9,8},{10,11... | collective-permute-start | bytes 3317768 | tf_op jit(solution)/shard_map/ppermute | solution.py:49
  95.8 74.0 %collective-permute-start.4 = (bf16[192,2880]{1,0:T(8,128)(2,1)}, bf16[192,2880]{1,0:T(8,128)(2,1)}, u32[]{:S(2)}, u32[]{:S(2)}) collective-permute-start(bf16[192,2880]{1,0:T(8,128)(2,1)} %bitcast.140), channel_id=1, source_target_pairs={{0,1},{1,0},{2,3},{3,2},{4,5},{5,4},{6,7},{7,6},{8,9},{9,8},{10,11... | collective-permute-start | bytes 3317768 | tf_op jit(solution)/shard_map/ppermute | solution.py:49
  99.6 21.8 %collective-permute-start.10 = (bf16[64,1,2880]{2,0,1:T(8,128)(2,1)}, bf16[64,1,2880]{2,0,1:T(8,128)(2,1)}, u32[]{:S(2)}, u32[]{:S(2)}) collective-permute-start(bf16[64,1,2880]{2,0,1:T(8,128)(2,1)} %copy.79), channel_id=1, source_target_pairs={{0,256},{128,384},{256,0},{384,128},{1,257},{129,385},{257,1},{385... | collective-permute-start | bytes 1105928 | tf_op jit(solution)/shard_map/ppermute | solution.py:16
  104.7 21.9 %collective-permute-start.9 = (bf16[64,1,2880]{2,0,1:T(8,128)(2,1)}, bf16[64,1,2880]{2,0,1:T(8,128)(2,1)}, u32[]{:S(2)}, u32[]{:S(2)}) collective-permute-start(bf16[64,1,2880]{2,0,1:T(8,128)(2,1)} %copy.79), channel_id=1, source_target_pairs={{0,128},{128,256},{256,384},{384,0},{1,129},{129,257},{257,385},{3... | collective-permute-start | bytes 1105928 | tf_op jit(solution)/shard_map/ppermute | solution.py:16
  107.3 21.9 %collective-permute-start.11 = (bf16[64,1,2880]{2,0,1:T(8,128)(2,1)}, bf16[64,1,2880]{2,0,1:T(8,128)(2,1)}, u32[]{:S(2)}, u32[]{:S(2)}) collective-permute-start(bf16[64,1,2880]{2,0,1:T(8,128)(2,1)} %copy.79), channel_id=1, source_target_pairs={{0,384},{128,0},{256,128},{384,256},{1,385},{129,1},{257,129},{385... | collective-permute-start | bytes 1105928 | tf_op jit(solution)/shard_map/ppermute | solution.py:16
  113.2 58.9 %collective-permute-start.3 = (bf16[192,2880]{1,0:T(8,128)(2,1)}, bf16[192,2880]{1,0:T(8,128)(2,1)}, u32[]{:S(2)}, u32[]{:S(2)}) collective-permute-start(bf16[192,2880]{1,0:T(8,128)(2,1)} %bitcast.144), channel_id=1, source_target_pairs={{0,1},{1,0},{2,3},{3,2},{4,5},{5,4},{6,7},{7,6},{8,9},{9,8},{10,11... | collective-permute-start | bytes 3317768 | tf_op jit(solution)/shard_map/ppermute | solution.py:49
  121.4 15.4 %collective-permute-start.16 = (bf16[64,1,2880]{2,0,1:T(8,128)(2,1)}, bf16[64,1,2880]{2,0,1:T(8,128)(2,1)}, u32[]{:S(2)}, u32[]{:S(2)}) collective-permute-start(bf16[64,1,2880]{2,0,1:T(8,128)(2,1)} %copy.80), channel_id=1, source_target_pairs={{0,256},{128,384},{256,0},{384,128},{1,257},{129,385},{257,1},{385... | collective-permute-start | bytes 1105928 | tf_op jit(solution)/shard_map/ppermute | solution.py:16
  126.6 18.3 %collective-permute-start.15 = (bf16[64,1,2880]{2,0,1:T(8,128)(2,1)}, bf16[64,1,2880]{2,0,1:T(8,128)(2,1)}, u32[]{:S(2)}, u32[]{:S(2)}) collective-permute-start(bf16[64,1,2880]{2,0,1:T(8,128)(2,1)} %copy.80), channel_id=1, source_target_pairs={{0,128},{128,256},{256,384},{384,0},{1,129},{129,257},{257,385},{3... | collective-permute-start | bytes 1105928 | tf_op jit(solution)/shard_map/ppermute | solution.py:16
  129.2 18.0 %collective-permute-start.17 = (bf16[64,1,2880]{2,0,1:T(8,128)(2,1)}, bf16[64,1,2880]{2,0,1:T(8,128)(2,1)}, u32[]{:S(2)}, u32[]{:S(2)}) collective-permute-start(bf16[64,1,2880]{2,0,1:T(8,128)(2,1)} %copy.80), channel_id=1, source_target_pairs={{0,384},{128,0},{256,128},{384,256},{1,385},{129,1},{257,129},{385... | collective-permute-start | bytes 1105928 | tf_op jit(solution)/shard_map/ppermute | solution.py:16
  136.8 22.5 %collective-permute-start.1 = (bf16[64,1,2880]{2,0,1:T(8,128)(2,1)}, bf16[64,1,2880]{2,0,1:T(8,128)(2,1)}, u32[]{:S(2)}, u32[]{:S(2)}) collective-permute-start(bf16[64,1,2880]{2,0,1:T(8,128)(2,1)} %copy.78), channel_id=1, source_target_pairs={{0,256},{128,384},{256,0},{384,128},{1,257},{129,385},{257,1},{385... | collective-permute-start | bytes 1105928 | tf_op jit(solution)/shard_map/ppermute | solution.py:16
  144.8 15.5 %collective-permute-start = (bf16[64,1,2880]{2,0,1:T(8,128)(2,1)}, bf16[64,1,2880]{2,0,1:T(8,128)(2,1)}, u32[]{:S(2)}, u32[]{:S(2)}) collective-permute-start(bf16[64,1,2880]{2,0,1:T(8,128)(2,1)} %copy.78), channel_id=1, source_target_pairs={{0,128},{128,256},{256,384},{384,0},{1,129},{129,257},{257,385},{3... | collective-permute-start | bytes 1105928 | tf_op jit(solution)/shard_map/ppermute | solution.py:16
  147.2 13.1 %collective-permute-start.2 = (bf16[64,1,2880]{2,0,1:T(8,128)(2,1)}, bf16[64,1,2880]{2,0,1:T(8,128)(2,1)}, u32[]{:S(2)}, u32[]{:S(2)}) collective-permute-start(bf16[64,1,2880]{2,0,1:T(8,128)(2,1)} %copy.78), channel_id=1, source_target_pairs={{0,384},{128,0},{256,128},{384,256},{1,385},{129,1},{257,129},{385... | collective-permute-start | bytes 1105928 | tf_op jit(solution)/shard_map/ppermute | solution.py:16
  174.5 17.9 %collective-permute-start.7 = (bf16[256,384]{1,0:T(8,128)(2,1)S(1)}, bf16[256,384]{1,0:T(8,128)(2,1)S(1)}, u32[]{:S(2)}, u32[]{:S(2)}) collective-permute-start(bf16[256,384]{1,0:T(8,128)(2,1)S(1)} %fusion.13), channel_id=1, source_target_pairs={{0,384},{128,0},{256,128},{384,256},{1,385},{129,1},{257,129},{385... | collective-permute-start | bytes 589832 | tf_op jit(solution)/shard_map/ppermute | solution.py:16
  179.9 12.6 %collective-permute-start.6 = (bf16[256,384]{1,0:T(8,128)(2,1)S(1)}, bf16[256,384]{1,0:T(8,128)(2,1)S(1)}, u32[]{:S(2)}, u32[]{:S(2)}) collective-permute-start(bf16[256,384]{1,0:T(8,128)(2,1)S(1)} %fusion.13), channel_id=1, source_target_pairs={{0,256},{128,384},{256,0},{384,128},{1,257},{129,385},{257,1},{385... | collective-permute-start | bytes 589832 | tf_op jit(solution)/shard_map/ppermute | solution.py:16
  181.8 10.7 %collective-permute-start.5 = (bf16[256,384]{1,0:T(8,128)(2,1)S(1)}, bf16[256,384]{1,0:T(8,128)(2,1)S(1)}, u32[]{:S(2)}, u32[]{:S(2)}) collective-permute-start(bf16[256,384]{1,0:T(8,128)(2,1)S(1)} %fusion.13), channel_id=1, source_target_pairs={{0,128},{128,256},{256,384},{384,0},{1,129},{129,257},{257,385},{3... | collective-permute-start | bytes 589832 | tf_op jit(solution)/shard_map/ppermute | solution.py:16
  196.1 40.8 %all-to-all-start.1 = ((bf16[4,64,720]{2,0,1:T(4,128)(2,1)}), bf16[4,64,720]{2,0,1:T(4,128)(2,1)S(1)}, u32[]{:S(2)}, u32[]{:S(2)}) async-start(bf16[4,64,720]{2,0,1:T(4,128)(2,1)} %copy.63), calls=%async_computation.1 | async-start | bytes 786432 | tf_op jit(solution)/shard_map/all_to_all | solution.py:78
  216.7 10.0 %collective-permute-start.20 = (bf16[256,384]{1,0:T(8,128)(2,1)S(1)}, bf16[256,384]{1,0:T(8,128)(2,1)S(1)}, u32[]{:S(2)}, u32[]{:S(2)}) collective-permute-start(bf16[256,384]{1,0:T(8,128)(2,1)S(1)} %fusion.15), channel_id=1, source_target_pairs={{0,384},{128,0},{256,128},{384,256},{1,385},{129,1},{257,129},{385... | collective-permute-start | bytes 589832 | tf_op jit(solution)/shard_map/ppermute | solution.py:16
  220.6 10.8 %collective-permute-start.19 = (bf16[256,384]{1,0:T(8,128)(2,1)S(1)}, bf16[256,384]{1,0:T(8,128)(2,1)S(1)}, u32[]{:S(2)}, u32[]{:S(2)}) collective-permute-start(bf16[256,384]{1,0:T(8,128)(2,1)S(1)} %fusion.15), channel_id=1, source_target_pairs={{0,256},{128,384},{256,0},{384,128},{1,257},{129,385},{257,1},{385... | collective-permute-start | bytes 589832 | tf_op jit(solution)/shard_map/ppermute | solution.py:16
  236.9 38.7 %all-to-all-start.5 = ((bf16[4,64,720]{2,0,1:T(4,128)(2,1)}), bf16[4,64,720]{2,0,1:T(4,128)(2,1)S(1)}, u32[]{:S(2)}, u32[]{:S(2)}) async-start(bf16[4,64,720]{2,0,1:T(4,128)(2,1)} %copy.75), calls=%async_computation.5 | async-start | bytes 786432 | tf_op jit(solution)/shard_map/all_to_all | solution.py:78
  258.5 10.8 %collective-permute-start.13 = (bf16[256,384]{1,0:T(8,128)(2,1)S(1)}, bf16[256,384]{1,0:T(8,128)(2,1)S(1)}, u32[]{:S(2)}, u32[]{:S(2)}) collective-permute-start(bf16[256,384]{1,0:T(8,128)(2,1)S(1)} %fusion.14), channel_id=1, source_target_pairs={{0,256},{128,384},{256,0},{384,128},{1,257},{129,385},{257,1},{385... | collective-permute-start | bytes 589832 | tf_op jit(solution)/shard_map/ppermute | solution.py:16
  275.6 37.0 %all-to-all-start.3 = ((bf16[4,64,720]{2,0,1:T(4,128)(2,1)}), bf16[4,64,720]{2,0,1:T(4,128)(2,1)S(1)}, u32[]{:S(2)}, u32[]{:S(2)}) async-start(bf16[4,64,720]{2,0,1:T(4,128)(2,1)} %copy.69), calls=%async_computation.3 | async-start | bytes 786432 | tf_op jit(solution)/shard_map/all_to_all | solution.py:78
  (16 other events, 190.7 us)

commit v5 on v3

--- a/solution.py
+++ b/solution.py
@@ -50,9 +50,16 @@
     down_units = jnp.stack([own_half, other_half], axis=1).reshape(n_rep, 2 * quarter, col_count)
     contract = (((1,), (1,)), ((), ()))
 
+    lead = max(1, part - part // 2)
+    spans = [(0, lead)] + ([(lead, part - lead)] if part > lead else [])
     chunks = []
-    for chunk in range(part):
-        arrived = lax.all_to_all(outgoing[chunk], GROUP, 0, 0, tiled=True)
+    pick = jnp.zeros_like(slot_index)
+    offset = 0
+    plane = slot_index // part
+    within = slot_index % part
+    for first, size in spans:
+        sending = outgoing[first:first + size].reshape(size, expert_count, model_width)
+        arrived = lax.all_to_all(sending, GROUP, 1, 1, tiled=True)
         rows = lax.all_gather(arrived, REP, axis=0, tiled=False).reshape(-1, model_width)
         gate_proj = lax.dot_general(rows, gate_units, contract, preferred_element_type=jnp.float32)
         up_proj = lax.dot_general(rows, up_units, contract, preferred_element_type=jnp.float32)
@@ -63,11 +70,15 @@
         projected = jnp.einsum(
             "rnk,rkc->nc", hidden_all, down_units, preferred_element_type=jnp.float32
         )
-        expert_out = projected.astype(jnp.bfloat16).reshape(n_rep, expert_count, col_count)
-        chunks.append(lax.all_to_all(expert_out, GROUP, 1, 1, tiled=True))
+        expert_out = projected.astype(jnp.bfloat16).reshape(n_rep, size, expert_count, col_count)
+        back = lax.all_to_all(expert_out, GROUP, 2, 2, tiled=True)
+        chunks.append(back.reshape(-1, col_count))
+        here = offset + (plane * size + within - first) * expert_count + flat_ids
+        in_span = (within >= first) & (within < first + size)
+        pick = jnp.where(in_span, here, pick)
+        offset += n_rep * size * expert_count
 
-    returned = jnp.stack(chunks, axis=0).reshape(-1, col_count)
-    pick = ((slot_index % part) * n_rep + slot_index // part) * expert_count + flat_ids
+    returned = jnp.concatenate(chunks, axis=0)
     picked = returned[pick].astype(jnp.float32)
     levels = gate_levels.astype(jnp.float32)
     mixing = (levels / jnp.sum(levels, axis=1, keepdims=True)).reshape(-1, 1)

time: 268 us -> 270 us (level)
  waiting for transfers between devices: 34.2 us -> 100 us
  blocking collectives: 121 us -> 74 us
  starting transfers between devices: 50.2 us -> 36 us
    all_to_all x4 -> x3, waiting for transfers between devices: 34.1 us -> 81.9 us  [the longest x2 57.8 us: on_device(): back = lax.all_to_all(expert_out, GROUP, 2, 2, tiled=True)]
    all_gather x3 -> x1, blocking collectives: 43.7 us -> 14 us  [on_device(): hidden_all = lax.all_gather(hidden, REP, axis=0, tiled=False)]
    all_gather x3 -> x2, waiting for transfers between devices: 0.06 us -> 18.1 us  [on_device(): lax.all_gather(arrived, REP, axis=0, tiled=False).reshape(-1, model_width)]
    all_to_all x2 -> x1, blocking collectives: 76.9 us -> 59.9 us  [on_device(): arrived = lax.all_to_all(sending, GROUP, 1, 1, tiled=True)]
    all_to_all x4 -> x3, starting transfers between devices: 43.7 us -> 29.4 us  [the longest x2 22.8 us: on_device(): back = lax.all_to_all(expert_out, GROUP, 2, 2, tiled=True)]
    unnamed x0 -> x1, other arithmetic: none -> 2.98 us
    dot_general x3 -> x2, matrix products: 9.48 us -> 7.22 us  [on_device(): lax.dot_general(rows, gate_units, contract, preferred_element_type=jnp.fl...]
    dot_general x3 -> x2, matrix products: 6.73 us -> 6.17 us  [on_device(): lax.dot_general(rows, up_units, contract, preferred_element_type=jnp.floa...]
  transfers between devices with their start and end apart: 10 -> 9, of which waited for: 2 -> 4; matrix products, arithmetic and copies ran while one was open for 12% -> 12% of each run, Pallas kernels for 0% -> 0%
where the time goes in v5:
time: 270 us; the launch traced here: 269 us
  waiting for transfers between devices  100 us (37%)
  blocking collectives  74 us (27%)
  starting transfers between devices  36 us (13%)
  local copies, waits for them, and re-layouts  19.9 us (7%)
  matrix products  17.2 us (6%)
  between operations  13.5 us (5%)
  other arithmetic  8.48 us (3%)
    all_to_all x1, blocking collectives, on_device(): arrived = lax.all_to_all(sending, GROUP, 1, 1, tiled=True)  59.9 us
    all_to_all x2, waiting for transfers between devices, on_device(): back = lax.all_to_all(expert_out, GROUP, 2, 2, tiled=True)  57.8 us
    all_to_all x1, waiting for transfers between devices, on_device(): arrived = lax.all_to_all(sending, GROUP, 1, 1, tiled=True)  24.1 us
    all_to_all x2, starting transfers between devices, on_device(): back = lax.all_to_all(expert_out, GROUP, 2, 2, tiled=True)  22.8 us
    all_gather x2, waiting for transfers between devices, on_device(): lax.all_gather(arrived, REP, axis=0, tiled=False).reshape(-1, model_width)  18.1 us
    all_gather x1, blocking collectives, on_device(): hidden_all = lax.all_gather(hidden, REP, axis=0, tiled=False)  14 us
    dot_general x2, matrix products, on_device(): lax.dot_general(rows, gate_units, contract, preferred_element_type=jnp.fl...  7.22 us
    all_to_all x1, starting transfers between devices, on_device(): arrived = lax.all_to_all(sending, GROUP, 1, 1, tiled=True)  6.64 us
  transfers between devices with their start and end apart: 9, of which 4 were waited for; matrix products, arithmetic and copies ran while one was open for 12% of the time, Pallas kernels for 0%

profile of v5, /device:TPU:6, one launch (start us, length us, event | category | flops | bytes accessed | tf_op | source)
XLA Modules:
  0.0 269.2 jit_solution(2684396723781095330)
XLA Ops:
  9.4 2.4 scatter_custom_fusion
  11.8 1.5 copy.54
  13.3 1.3 gather_fusion
  15.5 59.9 %all_to_all.20 = bf16[2,64,2880]{2,0,1:T(2,128)(2,1)S(1)} all-to-all(bf16[2,64,2880]{2,0,1:T(2,128)(2,1)S(1)} %copy.55), channel_id=1, replica_groups=mesh['rep'=4,'grp'=64,'core'=2] {'grp'}, dimensions={1} | all-to-all | bytes 1474560 | tf_op jit(solution)/shard_map/all_to_all | solution.py:62
  77.7 3.0 %reduce.2 = bf16[64,2880]{1,0:T(8,128)(2,1)S(1)} reduce(bf16[64,1,2880]{2,1,0:T(2,128)(2,1)S(1)} %bitcast.69, bf16[]{:T(256)} %broadcast.306), dimensions={1}, to_apply=%bitcast.63.reduce_sub_computation | reduce | bytes 737282
  81.9 6.6 %all-to-all-start.2 = ((bf16[64,2,1440]{2,1,0:T(2,128)(2,1)}), bf16[64,2,1440]{2,1,0:T(2,128)(2,1)S(1)}, u32[]{:S(2)}, u32[]{:S(2)}) async-start(bf16[64,2,1440]{2,1,0:T(2,128)(2,1)} %reshape.292), calls=%async_computation.2 | async-start | bytes 786432 | tf_op jit(solution)/shard_map/all_to_all | solution.py:62
  88.6 1.9 collective-permute-start.2
  90.5 24.1 %all-to-all-done.2 = bf16[64,2,1440]{2,1,0:T(2,128)(2,1)S(1)} async-done(((bf16[64,2,1440]{2,1,0:T(2,128)(2,1)}), bf16[64,2,1440]{2,1,0:T(2,128)(2,1)S(1)}, u32[]{:S(2)}, u32[]{:S(2)}) %all-to-all-start.2) | async-done | bytes 368672 | tf_op jit(solution)/shard_map/all_to_all | solution.py:62
  116.0 1.9 collective-permute-start.1
  118.0 2.6 collective-permute-start
  122.1 1.9 fusion.15
  124.0 4.4 %fusion.1 = f32[512,384]{1,0:T(8,128)S(1)} fusion(bf16[512,2880]{1,0:T(8,128)(2,1)} %bitcast.84, bf16[192,2880]{1,0:T(8,128)(2,1)} %collective-permute-done.1, bf16[192,2880]{1,0:T(8,128)(2,1)} %bitcast.90), kind=kOutput, calls=%fused_computation.13 | convolution fusion | flops 1136885760 | bytes 5947392 | tf_op jit(solution)/shard_map/dot_general | solution.py:64
  128.5 3.9 %fusion.7 = bf16[512,384]{1,0:T(8,128)(2,1)} fusion(f32[512,384]{1,0:T(8,128)S(1)} %fusion.1, bf16[512,2880]{1,0:T(8,128)(2,1)S(1)} %bitcast.85, bf16[192,2880]{1,0:T(8,128)(2,1)} %collective-permute-done, bf16[192,2880]{1,0:T(8,128)(2,1)S(1)} %bitcast.93), kind=kOutput, calls=%fused_computation.20 | convolution fusion | flops 1138458624 | bytes 6340608 | tf_op jit(solution)/shard_map/dot_general | solution.py:65
  132.8 18.1 %all-gather.12.cloned.1.call-done = bf16[4,64,2880]{2,1,0:T(8,128)(2,1)} async-done(((bf16[1,64,2880]{2,1,0:T(8,128)(2,1)}), bf16[4,64,2880]{2,1,0:T(8,128)(2,1)}) %all-gather.12.cloned.1.call-update) | async-done | bytes 1474576 | tf_op jit(solution)/shard_map/all_gather | solution.py:63
  151.0 2.8 %fusion = f32[256,384]{1,0:T(8,128)S(1)} fusion(bf16[256,2880]{1,0:T(8,128)(2,1)} %bitcast.87, bf16[192,2880]{1,0:T(8,128)(2,1)} %collective-permute-done.1, bf16[192,2880]{1,0:T(8,128)(2,1)S(1)} %bitcast.91), kind=kOutput, calls=%fused_computation.12 | convolution fusion | flops 570654720 | bytes 4079616 | tf_op jit(solution)/shard_map/dot_general | solution.py:64
  153.8 2.2 fusion.16
  156.1 14.0 %all-gather.3 = bf16[1024,384]{1,0:T(8,128)(2,1)S(1)} all-gather(bf16[256,384]{1,0:T(8,128)(2,1)S(1)} %fusion.16), channel_id=5, replica_groups=mesh['rep'=4,'grp'=64,'core'=2] {'rep'}, dimensions={0}, use_global_device_ids=true | all-gather | bytes 983040 | tf_op jit(solution)/shard_map/all_gather | solution.py:69
  172.4 15.9 %all-to-all-start.3 = ((bf16[4,1,64,720]{3,0,1,2:T(4,128)(2,1)}), bf16[4,1,64,720]{3,0,1,2:T(4,128)(2,1)S(1)}, u32[]{:S(2)}, u32[]{:S(2)}) async-start(bf16[4,1,64,720]{3,0,1,2:T(4,128)(2,1)} %copy.68), calls=%async_computation.3 | async-start | bytes 786432 | tf_op jit(solution)/shard_map/all_to_all | solution.py:74
  188.4 2.8 %bitcast_convert_fusion = bf16[512,720]{0,1:T(8,128)(2,1)S(1)} fusion(bf16[4,512,384]{2,1,0:T(8,128)(2,1)} %bitcast.86, bf16[4,384,720]{2,1,0:T(8,128)(2,1)S(1)} %bitcast.73), kind=kOutput, calls=%fused_computation.11 | convolution fusion | flops 1132830720 | bytes 4521984 | tf_op jit(solution)/shard_map/rnk,rkc->nc/dot_general | solution.py:70
  191.4 1.7 copy.62
  193.1 18.7 %all-to-all-done.3 = bf16[4,1,64,720]{3,0,1,2:T(4,128)(2,1)S(1)} async-done(((bf16[4,1,64,720]{3,0,1,2:T(4,128)(2,1)}), bf16[4,1,64,720]{3,0,1,2:T(4,128)(2,1)S(1)}, u32[]{:S(2)}, u32[]{:S(2)}) %all-to-all-start.3) | async-done | bytes 368672 | tf_op jit(solution)/shard_map/all_to_all | solution.py:74
  211.8 6.9 %all-to-all-start.1 = ((bf16[4,2,64,720]{3,1,0,2:T(2,128)(2,1)}), bf16[4,2,64,720]{3,1,0,2:T(2,128)(2,1)S(1)}, u32[]{:S(2)}, u32[]{:S(2)}) async-start(bf16[4,2,64,720]{3,1,0,2:T(2,128)(2,1)} %copy.62), calls=%async_computation.1 | async-start | bytes 1572864 | tf_op jit(solution)/shard_map/all_to_all | solution.py:74
  218.9 39.1 %all-to-all-done.1 = bf16[4,2,64,720]{3,1,0,2:T(2,128)(2,1)S(1)} async-done(((bf16[4,2,64,720]{3,1,0,2:T(2,128)(2,1)}), bf16[4,2,64,720]{3,1,0,2:T(2,128)(2,1)S(1)}, u32[]{:S(2)}, u32[]{:S(2)}) %all-to-all-start.1) | async-done | bytes 737312 | tf_op jit(solution)/shard_map/all_to_all | solution.py:74
  258.3 2.0 gather_fusion.1
  (71 shorter events, 15.7 us)
Async XLA Ops:
  6.5 117.5 %all-gather.8.cloned.1.call-start = ((), (), s32[]{:S(2)}) async-start(), calls=%async_computation.4 | async-start | bytes 3768320 | tf_op jit(solution)/shard_map/all_gather | solution.py:63
  77.1 11.4 %copy-start.1 = (bf16[1,1536,360]{1,2,0:T(8,128)(2,1)S(1)}, bf16[1,1536,360]{1,2,0:T(8,128)(2,1)}, u32[]{:S(2)}) copy-start(bf16[1,1536,360]{1,2,0:T(8,128)(2,1)} %param.11) | copy-start | bytes 3317764
  81.9 32.7 %all-to-all-start.2 = ((bf16[64,2,1440]{2,1,0:T(2,128)(2,1)}), bf16[64,2,1440]{2,1,0:T(2,128)(2,1)S(1)}, u32[]{:S(2)}, u32[]{:S(2)}) async-start(bf16[64,2,1440]{2,1,0:T(2,128)(2,1)} %reshape.292), calls=%async_computation.2 | async-start | bytes 786432 | tf_op jit(solution)/shard_map/all_to_all | solution.py:62
  88.5 62.5 %all-gather.12.cloned.1.call-start = ((), (), s32[]{:S(2)}) async-start(), calls=%async_computation.6 | async-start | bytes 1884160 | tf_op jit(solution)/shard_map/all_gather | solution.py:63
  88.6 32.7 %collective-permute-start.2 = (bf16[1536,360]{0,1:T(8,128)(2,1)S(1)}, bf16[1536,360]{0,1:T(8,128)(2,1)S(1)}, u32[]{:S(2)}, u32[]{:S(2)}) collective-permute-start(bf16[1536,360]{0,1:T(8,128)(2,1)S(1)} %bitcast.76), channel_id=1, source_target_pairs={{0,1},{1,0},{2,3},{3,2},{4,5},{5,4},{6,7},{7,6},{8,9},{9,8},{10,11... | collective-permute-start | bytes 3317768 | tf_op jit(solution)/shard_map/ppermute | solution.py:41
  116.0 72.4 %all-gather.10.cloned.1.call-start = ((), (), s32[]{:S(2)}) async-start(), calls=%async_computation.5 | async-start | bytes 1966080 | tf_op jit(solution)/shard_map/all_gather | solution.py:69
  116.0 8.0 %collective-permute-start.1 = (bf16[192,2880]{1,0:T(8,128)(2,1)}, bf16[192,2880]{1,0:T(8,128)(2,1)}, u32[]{:S(2)}, u32[]{:S(2)}) collective-permute-start(bf16[192,2880]{1,0:T(8,128)(2,1)} %bitcast.89), channel_id=1, source_target_pairs={{0,1},{1,0},{2,3},{3,2},{4,5},{5,4},{6,7},{7,6},{8,9},{9,8},{10,11... | collective-permute-start | bytes 3317768 | tf_op jit(solution)/shard_map/ppermute | solution.py:41
  118.0 10.5 %collective-permute-start = (bf16[192,2880]{1,0:T(8,128)(2,1)}, bf16[192,2880]{1,0:T(8,128)(2,1)}, u32[]{:S(2)}, u32[]{:S(2)}) collective-permute-start(bf16[192,2880]{1,0:T(8,128)(2,1)} %bitcast.92), channel_id=1, source_target_pairs={{0,1},{1,0},{2,3},{3,2},{4,5},{5,4},{6,7},{7,6},{8,9},{9,8},{10,11... | collective-permute-start | bytes 3317768 | tf_op jit(solution)/shard_map/ppermute | solution.py:41
  124.0 4.4 %copy-start.3 = (bf16[8,64,2880]{2,1,0:T(8,128)(2,1)S(1)}, bf16[8,64,2880]{2,1,0:T(8,128)(2,1)}, u32[]{:S(2)}) copy-start(bf16[8,64,2880]{2,1,0:T(8,128)(2,1)} %all-gather.8.cloned.1.call-done) | copy-start | bytes 8847364
  124.0 4.5 %copy-start.6 = (bf16[1,192,2880]{2,1,0:T(8,128)(2,1)S(1)}, bf16[1,192,2880]{2,1,0:T(8,128)(2,1)}, u32[]{:S(2)}) copy-start(bf16[1,192,2880]{2,1,0:T(8,128)(2,1)} %param.10) | copy-start | bytes 3317764
  128.4 4.0 %copy-start = (bf16[4,1,192,720]{3,2,0,1:T(8,128)(2,1)S(1)}, bf16[4,1,192,720]{3,2,0,1:T(8,128)(2,1)}, u32[]{:S(2)}) copy-start(bf16[4,1,192,720]{3,2,0,1:T(8,128)(2,1)} %get-tuple-element.6) | copy-start | bytes 3317764
  132.7 18.3 %copy-start.5 = (bf16[1,192,2880]{2,1,0:T(8,128)(2,1)S(1)}, bf16[1,192,2880]{2,1,0:T(8,128)(2,1)}, u32[]{:S(2)}) copy-start(bf16[1,192,2880]{2,1,0:T(8,128)(2,1)} %param.9) | copy-start | bytes 3317764
  151.0 2.8 %copy-start.4 = (bf16[4,64,2880]{2,1,0:T(8,128)(2,1)S(1)}, bf16[4,64,2880]{2,1,0:T(8,128)(2,1)}, u32[]{:S(2)}) copy-start(bf16[4,64,2880]{2,1,0:T(8,128)(2,1)} %all-gather.12.cloned.1.call-done) | copy-start | bytes 4423684
  151.0 2.8 %copy-start.7 = (bf16[1,192,2880]{2,1,0:T(8,128)(2,1)S(1)}, bf16[1,192,2880]{2,1,0:T(8,128)(2,1)}, u32[]{:S(2)}) copy-start(bf16[1,192,2880]{2,1,0:T(8,128)(2,1)} %param.10) | copy-start | bytes 3317764
  172.4 39.4 %all-to-all-start.3 = ((bf16[4,1,64,720]{3,0,1,2:T(4,128)(2,1)}), bf16[4,1,64,720]{3,0,1,2:T(4,128)(2,1)S(1)}, u32[]{:S(2)}, u32[]{:S(2)}) async-start(bf16[4,1,64,720]{3,0,1,2:T(4,128)(2,1)} %copy.68), calls=%async_computation.3 | async-start | bytes 786432 | tf_op jit(solution)/shard_map/all_to_all | solution.py:74
  191.4 27.3 %copy-start.2 = (s32[128,4]{0,1:T(4,128)S(1)}, s32[128,4]{0,1:T(4,128)}, u32[]{:S(2)}) copy-start(s32[128,4]{0,1:T(4,128)} %param.8) | copy-start | bytes 6148
  211.8 46.3 %all-to-all-start.1 = ((bf16[4,2,64,720]{3,1,0,2:T(2,128)(2,1)}), bf16[4,2,64,720]{3,1,0,2:T(2,128)(2,1)S(1)}, u32[]{:S(2)}, u32[]{:S(2)}) async-start(bf16[4,2,64,720]{3,1,0,2:T(2,128)(2,1)} %copy.62), calls=%async_computation.1 | async-start | bytes 1572864 | tf_op jit(solution)/shard_map/all_to_all | solution.py:74
Sparse Core Ops, SparseCore 0:
  76.6 38.3 all-gather.7
  117.1 33.8 all-gather.11
  153.1 34.3 all-gather.9

commit v6 on v5

--- a/solution.py
+++ b/solution.py
@@ -4,9 +4,19 @@
 from jax.sharding import Mesh
 from jax.sharding import PartitionSpec as P
 
-GROUP = "grp"
+GROUP = ("gx", "gz")
 CORE = "core"
 REP = "rep"
+
+
+def plane_all_to_all(value, axis):
+    n_x = lax.axis_size(GROUP[0])
+    n_z = lax.axis_size(GROUP[1])
+    shape = value.shape
+    split = value.reshape(*shape[:axis], n_x, n_z, *shape[axis + 1:])
+    split = lax.all_to_all(split, GROUP[1], axis + 1, axis + 1, tiled=True)
+    split = lax.all_to_all(split, GROUP[0], axis, axis, tiled=True)
+    return split.reshape(shape)
 
 
 def on_device(tokens, expert_ids, gate_levels, w_gate, w_up, w_down):
@@ -14,7 +24,7 @@
     model_width = tokens.shape[1]
     top_count = expert_ids.shape[1]
     n_rep = lax.axis_size(REP)
-    expert_count = lax.axis_size(GROUP)
+    expert_count = lax.axis_size(GROUP[0]) * lax.axis_size(GROUP[1])
     capacity = min(
         tok_rows, max(4, (tok_rows * top_count * 3 // (2 * expert_count) + 3) // 4 * 4)
     )
@@ -59,7 +69,7 @@
     within = slot_index % part
     for first, size in spans:
         sending = outgoing[first:first + size].reshape(size, expert_count, model_width)
-        arrived = lax.all_to_all(sending, GROUP, 1, 1, tiled=True)
+        arrived = plane_all_to_all(sending, 1)
         rows = lax.all_gather(arrived, REP, axis=0, tiled=False).reshape(-1, model_width)
         gate_proj = lax.dot_general(rows, gate_units, contract, preferred_element_type=jnp.float32)
         up_proj = lax.dot_general(rows, up_units, contract, preferred_element_type=jnp.float32)
@@ -71,7 +81,7 @@
             "rnk,rkc->nc", hidden_all, down_units, preferred_element_type=jnp.float32
         )
         expert_out = projected.astype(jnp.bfloat16).reshape(n_rep, size, expert_count, col_count)
-        back = lax.all_to_all(expert_out, GROUP, 2, 2, tiled=True)
+        back = plane_all_to_all(expert_out, 2)
         chunks.append(back.reshape(-1, col_count))
         here = offset + (plane * size + within - first) * expert_count + flat_ids
         in_span = (within >= first) & (within < first + size)
@@ -91,8 +101,10 @@
 def solution(mesh):
     n_rep = mesh.shape[REP]
     n_exp = mesh.shape["exp"]
-    split = Mesh(mesh.devices.reshape(n_rep, n_exp // 2, 2), (REP, GROUP, CORE))
-    shards = (GROUP, CORE)
+    n_z = len({device.coords[2] for device in mesh.devices.reshape(-1)})
+    grid = mesh.devices.reshape(n_rep, n_exp // (2 * n_z), n_z, 2)
+    split = Mesh(grid, (REP, *GROUP, CORE))
+    shards = (*GROUP, CORE)
     return jax.shard_map(
         on_device,
         mesh=split,

time: 270 us -> 297 us (1.10)
  blocking collectives: 74 us -> 111 us
  waiting for transfers between devices: 100 us -> 87 us
  starting transfers between devices: 36 us -> 41.2 us
  other arithmetic: 8.48 us -> 5.47 us
    all_to_all x1 -> x3, blocking collectives: 59.9 us -> 96.5 us  [the longest x2 84.7 us: plane_all_to_all(): split = lax.all_to_all(split, GROUP[1], axis + 1, axis + 1, tiled=True)]
    all_to_all x3 -> x5, waiting for transfers between devices: 81.9 us -> 63.9 us  [the longest x2 49.4 us: plane_all_to_all(): split = lax.all_to_all(split, GROUP[1], axis + 1, axis + 1, tiled=True)]
    all_to_all x3 -> x5, starting transfers between devices: 29.4 us -> 34.7 us  [the longest x2 18.9 us: plane_all_to_all(): split = lax.all_to_all(split, GROUP[1], axis + 1, axis + 1, tiled=True)]
    reshape x5 -> x0, local copies, waits for them, and re-layouts: 4.15 us -> none  [the longest x2 2.76 us: on_device(): projected.astype(jnp.bfloat16).reshape(n_rep, size, expert_count, col_count)]
    unnamed x1 -> x0, other arithmetic: 2.98 us -> none
  transfers between devices with their start and end apart: 9 -> 11, of which waited for: 4 -> 7; matrix products, arithmetic and copies ran while one was open for 12% -> 9% of each run, Pallas kernels for 0% -> 0%
where the time goes in v6:
time: 297 us; the launch traced here: 294 us
  blocking collectives  111 us (37%)
  waiting for transfers between devices  87 us (29%)
  starting transfers between devices  41.2 us (14%)
  local copies, waits for them, and re-layouts  19 us (6%)
  matrix products  17.2 us (6%)
  between operations  13.5 us (5%)
  other arithmetic  5.47 us (2%)
    all_to_all x2, blocking collectives, plane_all_to_all(): split = lax.all_to_all(split, GROUP[1], axis + 1, axis + 1, tiled=True)  84.7 us
    all_to_all x2, waiting for transfers between devices, plane_all_to_all(): split = lax.all_to_all(split, GROUP[1], axis + 1, axis + 1, tiled=True)  49.4 us
    all_gather x2, waiting for transfers between devices, on_device(): lax.all_gather(arrived, REP, axis=0, tiled=False).reshape(-1, model_width)  20.2 us
    all_to_all x2, starting transfers between devices, plane_all_to_all(): split = lax.all_to_all(split, GROUP[1], axis + 1, axis + 1, tiled=True)  18.9 us
    all_to_all x3, starting transfers between devices, plane_all_to_all(): split = lax.all_to_all(split, GROUP[0], axis, axis, tiled=True)  15.8 us
    all_to_all x3, waiting for transfers between devices, plane_all_to_all(): split = lax.all_to_all(split, GROUP[0], axis, axis, tiled=True)  14.5 us
    all_gather x1, blocking collectives, on_device(): hidden_all = lax.all_gather(hidden, REP, axis=0, tiled=False)  14 us
    all_to_all x1, blocking collectives, plane_all_to_all(): split = lax.all_to_all(split, GROUP[0], axis, axis, tiled=True)  11.8 us
  transfers between devices with their start and end apart: 11, of which 7 were waited for; matrix products, arithmetic and copies ran while one was open for 9% of the time, Pallas kernels for 0%

profile of v6, /device:TPU:6, one launch (start us, length us, event | category | flops | bytes accessed | tf_op | source)
XLA Modules:
  0.0 293.9 jit_solution(11005748004032388544)
XLA Ops:
  9.4 2.4 scatter_custom_fusion
  15.0 54.9 %all_to_all.40 = bf16[2,4,16,2880]{3,1,0,2:T(4,128)(2,1)S(1)} all-to-all(bf16[2,4,16,2880]{3,1,0,2:T(4,128)(2,1)S(1)} %copy.57), channel_id=1, replica_groups=mesh['rep'=4,'gx'=4,'gz'=16,'core'=2] {'gz'}, dimensions={2} | all-to-all | bytes 1474560 | tf_op jit(solution)/shard_map/all_to_all | solution.py:17
  70.0 11.8 %all_to_all.41 = bf16[2,4,16,2880]{3,2,0,1:T(8,128)(2,1)S(1)} all-to-all(bf16[2,4,16,2880]{3,2,0,1:T(8,128)(2,1)S(1)} %copy.58), channel_id=1, replica_groups=mesh['rep'=4,'gx'=4,'gz'=16,'core'=2] {'gx'}, dimensions={1} | all-to-all | bytes 1474560 | tf_op jit(solution)/shard_map/all_to_all | solution.py:18
  83.0 29.7 %all_to_all.42 = bf16[1,4,16,2880]{3,1,0,2:T(4,128)(2,1)S(1)} all-to-all(bf16[1,4,16,2880]{3,1,0,2:T(4,128)(2,1)S(1)} %copy.68), channel_id=1, replica_groups=mesh['rep'=4,'gx'=4,'gz'=16,'core'=2] {'gz'}, dimensions={2} | all-to-all | bytes 737280 | tf_op jit(solution)/shard_map/all_to_all | solution.py:17
  113.6 5.5 %all-to-all-start.5 = ((bf16[1,4,16,2880]{3,2,0,1:T(8,128)(2,1)}), bf16[1,4,16,2880]{3,2,0,1:T(8,128)(2,1)S(1)}, u32[]{:S(2)}, u32[]{:S(2)}) async-start(bf16[1,4,16,2880]{3,2,0,1:T(8,128)(2,1)} %copy.69), calls=%async_computation.5 | async-start | bytes 753664 | tf_op jit(solution)/shard_map/all_to_all | solution.py:18
  121.0 3.3 %all-to-all-done.5 = bf16[1,4,16,2880]{3,2,0,1:T(8,128)(2,1)S(1)} async-done(((bf16[1,4,16,2880]{3,2,0,1:T(8,128)(2,1)}), bf16[1,4,16,2880]{3,2,0,1:T(8,128)(2,1)S(1)}, u32[]{:S(2)}, u32[]{:S(2)}) %all-to-all-start.5) | async-done | bytes 368672 | tf_op jit(solution)/shard_map/all_to_all | solution.py:18
  127.1 2.6 collective-permute-start
  133.1 4.4 %fusion.1 = f32[512,384]{1,0:T(8,128)S(1)} fusion(bf16[512,2880]{1,0:T(8,128)(2,1)} %bitcast.82, bf16[192,2880]{1,0:T(8,128)(2,1)} %collective-permute-done.1, bf16[192,2880]{1,0:T(8,128)(2,1)} %bitcast.88), kind=kOutput, calls=%fused_computation.13 | convolution fusion | flops 1136885760 | bytes 5947392 | tf_op jit(solution)/shard_map/dot_general | solution.py:74
  137.6 3.9 %fusion.7 = bf16[512,384]{1,0:T(8,128)(2,1)} fusion(f32[512,384]{1,0:T(8,128)S(1)} %fusion.1, bf16[512,2880]{1,0:T(8,128)(2,1)S(1)} %bitcast.83, bf16[192,2880]{1,0:T(8,128)(2,1)} %collective-permute-done, bf16[192,2880]{1,0:T(8,128)(2,1)S(1)} %bitcast.91), kind=kOutput, calls=%fused_computation.20 | convolution fusion | flops 1138458624 | bytes 6340608 | tf_op jit(solution)/shard_map/dot_general | solution.py:75
  141.9 20.2 %all-gather.8.cloned.1.call-done = bf16[4,1,64,2880]{3,2,1,0:T(8,128)(2,1)} async-done(((bf16[1,1,64,2880]{3,2,1,0:T(8,128)(2,1)}), bf16[4,1,64,2880]{3,2,1,0:T(8,128)(2,1)}) %all-gather.8.cloned.1.call-update) | async-done | bytes 1474576 | tf_op jit(solution)/shard_map/all_gather | solution.py:73
  162.1 2.8 fusion
  164.9 2.2 fusion.16
  167.2 14.0 %all-gather.1 = bf16[1024,384]{1,0:T(8,128)(2,1)S(1)} all-gather(bf16[256,384]{1,0:T(8,128)(2,1)S(1)} %fusion.16), channel_id=3, replica_groups=mesh['rep'=4,'gx'=4,'gz'=16,'core'=2] {'rep'}, dimensions={0}, use_global_device_ids=true | all-gather | bytes 983040 | tf_op jit(solution)/shard_map/all_gather | solution.py:79
  183.4 12.3 %all-to-all-start.6 = ((bf16[4,1,4,16,720]{4,2,0,1,3:T(4,128)(2,1)}), bf16[4,1,4,16,720]{4,2,0,1,3:T(4,128)(2,1)S(1)}, u32[]{:S(2)}, u32[]{:S(2)}) async-start(bf16[4,1,4,16,720]{4,2,0,1,3:T(4,128)(2,1)} %copy.72), calls=%async_computation.6 | async-start | bytes 786432 | tf_op jit(solution)/shard_map/all_to_all | solution.py:17
  195.7 2.9 all-gather.10.cloned.1.call-done
  198.6 2.8 bitcast_convert_fusion
  202.9 13.1 %all-to-all-done.6 = bf16[4,1,4,16,720]{4,2,0,1,3:T(4,128)(2,1)S(1)} async-done(((bf16[4,1,4,16,720]{4,2,0,1,3:T(4,128)(2,1)}), bf16[4,1,4,16,720]{4,2,0,1,3:T(4,128)(2,1)S(1)}, u32[]{:S(2)}, u32[]{:S(2)}) %all-to-all-start.6) | async-done | bytes 368672 | tf_op jit(solution)/shard_map/all_to_all | solution.py:17
  216.1 6.6 %all-to-all-start.2 = ((bf16[4,2,4,16,720]{4,2,1,0,3:T(4,128)(2,1)}), bf16[4,2,4,16,720]{4,2,1,0,3:T(4,128)(2,1)S(1)}, u32[]{:S(2)}, u32[]{:S(2)}) async-start(bf16[4,2,4,16,720]{4,2,1,0,3:T(4,128)(2,1)} %copy.65), calls=%async_computation.2 | async-start | bytes 1572864 | tf_op jit(solution)/shard_map/all_to_all | solution.py:17
  223.5 36.3 %all-to-all-done.2 = bf16[4,2,4,16,720]{4,2,1,0,3:T(4,128)(2,1)S(1)} async-done(((bf16[4,2,4,16,720]{4,2,1,0,3:T(4,128)(2,1)}), bf16[4,2,4,16,720]{4,2,1,0,3:T(4,128)(2,1)S(1)}, u32[]{:S(2)}, u32[]{:S(2)}) %all-to-all-start.2) | async-done | bytes 737312 | tf_op jit(solution)/shard_map/all_to_all | solution.py:17
  259.8 4.8 %all-to-all-start.7 = ((bf16[4,1,4,16,720]{4,3,0,1,2:T(8,128)(2,1)}), bf16[4,1,4,16,720]{4,3,0,1,2:T(8,128)(2,1)S(1)}, u32[]{:S(2)}, u32[]{:S(2)}) async-start(bf16[4,1,4,16,720]{4,3,0,1,2:T(8,128)(2,1)} %copy.73), calls=%async_computation.7 | async-start | bytes 786432 | tf_op jit(solution)/shard_map/all_to_all | solution.py:18
  265.9 4.0 %all-to-all-done.7 = bf16[4,1,4,16,720]{4,3,0,1,2:T(8,128)(2,1)S(1)} async-done(((bf16[4,1,4,16,720]{4,3,0,1,2:T(8,128)(2,1)}), bf16[4,1,4,16,720]{4,3,0,1,2:T(8,128)(2,1)S(1)}, u32[]{:S(2)}, u32[]{:S(2)}) %all-to-all-start.7) | async-done | bytes 368672 | tf_op jit(solution)/shard_map/all_to_all | solution.py:18
  269.9 5.5 %all-to-all-start.3 = ((bf16[4,2,4,16,720]{4,3,1,0,2:T(8,128)(2,1)}), bf16[4,2,4,16,720]{4,3,1,0,2:T(8,128)(2,1)S(1)}, u32[]{:S(2)}, u32[]{:S(2)}) async-start(bf16[4,2,4,16,720]{4,3,1,0,2:T(8,128)(2,1)} %copy.66), calls=%async_computation.3 | async-start | bytes 1572864 | tf_op jit(solution)/shard_map/all_to_all | solution.py:18
  275.6 7.2 %all-to-all-done.3 = bf16[4,2,4,16,720]{4,3,1,0,2:T(8,128)(2,1)S(1)} async-done(((bf16[4,2,4,16,720]{4,3,1,0,2:T(8,128)(2,1)}), bf16[4,2,4,16,720]{4,3,1,0,2:T(8,128)(2,1)S(1)}, u32[]{:S(2)}, u32[]{:S(2)}) %all-to-all-start.3) | async-done | bytes 737312 | tf_op jit(solution)/shard_map/all_to_all | solution.py:18
  283.1 2.0 gather_fusion.1
  (78 shorter events, 25.0 us)
Async XLA Ops:
  6.5 126.6 %all-gather.6.cloned.1.call-start = ((), (), s32[]{:S(2)}) async-start(), calls=%async_computation.8 | async-start | bytes 3768320 | tf_op jit(solution)/shard_map/all_gather | solution.py:73
  82.9 36.2 %copy-start.2 = (bf16[1,1536,360]{1,2,0:T(8,128)(2,1)S(1)}, bf16[1,1536,360]{1,2,0:T(8,128)(2,1)}, u32[]{:S(2)}) copy-start(bf16[1,1536,360]{1,2,0:T(8,128)(2,1)} %param.11) | copy-start | bytes 3317764
  113.6 10.7 %all-to-all-start.5 = ((bf16[1,4,16,2880]{3,2,0,1:T(8,128)(2,1)}), bf16[1,4,16,2880]{3,2,0,1:T(8,128)(2,1)S(1)}, u32[]{:S(2)}, u32[]{:S(2)}) async-start(bf16[1,4,16,2880]{3,2,0,1:T(8,128)(2,1)} %copy.69), calls=%async_computation.5 | async-start | bytes 753664 | tf_op jit(solution)/shard_map/all_to_all | solution.py:18
  119.1 43.0 %all-gather.8.cloned.1.call-start = ((), (), s32[]{:S(2)}) async-start(), calls=%async_computation.9 | async-start | bytes 1884160 | tf_op jit(solution)/shard_map/all_gather | solution.py:73
  119.1 11.3 %collective-permute-start.2 = (bf16[1536,360]{0,1:T(8,128)(2,1)S(1)}, bf16[1536,360]{0,1:T(8,128)(2,1)S(1)}, u32[]{:S(2)}, u32[]{:S(2)}) collective-permute-start(bf16[1536,360]{0,1:T(8,128)(2,1)S(1)} %bitcast.74), channel_id=1, source_target_pairs={{0,1},{1,0},{2,3},{3,2},{4,5},{5,4},{6,7},{7,6},{8,9},{9,8},{10,11... | collective-permute-start | bytes 3317768 | tf_op jit(solution)/shard_map/ppermute | solution.py:51
  124.3 0.8 copy-start.1
  125.1 73.5 %all-gather.10.cloned.1.call-start = ((), (), s32[]{:S(2)}) async-start(), calls=%async_computation.10 | async-start | bytes 1966080 | tf_op jit(solution)/shard_map/all_gather | solution.py:79
  125.1 7.9 %collective-permute-start.1 = (bf16[192,2880]{1,0:T(8,128)(2,1)}, bf16[192,2880]{1,0:T(8,128)(2,1)}, u32[]{:S(2)}, u32[]{:S(2)}) collective-permute-start(bf16[192,2880]{1,0:T(8,128)(2,1)} %bitcast.87), channel_id=1, source_target_pairs={{0,1},{1,0},{2,3},{3,2},{4,5},{5,4},{6,7},{7,6},{8,9},{9,8},{10,11... | collective-permute-start | bytes 3317768 | tf_op jit(solution)/shard_map/ppermute | solution.py:51
  127.1 10.5 %collective-permute-start = (bf16[192,2880]{1,0:T(8,128)(2,1)}, bf16[192,2880]{1,0:T(8,128)(2,1)}, u32[]{:S(2)}, u32[]{:S(2)}) collective-permute-start(bf16[192,2880]{1,0:T(8,128)(2,1)} %bitcast.90), channel_id=1, source_target_pairs={{0,1},{1,0},{2,3},{3,2},{4,5},{5,4},{6,7},{7,6},{8,9},{9,8},{10,11... | collective-permute-start | bytes 3317768 | tf_op jit(solution)/shard_map/ppermute | solution.py:51
  133.1 4.4 %copy-start.4 = (bf16[4,2,64,2880]{3,2,1,0:T(8,128)(2,1)S(1)}, bf16[4,2,64,2880]{3,2,1,0:T(8,128)(2,1)}, u32[]{:S(2)}) copy-start(bf16[4,2,64,2880]{3,2,1,0:T(8,128)(2,1)} %all-gather.6.cloned.1.call-done) | copy-start | bytes 8847364
  133.1 4.5 %copy-start.7 = (bf16[1,192,2880]{2,1,0:T(8,128)(2,1)S(1)}, bf16[1,192,2880]{2,1,0:T(8,128)(2,1)}, u32[]{:S(2)}) copy-start(bf16[1,192,2880]{2,1,0:T(8,128)(2,1)} %param.10) | copy-start | bytes 3317764
  137.5 4.0 %copy-start = (bf16[4,1,192,720]{3,2,0,1:T(8,128)(2,1)S(1)}, bf16[4,1,192,720]{3,2,0,1:T(8,128)(2,1)}, u32[]{:S(2)}) copy-start(bf16[4,1,192,720]{3,2,0,1:T(8,128)(2,1)} %get-tuple-element.6) | copy-start | bytes 3317764
  141.7 20.4 %copy-start.6 = (bf16[1,192,2880]{2,1,0:T(8,128)(2,1)S(1)}, bf16[1,192,2880]{2,1,0:T(8,128)(2,1)}, u32[]{:S(2)}) copy-start(bf16[1,192,2880]{2,1,0:T(8,128)(2,1)} %param.9) | copy-start | bytes 3317764
  162.1 2.8 copy-start.5
  162.1 2.8 copy-start.8
  183.4 32.7 %all-to-all-start.6 = ((bf16[4,1,4,16,720]{4,2,0,1,3:T(4,128)(2,1)}), bf16[4,1,4,16,720]{4,2,0,1,3:T(4,128)(2,1)S(1)}, u32[]{:S(2)}, u32[]{:S(2)}) async-start(bf16[4,1,4,16,720]{4,2,0,1,3:T(4,128)(2,1)} %copy.72), calls=%async_computation.6 | async-start | bytes 786432 | tf_op jit(solution)/shard_map/all_to_all | solution.py:17
  216.1 43.7 %all-to-all-start.2 = ((bf16[4,2,4,16,720]{4,2,1,0,3:T(4,128)(2,1)}), bf16[4,2,4,16,720]{4,2,1,0,3:T(4,128)(2,1)S(1)}, u32[]{:S(2)}, u32[]{:S(2)}) async-start(bf16[4,2,4,16,720]{4,2,1,0,3:T(4,128)(2,1)} %copy.65), calls=%async_computation.2 | async-start | bytes 1572864 | tf_op jit(solution)/shard_map/all_to_all | solution.py:17
  259.8 10.1 %all-to-all-start.7 = ((bf16[4,1,4,16,720]{4,3,0,1,2:T(8,128)(2,1)}), bf16[4,1,4,16,720]{4,3,0,1,2:T(8,128)(2,1)S(1)}, u32[]{:S(2)}, u32[]{:S(2)}) async-start(bf16[4,1,4,16,720]{4,3,0,1,2:T(8,128)(2,1)} %copy.73), calls=%async_computation.7 | async-start | bytes 786432 | tf_op jit(solution)/shard_map/all_to_all | solution.py:18
  264.6 10.9 %copy-start.3 = (s32[128,4]{0,1:T(4,128)S(1)}, s32[128,4]{0,1:T(4,128)}, u32[]{:S(2)}) copy-start(s32[128,4]{0,1:T(4,128)} %param.8) | copy-start | bytes 6148
  269.9 13.0 %all-to-all-start.3 = ((bf16[4,2,4,16,720]{4,3,1,0,2:T(8,128)(2,1)}), bf16[4,2,4,16,720]{4,3,1,0,2:T(8,128)(2,1)S(1)}, u32[]{:S(2)}, u32[]{:S(2)}) async-start(bf16[4,2,4,16,720]{4,3,1,0,2:T(8,128)(2,1)} %copy.66), calls=%async_computation.3 | async-start | bytes 1572864 | tf_op jit(solution)/shard_map/all_to_all | solution.py:18
Sparse Core Ops, SparseCore 0:
  83.0 43.1 all-gather.5
  128.2 33.8 all-gather.7
  164.2 34.3 all-gather.9

commit v7 on v5

--- a/solution.py
+++ b/solution.py
@@ -66,7 +66,8 @@
         hidden = ((up_proj + 1.0) * gate_proj * jax.nn.sigmoid(1.702 * gate_proj)).astype(
             jnp.bfloat16
         )
-        hidden_all = lax.all_gather(hidden, REP, axis=0, tiled=False)
+        copies = jnp.broadcast_to(hidden[None], (n_rep, *hidden.shape))
+        hidden_all = lax.all_to_all(copies, REP, 0, 0, tiled=True)
         projected = jnp.einsum(
             "rnk,rkc->nc", hidden_all, down_units, preferred_element_type=jnp.float32
         )

time: 270 us -> 296 us (1.096)
  waiting for transfers between devices: 100 us -> 176 us
  blocking collectives: 74 us -> 0 us
  starting transfers between devices: 36 us -> 57.2 us
  local copies, waits for them, and re-layouts: 19.9 us -> 23.9 us
    all_to_all x1 -> x0, blocking collectives: 59.9 us -> none  [on_device(): arrived = lax.all_to_all(sending, GROUP, 1, 1, tiled=True)]
    all_to_all x1 -> x2, waiting for transfers between devices: 24.1 us -> 63.8 us  [on_device(): arrived = lax.all_to_all(sending, GROUP, 1, 1, tiled=True)]
    all_to_all x1 -> x2, starting transfers between devices: 6.64 us -> 25.4 us  [on_device(): arrived = lax.all_to_all(sending, GROUP, 1, 1, tiled=True)]
    all_gather x2, waiting for transfers between devices: 18.1 us -> 34.8 us  [on_device(): lax.all_gather(arrived, REP, axis=0, tiled=False).reshape(-1, model_width)]
    all_to_all x0 -> x2, waiting for transfers between devices: none -> 14.9 us  [on_device(): hidden_all = lax.all_to_all(copies, REP, 0, 0, tiled=True)]
    all_gather x1 -> x0, blocking collectives: 14 us -> none  [on_device(): hidden_all = lax.all_gather(hidden, REP, axis=0, tiled=False)]
    all_to_all x0 -> x2, starting transfers between devices: none -> 8.79 us  [on_device(): hidden_all = lax.all_to_all(copies, REP, 0, 0, tiled=True)]
    all_to_all x2, starting transfers between devices: 22.8 us -> 16.5 us  [on_device(): back = lax.all_to_all(expert_out, GROUP, 2, 2, tiled=True)]
  transfers between devices with their start and end apart: 9 -> 11, of which waited for: 4 -> 6; matrix products, arithmetic and copies ran while one was open for 12% -> 10% of each run, Pallas kernels for 0% -> 0%
where the time goes in v7:
time: 296 us; the launch traced here: 295 us
  waiting for transfers between devices  176 us (59%)
  starting transfers between devices  57.2 us (19%)
  local copies, waits for them, and re-layouts  23.9 us (8%)
  matrix products  17.3 us (6%)
  between operations  13.9 us (5%)
  other arithmetic  7.42 us (3%)
    all_to_all x2, waiting for transfers between devices, on_device(): arrived = lax.all_to_all(sending, GROUP, 1, 1, tiled=True)  63.8 us
    all_to_all x2, waiting for transfers between devices, on_device(): back = lax.all_to_all(expert_out, GROUP, 2, 2, tiled=True)  62.1 us
    all_gather x2, waiting for transfers between devices, on_device(): lax.all_gather(arrived, REP, axis=0, tiled=False).reshape(-1, model_width)  34.8 us
    all_to_all x2, starting transfers between devices, on_device(): arrived = lax.all_to_all(sending, GROUP, 1, 1, tiled=True)  25.4 us
    all_to_all x2, starting transfers between devices, on_device(): back = lax.all_to_all(expert_out, GROUP, 2, 2, tiled=True)  16.5 us
    all_to_all x2, waiting for transfers between devices, on_device(): hidden_all = lax.all_to_all(copies, REP, 0, 0, tiled=True)  14.9 us
    all_to_all x2, starting transfers between devices, on_device(): hidden_all = lax.all_to_all(copies, REP, 0, 0, tiled=True)  8.79 us
    dot_general x2, matrix products, on_device(): lax.dot_general(rows, gate_units, contract, preferred_element_type=jnp.fl...  7.49 us
  transfers between devices with their start and end apart: 11, of which 6 were waited for; matrix products, arithmetic and copies ran while one was open for 10% of the time, Pallas kernels for 0%

profile of v7, /device:TPU:6, one launch (start us, length us, event | category | flops | bytes accessed | tf_op | source)
XLA Modules:
  0.0 295.4 jit_solution(3991755945413502305)
XLA Ops:
  9.4 2.4 scatter_custom_fusion
  15.8 3.0 %reduce.2 = bf16[64,2880]{1,0:T(8,128)(2,1)S(1)} reduce(bf16[64,1,2880]{2,1,0:T(2,128)(2,1)S(1)} %bitcast.67, bf16[]{:T(256)} %broadcast.308), dimensions={1}, to_apply=%bitcast.61.reduce_sub_computation | reduce | bytes 737282
  20.0 18.8 %all-to-all-start.3 = ((bf16[64,2,1440]{2,1,0:T(2,128)(2,1)}), bf16[64,2,1440]{2,1,0:T(2,128)(2,1)S(1)}, u32[]{:S(2)}, u32[]{:S(2)}) async-start(bf16[64,2,1440]{2,1,0:T(2,128)(2,1)} %reshape.292), calls=%async_computation.3 | async-start | bytes 786432 | tf_op jit(solution)/shard_map/all_to_all | solution.py:62
  40.5 24.6 %all-to-all-done.3 = bf16[64,2,1440]{2,1,0:T(2,128)(2,1)S(1)} async-done(((bf16[64,2,1440]{2,1,0:T(2,128)(2,1)}), bf16[64,2,1440]{2,1,0:T(2,128)(2,1)S(1)}, u32[]{:S(2)}, u32[]{:S(2)}) %all-to-all-start.3) | async-done | bytes 368672 | tf_op jit(solution)/shard_map/all_to_all | solution.py:62
  65.1 6.6 %all-to-all-start = ((bf16[2,64,2880]{2,0,1:T(2,128)(2,1)}), bf16[2,64,2880]{2,0,1:T(2,128)(2,1)S(1)}, u32[]{:S(2)}, u32[]{:S(2)}) async-start(bf16[2,64,2880]{2,0,1:T(2,128)(2,1)} %copy.55), calls=%async_computation | async-start | bytes 1507328 | tf_op jit(solution)/shard_map/all_to_all | solution.py:62
  73.2 39.2 %all-to-all-done = bf16[2,64,2880]{2,0,1:T(2,128)(2,1)S(1)} async-done(((bf16[2,64,2880]{2,0,1:T(2,128)(2,1)}), bf16[2,64,2880]{2,0,1:T(2,128)(2,1)S(1)}, u32[]{:S(2)}, u32[]{:S(2)}) %all-to-all-start) | async-done | bytes 737312 | tf_op jit(solution)/shard_map/all_to_all | solution.py:62
  113.4 1.9 collective-permute-start.1
  115.4 2.4 collective-permute-start
  117.8 2.1 collective-permute-start.2
  119.9 3.1 %fusion = f32[256,384]{1,0:T(8,128)S(1)} fusion(bf16[256,2880]{1,0:T(8,128)(2,1)} %bitcast.83, bf16[192,2880]{1,0:T(8,128)(2,1)S(1)} %collective-permute-done.1, bf16[192,2880]{1,0:T(8,128)(2,1)} %bitcast.6), kind=kOutput, calls=%fused_computation.12 | convolution fusion | flops 570654720 | bytes 4079616 | tf_op jit(solution)/shard_map/dot_general | solution.py:64
  123.1 2.6 fusion.16
  126.6 4.5 %all-to-all-start.4 = ((bf16[4,256,384]{2,1,0:T(8,128)(2,1)}), bf16[4,256,384]{2,1,0:T(8,128)(2,1)S(1)}, u32[]{:S(2)}, u32[]{:S(2)}) async-start(bf16[4,256,384]{2,1,0:T(8,128)(2,1)} %broadcast_in_dim.13), calls=%async_computation.4 | async-start | bytes 1572864 | tf_op jit(solution)/shard_map/all_to_all | solution.py:70
  131.1 34.8 %all-gather.5.cloned.1.call-done = bf16[8,64,2880]{2,1,0:T(8,128)(2,1)} async-done(((bf16[2,64,2880]{2,1,0:T(8,128)(2,1)}), bf16[8,64,2880]{2,1,0:T(8,128)(2,1)}) %all-gather.5.cloned.1.call-update) | async-done | bytes 2949136 | tf_op jit(solution)/shard_map/all_gather | solution.py:63
  165.9 4.4 %fusion.1 = f32[512,384]{1,0:T(8,128)S(1)} fusion(bf16[512,2880]{1,0:T(8,128)(2,1)} %bitcast.81, bf16[192,2880]{1,0:T(8,128)(2,1)} %copy-done.6, bf16[192,2880]{1,0:T(8,128)(2,1)} %bitcast.6), kind=kOutput, calls=%fused_computation.13 | convolution fusion | flops 1136885760 | bytes 5947392 | tf_op jit(solution)/shard_map/dot_general | solution.py:64
  170.3 3.4 %fusion.7 = bf16[512,384]{1,0:T(8,128)(2,1)S(1)} fusion(f32[512,384]{1,0:T(8,128)S(1)} %fusion.1, bf16[512,2880]{1,0:T(8,128)(2,1)S(1)} %bitcast.82, bf16[192,2880]{1,0:T(8,128)(2,1)} %collective-permute-done, bf16[192,2880]{1,0:T(8,128)(2,1)} %bitcast.5), kind=kOutput, calls=%fused_computation.20 | convolution fusion | flops 1138458624 | bytes 6340608 | tf_op jit(solution)/shard_map/dot_general | solution.py:65
  175.1 4.3 %all-to-all-start.1 = ((bf16[4,512,384]{2,1,0:T(8,128)(2,1)}), bf16[4,512,384]{2,1,0:T(8,128)(2,1)}, u32[]{:S(2)}, u32[]{:S(2)}) async-start(bf16[4,512,384]{2,1,0:T(8,128)(2,1)} %broadcast_in_dim.12), calls=%async_computation.1 | async-start | bytes 3145728 | tf_op jit(solution)/shard_map/all_to_all | solution.py:70
  185.5 14.9 %all-to-all-done.1 = bf16[4,512,384]{2,1,0:T(8,128)(2,1)} async-done(((bf16[4,512,384]{2,1,0:T(8,128)(2,1)}), bf16[4,512,384]{2,1,0:T(8,128)(2,1)}, u32[]{:S(2)}, u32[]{:S(2)}) %all-to-all-start.1) | async-done | bytes 1572896 | tf_op jit(solution)/shard_map/all_to_all | solution.py:70
  200.4 9.7 %all-to-all-start.5 = ((bf16[4,1,64,720]{3,0,1,2:T(4,128)(2,1)}), bf16[4,1,64,720]{3,0,1,2:T(4,128)(2,1)S(1)}, u32[]{:S(2)}, u32[]{:S(2)}) async-start(bf16[4,1,64,720]{3,0,1,2:T(4,128)(2,1)} %copy.68), calls=%async_computation.5 | async-start | bytes 786432 | tf_op jit(solution)/shard_map/all_to_all | solution.py:75
  210.0 2.8 bitcast_convert_fusion
  213.1 1.7 copy.62
  214.8 20.7 %all-to-all-done.5 = bf16[4,1,64,720]{3,0,1,2:T(4,128)(2,1)S(1)} async-done(((bf16[4,1,64,720]{3,0,1,2:T(4,128)(2,1)}), bf16[4,1,64,720]{3,0,1,2:T(4,128)(2,1)S(1)}, u32[]{:S(2)}, u32[]{:S(2)}) %all-to-all-start.5) | async-done | bytes 368672 | tf_op jit(solution)/shard_map/all_to_all | solution.py:75
  235.5 6.8 %all-to-all-start.2 = ((bf16[4,2,64,720]{3,1,0,2:T(2,128)(2,1)}), bf16[4,2,64,720]{3,1,0,2:T(2,128)(2,1)S(1)}, u32[]{:S(2)}, u32[]{:S(2)}) async-start(bf16[4,2,64,720]{3,1,0,2:T(2,128)(2,1)} %copy.62), calls=%async_computation.2 | async-start | bytes 1572864 | tf_op jit(solution)/shard_map/all_to_all | solution.py:75
  242.5 41.4 %all-to-all-done.2 = bf16[4,2,64,720]{3,1,0,2:T(2,128)(2,1)S(1)} async-done(((bf16[4,2,64,720]{3,1,0,2:T(2,128)(2,1)}), bf16[4,2,64,720]{3,1,0,2:T(2,128)(2,1)S(1)}, u32[]{:S(2)}, u32[]{:S(2)}) %all-to-all-start.2) | async-done | bytes 737312 | tf_op jit(solution)/shard_map/all_to_all | solution.py:75
  284.2 2.0 gather_fusion.1
  (72 shorter events, 23.4 us)
Async XLA Ops:
  20.0 45.1 %all-to-all-start.3 = ((bf16[64,2,1440]{2,1,0:T(2,128)(2,1)}), bf16[64,2,1440]{2,1,0:T(2,128)(2,1)S(1)}, u32[]{:S(2)}, u32[]{:S(2)}) async-start(bf16[64,2,1440]{2,1,0:T(2,128)(2,1)} %reshape.292), calls=%async_computation.3 | async-start | bytes 786432 | tf_op jit(solution)/shard_map/all_to_all | solution.py:62
  65.1 47.4 %all-to-all-start = ((bf16[2,64,2880]{2,0,1:T(2,128)(2,1)}), bf16[2,64,2880]{2,0,1:T(2,128)(2,1)S(1)}, u32[]{:S(2)}, u32[]{:S(2)}) async-start(bf16[2,64,2880]{2,0,1:T(2,128)(2,1)} %copy.55), calls=%async_computation | async-start | bytes 1507328 | tf_op jit(solution)/shard_map/all_to_all | solution.py:62
  71.7 48.2 %all-gather.7.cloned.1.call-start = ((), (), s32[]{:S(2)}) async-start(), calls=%async_computation.7 | async-start | bytes 1884160 | tf_op jit(solution)/shard_map/all_gather | solution.py:63
  73.1 44.6 %copy-start = (bf16[1,1536,360]{1,2,0:T(8,128)(2,1)S(1)}, bf16[1,1536,360]{1,2,0:T(8,128)(2,1)}, u32[]{:S(2)}) copy-start(bf16[1,1536,360]{1,2,0:T(8,128)(2,1)} %param.11) | copy-start | bytes 3317764
  73.2 92.7 %all-gather.5.cloned.1.call-start = ((), (), s32[]{:S(2)}) async-start(), calls=%async_computation.6 | async-start | bytes 3768320 | tf_op jit(solution)/shard_map/all_gather | solution.py:63
  113.4 6.5 %collective-permute-start.1 = (bf16[192,2880]{1,0:T(8,128)(2,1)}, bf16[192,2880]{1,0:T(8,128)(2,1)S(1)}, u32[]{:S(2)}, u32[]{:S(2)}) collective-permute-start(bf16[192,2880]{1,0:T(8,128)(2,1)} %bitcast.6), channel_id=1, source_target_pairs={{0,1},{1,0},{2,3},{3,2},{4,5},{5,4},{6,7},{7,6},{8,9},{9,8},{10,11... | collective-permute-start | bytes 3317768 | tf_op jit(solution)/shard_map/ppermute | solution.py:41
  115.4 7.7 %collective-permute-start = (bf16[192,2880]{1,0:T(8,128)(2,1)}, bf16[192,2880]{1,0:T(8,128)(2,1)}, u32[]{:S(2)}, u32[]{:S(2)}) collective-permute-start(bf16[192,2880]{1,0:T(8,128)(2,1)} %bitcast.5), channel_id=1, source_target_pairs={{0,1},{1,0},{2,3},{3,2},{4,5},{5,4},{6,7},{7,6},{8,9},{9,8},{10,11... | collective-permute-start | bytes 3317768 | tf_op jit(solution)/shard_map/ppermute | solution.py:41
  117.8 62.4 %collective-permute-start.2 = (bf16[1536,360]{0,1:T(8,128)(2,1)S(1)}, bf16[1536,360]{0,1:T(8,128)(2,1)S(1)}, u32[]{:S(2)}, u32[]{:S(2)}) collective-permute-start(bf16[1536,360]{0,1:T(8,128)(2,1)S(1)} %bitcast.74), channel_id=1, source_target_pairs={{0,1},{1,0},{2,3},{3,2},{4,5},{5,4},{6,7},{7,6},{8,9},{9,8},{10,11... | collective-permute-start | bytes 3317768 | tf_op jit(solution)/shard_map/ppermute | solution.py:41
  119.9 5.8 %copy-start.6 = (bf16[192,2880]{1,0:T(8,128)(2,1)}, bf16[192,2880]{1,0:T(8,128)(2,1)S(1)}, u32[]{:S(2)}) copy-start(bf16[192,2880]{1,0:T(8,128)(2,1)S(1)} %collective-permute-done.1) | copy-start | bytes 3317764
  119.9 3.1 %copy-start.5 = (bf16[4,64,2880]{2,1,0:T(8,128)(2,1)S(1)}, bf16[4,64,2880]{2,1,0:T(8,128)(2,1)}, u32[]{:S(2)}) copy-start(bf16[4,64,2880]{2,1,0:T(8,128)(2,1)} %all-gather.7.cloned.1.call-done) | copy-start | bytes 4423684
  126.6 47.1 %all-to-all-start.4 = ((bf16[4,256,384]{2,1,0:T(8,128)(2,1)}), bf16[4,256,384]{2,1,0:T(8,128)(2,1)S(1)}, u32[]{:S(2)}, u32[]{:S(2)}) async-start(bf16[4,256,384]{2,1,0:T(8,128)(2,1)} %broadcast_in_dim.13), calls=%async_computation.4 | async-start | bytes 1572864 | tf_op jit(solution)/shard_map/all_to_all | solution.py:70
  165.9 4.4 %copy-start.4 = (bf16[8,64,2880]{2,1,0:T(8,128)(2,1)S(1)}, bf16[8,64,2880]{2,1,0:T(8,128)(2,1)}, u32[]{:S(2)}) copy-start(bf16[8,64,2880]{2,1,0:T(8,128)(2,1)} %all-gather.5.cloned.1.call-done) | copy-start | bytes 8847364
  173.7 1.4 copy-start.1
  175.1 25.2 %all-to-all-start.1 = ((bf16[4,512,384]{2,1,0:T(8,128)(2,1)}), bf16[4,512,384]{2,1,0:T(8,128)(2,1)}, u32[]{:S(2)}, u32[]{:S(2)}) async-start(bf16[4,512,384]{2,1,0:T(8,128)(2,1)} %broadcast_in_dim.12), calls=%async_computation.1 | async-start | bytes 3145728 | tf_op jit(solution)/shard_map/all_to_all | solution.py:70
  182.1 1.1 copy-start.2
  200.4 35.2 %all-to-all-start.5 = ((bf16[4,1,64,720]{3,0,1,2:T(4,128)(2,1)}), bf16[4,1,64,720]{3,0,1,2:T(4,128)(2,1)S(1)}, u32[]{:S(2)}, u32[]{:S(2)}) async-start(bf16[4,1,64,720]{3,0,1,2:T(4,128)(2,1)} %copy.68), calls=%async_computation.5 | async-start | bytes 786432 | tf_op jit(solution)/shard_map/all_to_all | solution.py:75
  213.1 29.3 %copy-start.3 = (s32[128,4]{0,1:T(4,128)S(1)}, s32[128,4]{0,1:T(4,128)}, u32[]{:S(2)}) copy-start(s32[128,4]{0,1:T(4,128)} %param.8) | copy-start | bytes 6148
  235.5 48.4 %all-to-all-start.2 = ((bf16[4,2,64,720]{3,1,0,2:T(2,128)(2,1)}), bf16[4,2,64,720]{3,1,0,2:T(2,128)(2,1)S(1)}, u32[]{:S(2)}, u32[]{:S(2)}) async-start(bf16[4,2,64,720]{3,1,0,2:T(2,128)(2,1)} %copy.62), calls=%async_computation.2 | async-start | bytes 1572864 | tf_op jit(solution)/shard_map/all_to_all | solution.py:75
Sparse Core Ops, SparseCore 0:
  74.6 34.3 all-gather.6
  113.5 52.2 all-gather.4

commit v8 on v3

--- a/solution.py
+++ b/solution.py
@@ -7,6 +7,11 @@
 GROUP = "grp"
 CORE = "core"
 REP = "rep"
+
+
+def rep_gather(value, n_rep):
+    copies = jnp.broadcast_to(value[None], (n_rep, *value.shape))
+    return lax.all_to_all(copies, REP, 0, 0, tiled=True)
 
 
 def on_device(tokens, expert_ids, gate_levels, w_gate, w_up, w_down):
@@ -53,13 +58,13 @@
     chunks = []
     for chunk in range(part):
         arrived = lax.all_to_all(outgoing[chunk], GROUP, 0, 0, tiled=True)
-        rows = lax.all_gather(arrived, REP, axis=0, tiled=False).reshape(-1, model_width)
+        rows = rep_gather(arrived, n_rep).reshape(-1, model_width)
         gate_proj = lax.dot_general(rows, gate_units, contract, preferred_element_type=jnp.float32)
         up_proj = lax.dot_general(rows, up_units, contract, preferred_element_type=jnp.float32)
         hidden = ((up_proj + 1.0) * gate_proj * jax.nn.sigmoid(1.702 * gate_proj)).astype(
             jnp.bfloat16
         )
-        hidden_all = lax.all_gather(hidden, REP, axis=0, tiled=False)
+        hidden_all = rep_gather(hidden, n_rep)
         projected = jnp.einsum(
             "rnk,rkc->nc", hidden_all, down_units, preferred_element_type=jnp.float32
         )

time: 268 us -> 322 us (1.20)
  waiting for transfers between devices: 34.2 us -> 170 us
  blocking collectives: 121 us -> 0 us
  starting transfers between devices: 50.2 us -> 91.6 us
  between operations: 13.6 us -> 0.57 us
  local copies, waits for them, and re-layouts: 21.4 us -> 28.9 us
    all_to_all x2 -> x0, blocking collectives: 76.9 us -> none  [on_device(): arrived = lax.all_to_all(outgoing[chunk], GROUP, 0, 0, tiled=True)]
    all_to_all x1 -> x3, waiting for transfers between devices: 15.1 us -> 72.5 us  [on_device(): arrived = lax.all_to_all(outgoing[chunk], GROUP, 0, 0, tiled=True)]
    all_to_all x0 -> x6, waiting for transfers between devices: none -> 44.7 us  [rep_gather(): return lax.all_to_all(copies, REP, 0, 0, tiled=True)]
    all_gather x3 -> x0, blocking collectives: 43.7 us -> none  [on_device(): hidden_all = lax.all_gather(hidden, REP, axis=0, tiled=False)]
    all_to_all x3, waiting for transfers between devices: 19 us -> 52.4 us  [on_device(): chunks.append(lax.all_to_all(expert_out, GROUP, 1, 1, tiled=True))]
    all_to_all x1 -> x3, starting transfers between devices: 6.78 us -> 32.2 us  [on_device(): arrived = lax.all_to_all(outgoing[chunk], GROUP, 0, 0, tiled=True)]
    all_to_all x0 -> x6, starting transfers between devices: none -> 24.6 us  [rep_gather(): return lax.all_to_all(copies, REP, 0, 0, tiled=True)]
    all_to_all x3, starting transfers between devices: 36.9 us -> 28.6 us  [on_device(): chunks.append(lax.all_to_all(expert_out, GROUP, 1, 1, tiled=True))]
  transfers between devices with their start and end apart: 10 -> 15, of which waited for: 2 -> 12; matrix products, arithmetic and copies ran while one was open for 12% -> 12% of each run, Pallas kernels for 0% -> 0%
where the time goes in v8:
time: 322 us; the launch traced here: 321 us
  waiting for transfers between devices  170 us (53%)
  starting transfers between devices  91.6 us (28%)
  local copies, waits for them, and re-layouts  28.9 us (9%)
  matrix products  22.4 us (7%)
  other arithmetic  7.8 us (2%)
    all_to_all x3, waiting for transfers between devices, on_device(): arrived = lax.all_to_all(outgoing[chunk], GROUP, 0, 0, tiled=True)  72.5 us
    all_to_all x3, waiting for transfers between devices, on_device(): chunks.append(lax.all_to_all(expert_out, GROUP, 1, 1, tiled=True))  52.4 us
    all_to_all x6, waiting for transfers between devices, rep_gather(): return lax.all_to_all(copies, REP, 0, 0, tiled=True)  44.7 us
    all_to_all x3, starting transfers between devices, on_device(): arrived = lax.all_to_all(outgoing[chunk], GROUP, 0, 0, tiled=True)  32.2 us
    all_to_all x3, starting transfers between devices, on_device(): chunks.append(lax.all_to_all(expert_out, GROUP, 1, 1, tiled=True))  28.6 us
    all_to_all x6, starting transfers between devices, rep_gather(): return lax.all_to_all(copies, REP, 0, 0, tiled=True)  24.6 us
    dot_general x3, matrix products, on_device(): lax.dot_general(rows, gate_units, contract, preferred_element_type=jnp.fl...  9.37 us
    unnamed x34, local copies, waits for them, and re-layouts  8.77 us
  transfers between devices with their start and end apart: 15, of which 12 were waited for; matrix products, arithmetic and copies ran while one was open for 12% of the time, Pallas kernels for 0%

profile of v8, /device:TPU:6, one launch (start us, length us, event | category | flops | bytes accessed | tf_op | source)
XLA Modules:
  0.0 321.0 jit_solution(13071724422286506732)
XLA Ops:
  9.7 18.8 %all-to-all-start = ((bf16[64,2,1440]{2,1,0:T(2,128)(2,1)}), bf16[64,2,1440]{2,1,0:T(2,128)(2,1)S(1)}, u32[]{:S(2)}, u32[]{:S(2)}) async-start(bf16[64,2,1440]{2,1,0:T(2,128)(2,1)} %reshape.256), calls=%async_computation | async-start | bytes 786432 | tf_op jit(solution)/shard_map/all_to_all | solution.py:60
  30.6 24.2 %all-to-all-done = bf16[64,2,1440]{2,1,0:T(2,128)(2,1)S(1)} async-done(((bf16[64,2,1440]{2,1,0:T(2,128)(2,1)}), bf16[64,2,1440]{2,1,0:T(2,128)(2,1)S(1)}, u32[]{:S(2)}, u32[]{:S(2)}) %all-to-all-start) | async-done | bytes 368672 | tf_op jit(solution)/shard_map/all_to_all | solution.py:60
  54.8 6.6 %all-to-all-start.8 = ((bf16[64,2,1440]{2,1,0:T(2,128)(2,1)}), bf16[64,2,1440]{2,1,0:T(2,128)(2,1)S(1)}, u32[]{:S(2)}, u32[]{:S(2)}) async-start(bf16[64,2,1440]{2,1,0:T(2,128)(2,1)} %reshape.252), calls=%async_computation.8 | async-start | bytes 786432 | tf_op jit(solution)/shard_map/all_to_all | solution.py:60
  63.5 23.5 %all-to-all-done.8 = bf16[64,2,1440]{2,1,0:T(2,128)(2,1)S(1)} async-done(((bf16[64,2,1440]{2,1,0:T(2,128)(2,1)}), bf16[64,2,1440]{2,1,0:T(2,128)(2,1)S(1)}, u32[]{:S(2)}, u32[]{:S(2)}) %all-to-all-start.8) | async-done | bytes 368672 | tf_op jit(solution)/shard_map/all_to_all | solution.py:60
  87.1 6.8 %all-to-all-start.4 = ((bf16[64,2,1440]{2,1,0:T(2,128)(2,1)}), bf16[64,2,1440]{2,1,0:T(2,128)(2,1)S(1)}, u32[]{:S(2)}, u32[]{:S(2)}) async-start(bf16[64,2,1440]{2,1,0:T(2,128)(2,1)} %reshape.254), calls=%async_computation.4 | async-start | bytes 786432 | tf_op jit(solution)/shard_map/all_to_all | solution.py:60
  94.5 24.8 %all-to-all-done.4 = bf16[64,2,1440]{2,1,0:T(2,128)(2,1)S(1)} async-done(((bf16[64,2,1440]{2,1,0:T(2,128)(2,1)}), bf16[64,2,1440]{2,1,0:T(2,128)(2,1)S(1)}, u32[]{:S(2)}, u32[]{:S(2)}) %all-to-all-start.4) | async-done | bytes 368672 | tf_op jit(solution)/shard_map/all_to_all | solution.py:60
  120.5 4.5 %all-to-all-start.9 = ((bf16[4,64,1,2880]{3,1,2,0:T(8,128)(2,1)}), bf16[4,64,1,2880]{3,1,2,0:T(8,128)(2,1)S(1)}, u32[]{:S(2)}, u32[]{:S(2)}) async-start(bf16[4,64,1,2880]{3,1,2,0:T(8,128)(2,1)} %broadcast_in_dim.62), calls=%async_computation.9 | async-start | bytes 3014656 | tf_op jit(solution)/shard_map/all_to_all | solution.py:14
  125.6 16.5 %all-to-all-done.9 = bf16[4,64,1,2880]{3,1,2,0:T(8,128)(2,1)S(1)} async-done(((bf16[4,64,1,2880]{3,1,2,0:T(8,128)(2,1)}), bf16[4,64,1,2880]{3,1,2,0:T(8,128)(2,1)S(1)}, u32[]{:S(2)}, u32[]{:S(2)}) %all-to-all-start.9) | async-done | bytes 1474592 | tf_op jit(solution)/shard_map/all_to_all | solution.py:14
  143.7 4.5 %all-to-all-start.1 = ((bf16[4,64,1,2880]{3,1,2,0:T(8,128)(2,1)}), bf16[4,64,1,2880]{3,1,2,0:T(8,128)(2,1)}, u32[]{:S(2)}, u32[]{:S(2)}) async-start(bf16[4,64,1,2880]{3,1,2,0:T(8,128)(2,1)} %broadcast_in_dim.27), calls=%async_computation.1 | async-start | bytes 3014656 | tf_op jit(solution)/shard_map/all_to_all | solution.py:14
  155.1 9.2 %all-to-all-done.1 = bf16[4,64,1,2880]{3,1,2,0:T(8,128)(2,1)} async-done(((bf16[4,64,1,2880]{3,1,2,0:T(8,128)(2,1)}), bf16[4,64,1,2880]{3,1,2,0:T(8,128)(2,1)}, u32[]{:S(2)}, u32[]{:S(2)}) %all-to-all-start.1) | async-done | bytes 1474592 | tf_op jit(solution)/shard_map/all_to_all | solution.py:14
  165.5 4.5 %all-to-all-start.5 = ((bf16[4,64,1,2880]{3,1,2,0:T(8,128)(2,1)}), bf16[4,64,1,2880]{3,1,2,0:T(8,128)(2,1)}, u32[]{:S(2)}, u32[]{:S(2)}) async-start(bf16[4,64,1,2880]{3,1,2,0:T(8,128)(2,1)} %broadcast_in_dim.30), calls=%async_computation.5 | async-start | bytes 3014656 | tf_op jit(solution)/shard_map/all_to_all | solution.py:14
  178.3 6.4 %all-to-all-done.5 = bf16[4,64,1,2880]{3,1,2,0:T(8,128)(2,1)} async-done(((bf16[4,64,1,2880]{3,1,2,0:T(8,128)(2,1)}), bf16[4,64,1,2880]{3,1,2,0:T(8,128)(2,1)}, u32[]{:S(2)}, u32[]{:S(2)}) %all-to-all-start.5) | async-done | bytes 1474592 | tf_op jit(solution)/shard_map/all_to_all | solution.py:14
  185.7 3.5 %all-to-all-start.2 = ((bf16[4,256,384]{2,1,0:T(8,128)(2,1)}), bf16[4,256,384]{2,1,0:T(8,128)(2,1)S(1)}, u32[]{:S(2)}, u32[]{:S(2)}) async-start(bf16[4,256,384]{2,1,0:T(8,128)(2,1)} %broadcast_in_dim.28), calls=%async_computation.2 | async-start | bytes 1572864 | tf_op jit(solution)/shard_map/all_to_all | solution.py:14
  194.7 4.0 %all-to-all-done.2 = bf16[4,256,384]{2,1,0:T(8,128)(2,1)S(1)} async-done(((bf16[4,256,384]{2,1,0:T(8,128)(2,1)}), bf16[4,256,384]{2,1,0:T(8,128)(2,1)S(1)}, u32[]{:S(2)}, u32[]{:S(2)}) %all-to-all-start.2) | async-done | bytes 786464 | tf_op jit(solution)/shard_map/all_to_all | solution.py:14
  199.8 3.5 %all-to-all-start.10 = ((bf16[4,256,384]{2,1,0:T(8,128)(2,1)}), bf16[4,256,384]{2,1,0:T(8,128)(2,1)S(1)}, u32[]{:S(2)}, u32[]{:S(2)}) async-start(bf16[4,256,384]{2,1,0:T(8,128)(2,1)} %broadcast_in_dim.63), calls=%async_computation.10 | async-start | bytes 1572864 | tf_op jit(solution)/shard_map/all_to_all | solution.py:14
  209.2 3.6 %all-to-all-done.10 = bf16[4,256,384]{2,1,0:T(8,128)(2,1)S(1)} async-done(((bf16[4,256,384]{2,1,0:T(8,128)(2,1)}), bf16[4,256,384]{2,1,0:T(8,128)(2,1)S(1)}, u32[]{:S(2)}, u32[]{:S(2)}) %all-to-all-start.10) | async-done | bytes 786464 | tf_op jit(solution)/shard_map/all_to_all | solution.py:14
  213.8 4.2 %all-to-all-start.6 = ((bf16[4,256,384]{2,1,0:T(8,128)(2,1)}), bf16[4,256,384]{2,1,0:T(8,128)(2,1)}, u32[]{:S(2)}, u32[]{:S(2)}) async-start(bf16[4,256,384]{2,1,0:T(8,128)(2,1)} %broadcast_in_dim.60), calls=%async_computation.6 | async-start | bytes 1572864 | tf_op jit(solution)/shard_map/all_to_all | solution.py:14
  222.5 5.0 %all-to-all-done.6 = bf16[4,256,384]{2,1,0:T(8,128)(2,1)} async-done(((bf16[4,256,384]{2,1,0:T(8,128)(2,1)}), bf16[4,256,384]{2,1,0:T(8,128)(2,1)}, u32[]{:S(2)}, u32[]{:S(2)}) %all-to-all-start.6) | async-done | bytes 786464 | tf_op jit(solution)/shard_map/all_to_all | solution.py:14
  227.5 14.8 %all-to-all-start.3 = ((bf16[4,64,720]{2,0,1:T(4,128)(2,1)}), bf16[4,64,720]{2,0,1:T(4,128)(2,1)S(1)}, u32[]{:S(2)}, u32[]{:S(2)}) async-start(bf16[4,64,720]{2,0,1:T(4,128)(2,1)} %copy.63), calls=%async_computation.3 | async-start | bytes 786432 | tf_op jit(solution)/shard_map/all_to_all | solution.py:72
  245.7 16.0 %all-to-all-done.3 = bf16[4,64,720]{2,0,1:T(4,128)(2,1)S(1)} async-done(((bf16[4,64,720]{2,0,1:T(4,128)(2,1)}), bf16[4,64,720]{2,0,1:T(4,128)(2,1)S(1)}, u32[]{:S(2)}, u32[]{:S(2)}) %all-to-all-start.3) | async-done | bytes 368672 | tf_op jit(solution)/shard_map/all_to_all | solution.py:72
  261.7 7.1 %all-to-all-start.7 = ((bf16[4,64,720]{2,0,1:T(4,128)(2,1)}), bf16[4,64,720]{2,0,1:T(4,128)(2,1)S(1)}, u32[]{:S(2)}, u32[]{:S(2)}) async-start(bf16[4,64,720]{2,0,1:T(4,128)(2,1)} %copy.67), calls=%async_computation.7 | async-start | bytes 786432 | tf_op jit(solution)/shard_map/all_to_all | solution.py:72
  272.2 16.4 %all-to-all-done.7 = bf16[4,64,720]{2,0,1:T(4,128)(2,1)S(1)} async-done(((bf16[4,64,720]{2,0,1:T(4,128)(2,1)}), bf16[4,64,720]{2,0,1:T(4,128)(2,1)S(1)}, u32[]{:S(2)}, u32[]{:S(2)}) %all-to-all-start.7) | async-done | bytes 368672 | tf_op jit(solution)/shard_map/all_to_all | solution.py:72
  288.6 6.7 %all-to-all-start.11 = ((bf16[4,64,720]{2,0,1:T(4,128)(2,1)}), bf16[4,64,720]{2,0,1:T(4,128)(2,1)S(1)}, u32[]{:S(2)}, u32[]{:S(2)}) async-start(bf16[4,64,720]{2,0,1:T(4,128)(2,1)} %copy.71), calls=%async_computation.11 | async-start | bytes 786432 | tf_op jit(solution)/shard_map/all_to_all | solution.py:72
  295.5 20.0 %all-to-all-done.11 = bf16[4,64,720]{2,0,1:T(4,128)(2,1)S(1)} async-done(((bf16[4,64,720]{2,0,1:T(4,128)(2,1)}), bf16[4,64,720]{2,0,1:T(4,128)(2,1)S(1)}, u32[]{:S(2)}, u32[]{:S(2)}) %all-to-all-start.11) | async-done | bytes 368672 | tf_op jit(solution)/shard_map/all_to_all | solution.py:72
  (98 shorter events, 65.4 us)
Async XLA Ops:
  0.0 5.4 %copy-start.6 = (bf16[128,2880]{0,1:T(8,128)(2,1)S(1)}, bf16[128,2880]{0,1:T(8,128)(2,1)}, u32[]{:S(2)}) copy-start(bf16[128,2880]{0,1:T(8,128)(2,1)} %param.6) | copy-start | bytes 2211844
  9.7 45.1 %all-to-all-start = ((bf16[64,2,1440]{2,1,0:T(2,128)(2,1)}), bf16[64,2,1440]{2,1,0:T(2,128)(2,1)S(1)}, u32[]{:S(2)}, u32[]{:S(2)}) async-start(bf16[64,2,1440]{2,1,0:T(2,128)(2,1)} %reshape.256), calls=%async_computation | async-start | bytes 786432 | tf_op jit(solution)/shard_map/all_to_all | solution.py:60
  54.8 32.2 %all-to-all-start.8 = ((bf16[64,2,1440]{2,1,0:T(2,128)(2,1)}), bf16[64,2,1440]{2,1,0:T(2,128)(2,1)S(1)}, u32[]{:S(2)}, u32[]{:S(2)}) async-start(bf16[64,2,1440]{2,1,0:T(2,128)(2,1)} %reshape.252), calls=%async_computation.8 | async-start | bytes 786432 | tf_op jit(solution)/shard_map/all_to_all | solution.py:60
  87.1 32.2 %all-to-all-start.4 = ((bf16[64,2,1440]{2,1,0:T(2,128)(2,1)}), bf16[64,2,1440]{2,1,0:T(2,128)(2,1)S(1)}, u32[]{:S(2)}, u32[]{:S(2)}) async-start(bf16[64,2,1440]{2,1,0:T(2,128)(2,1)} %reshape.254), calls=%async_computation.4 | async-start | bytes 786432 | tf_op jit(solution)/shard_map/all_to_all | solution.py:60
  120.5 21.6 %all-to-all-start.9 = ((bf16[4,64,1,2880]{3,1,2,0:T(8,128)(2,1)}), bf16[4,64,1,2880]{3,1,2,0:T(8,128)(2,1)S(1)}, u32[]{:S(2)}, u32[]{:S(2)}) async-start(bf16[4,64,1,2880]{3,1,2,0:T(8,128)(2,1)} %broadcast_in_dim.62), calls=%async_computation.9 | async-start | bytes 3014656 | tf_op jit(solution)/shard_map/all_to_all | solution.py:14
  142.1 1.6 copy-start
  143.5 4.7 %copy-start.2 = (bf16[1,1536,360]{1,2,0:T(8,128)(2,1)S(1)}, bf16[1,1536,360]{1,2,0:T(8,128)(2,1)}, u32[]{:S(2)}) copy-start(bf16[1,1536,360]{1,2,0:T(8,128)(2,1)} %param.11) | copy-start | bytes 3317764
  143.7 20.5 %all-to-all-start.1 = ((bf16[4,64,1,2880]{3,1,2,0:T(8,128)(2,1)}), bf16[4,64,1,2880]{3,1,2,0:T(8,128)(2,1)}, u32[]{:S(2)}, u32[]{:S(2)}) async-start(bf16[4,64,1,2880]{3,1,2,0:T(8,128)(2,1)} %broadcast_in_dim.27), calls=%async_computation.1 | async-start | bytes 3014656 | tf_op jit(solution)/shard_map/all_to_all | solution.py:14
  148.2 22.6 %collective-permute-start.2 = (bf16[1536,360]{0,1:T(8,128)(2,1)S(1)}, bf16[1536,360]{0,1:T(8,128)(2,1)}, u32[]{:S(2)}, u32[]{:S(2)}) collective-permute-start(bf16[1536,360]{0,1:T(8,128)(2,1)S(1)} %bitcast.102), channel_id=1, source_target_pairs={{0,1},{1,0},{2,3},{3,2},{4,5},{5,4},{6,7},{7,6},{8,9},{9,8},{10,11... | collective-permute-start | bytes 3317768 | tf_op jit(solution)/shard_map/ppermute | solution.py:46
  150.1 22.4 %collective-permute-start.1 = (bf16[192,2880]{1,0:T(8,128)(2,1)}, bf16[192,2880]{1,0:T(8,128)(2,1)}, u32[]{:S(2)}, u32[]{:S(2)}) collective-permute-start(bf16[192,2880]{1,0:T(8,128)(2,1)} %bitcast.109), channel_id=1, source_target_pairs={{0,1},{1,0},{2,3},{3,2},{4,5},{5,4},{6,7},{7,6},{8,9},{9,8},{10,11... | collective-permute-start | bytes 3317768 | tf_op jit(solution)/shard_map/ppermute | solution.py:46
  152.5 23.1 %collective-permute-start = (bf16[192,2880]{1,0:T(8,128)(2,1)}, bf16[192,2880]{1,0:T(8,128)(2,1)}, u32[]{:S(2)}, u32[]{:S(2)}) collective-permute-start(bf16[192,2880]{1,0:T(8,128)(2,1)} %bitcast.113), channel_id=1, source_target_pairs={{0,1},{1,0},{2,3},{3,2},{4,5},{5,4},{6,7},{7,6},{8,9},{9,8},{10,11... | collective-permute-start | bytes 3317768 | tf_op jit(solution)/shard_map/ppermute | solution.py:46
  165.5 19.2 %all-to-all-start.5 = ((bf16[4,64,1,2880]{3,1,2,0:T(8,128)(2,1)}), bf16[4,64,1,2880]{3,1,2,0:T(8,128)(2,1)}, u32[]{:S(2)}, u32[]{:S(2)}) async-start(bf16[4,64,1,2880]{3,1,2,0:T(8,128)(2,1)} %broadcast_in_dim.30), calls=%async_computation.5 | async-start | bytes 3014656 | tf_op jit(solution)/shard_map/all_to_all | solution.py:14
  172.5 3.1 copy-start.8
  185.7 13.0 %all-to-all-start.2 = ((bf16[4,256,384]{2,1,0:T(8,128)(2,1)}), bf16[4,256,384]{2,1,0:T(8,128)(2,1)S(1)}, u32[]{:S(2)}, u32[]{:S(2)}) async-start(bf16[4,256,384]{2,1,0:T(8,128)(2,1)} %broadcast_in_dim.28), calls=%async_computation.2 | async-start | bytes 1572864 | tf_op jit(solution)/shard_map/all_to_all | solution.py:14
  189.2 3.2 copy-start.1
  189.2 3.2 copy-start.9
  199.8 13.0 %all-to-all-start.10 = ((bf16[4,256,384]{2,1,0:T(8,128)(2,1)}), bf16[4,256,384]{2,1,0:T(8,128)(2,1)S(1)}, u32[]{:S(2)}, u32[]{:S(2)}) async-start(bf16[4,256,384]{2,1,0:T(8,128)(2,1)} %broadcast_in_dim.63), calls=%async_computation.10 | async-start | bytes 1572864 | tf_op jit(solution)/shard_map/all_to_all | solution.py:14
  203.3 3.1 copy-start.10
  212.8 6.1 %copy-start.3 = (bf16[4,256,384]{2,1,0:T(8,128)(2,1)}, bf16[4,256,384]{2,1,0:T(8,128)(2,1)S(1)}, u32[]{:S(2)}) copy-start(bf16[4,256,384]{2,1,0:T(8,128)(2,1)S(1)} %all-to-all-done.10) | copy-start | bytes 2359300
  213.8 13.7 %all-to-all-start.6 = ((bf16[4,256,384]{2,1,0:T(8,128)(2,1)}), bf16[4,256,384]{2,1,0:T(8,128)(2,1)}, u32[]{:S(2)}, u32[]{:S(2)}) async-start(bf16[4,256,384]{2,1,0:T(8,128)(2,1)} %broadcast_in_dim.60), calls=%async_computation.6 | async-start | bytes 1572864 | tf_op jit(solution)/shard_map/all_to_all | solution.py:14
  227.5 34.1 %all-to-all-start.3 = ((bf16[4,64,720]{2,0,1:T(4,128)(2,1)}), bf16[4,64,720]{2,0,1:T(4,128)(2,1)S(1)}, u32[]{:S(2)}, u32[]{:S(2)}) async-start(bf16[4,64,720]{2,0,1:T(4,128)(2,1)} %copy.63), calls=%async_computation.3 | async-start | bytes 786432 | tf_op jit(solution)/shard_map/all_to_all | solution.py:72
  261.7 27.0 %all-to-all-start.7 = ((bf16[4,64,720]{2,0,1:T(4,128)(2,1)}), bf16[4,64,720]{2,0,1:T(4,128)(2,1)S(1)}, u32[]{:S(2)}, u32[]{:S(2)}) async-start(bf16[4,64,720]{2,0,1:T(4,128)(2,1)} %copy.67), calls=%async_computation.7 | async-start | bytes 786432 | tf_op jit(solution)/shard_map/all_to_all | solution.py:72
  271.0 24.3 %copy-start.7 = (s32[128,4]{0,1:T(4,128)S(1)}, s32[128,4]{0,1:T(4,128)}, u32[]{:S(2)}) copy-start(s32[128,4]{0,1:T(4,128)} %param.8) | copy-start | bytes 6148
  288.6 26.9 %all-to-all-start.11 = ((bf16[4,64,720]{2,0,1:T(4,128)(2,1)}), bf16[4,64,720]{2,0,1:T(4,128)(2,1)S(1)}, u32[]{:S(2)}, u32[]{:S(2)}) async-start(bf16[4,64,720]{2,0,1:T(4,128)(2,1)} %copy.71), calls=%async_computation.11 | async-start | bytes 786432 | tf_op jit(solution)/shard_map/all_to_all | solution.py:72
  (2 other events, 2.3 us)

commit v9 on v3

--- a/solution.py
+++ b/solution.py
@@ -28,14 +28,17 @@
     )
     rank_counts = jnp.cumsum(onehot, axis=0) - onehot
     slot_index = jnp.sum(rank_counts * onehot, axis=1)
-    source_rows = jnp.arange(tok_rows * top_count, dtype=jnp.int32) // top_count
 
     local_slot = slot_index - part * rep_index
     in_part = (local_slot >= 0) & (local_slot < part)
     send_slots = expert_count * part
     position = jnp.where(in_part, local_slot * expert_count + flat_ids, send_slots)
-    table = jnp.zeros((send_slots,), jnp.int32).at[position].set(source_rows, mode="drop")
-    outgoing = tokens[table].reshape(part, expert_count, 1, model_width)
+    hits = position.reshape(tok_rows, top_count)[None, :, :] == jnp.arange(
+        send_slots, dtype=jnp.int32
+    )[:, None, None]
+    select = jnp.any(hits, axis=2).astype(tokens.dtype)
+    outgoing = jnp.dot(select, tokens, preferred_element_type=jnp.float32).astype(tokens.dtype)
+    outgoing = outgoing.reshape(part, expert_count, 1, model_width)
 
     swap = [(0, 1), (1, 0)]
     other_gate, other_up, other_down = lax.ppermute((w_gate[0], w_up[0], w_down[0]), CORE, swap)

time: 268 us -> 276 us (1.030)
  matrix products: 19.4 us -> 23.4 us
    convert_element_type x3, local copies, waits for them, and re-layouts: 0.51 us -> 4.26 us  [on_device(): projected.astype(jnp.bfloat16).reshape(n_rep, expert_count, col_count)]
    unnamed x27 -> x28, local copies, waits for them, and re-layouts: 5.75 us -> 5.4 us
  transfers between devices with their start and end apart: 10 -> 10, of which waited for: 2 -> 2; matrix products, arithmetic and copies ran while one was open for 12% -> 16% of each run, Pallas kernels for 0% -> 0%
where the time goes in v9:
time: 276 us; the launch traced here: 275 us
  blocking collectives  121 us (44%)
  starting transfers between devices  49.8 us (18%)
  waiting for transfers between devices  32.9 us (12%)
  local copies, waits for them, and re-layouts  23.8 us (9%)
  matrix products  23.4 us (8%)
  between operations  13.6 us (5%)
  other arithmetic  9.97 us (4%)
    all_to_all x2, blocking collectives, on_device(): arrived = lax.all_to_all(outgoing[chunk], GROUP, 0, 0, tiled=True)  76.9 us
    all_gather x3, blocking collectives, on_device(): hidden_all = lax.all_gather(hidden, REP, axis=0, tiled=False)  44.6 us
    all_to_all x3, starting transfers between devices, on_device(): chunks.append(lax.all_to_all(expert_out, GROUP, 1, 1, tiled=True))  36.7 us
    all_to_all x3, waiting for transfers between devices, on_device(): chunks.append(lax.all_to_all(expert_out, GROUP, 1, 1, tiled=True))  18.9 us
    all_to_all x1, waiting for transfers between devices, on_device(): arrived = lax.all_to_all(outgoing[chunk], GROUP, 0, 0, tiled=True)  13.9 us
    dot_general x3, matrix products, on_device(): lax.dot_general(rows, gate_units, contract, preferred_element_type=jnp.fl...  9.5 us
    dot_general x3, matrix products, on_device(): lax.dot_general(rows, up_units, contract, preferred_element_type=jnp.floa...  7.96 us
    all_to_all x1, starting transfers between devices, on_device(): arrived = lax.all_to_all(outgoing[chunk], GROUP, 0, 0, tiled=True)  6.78 us
  transfers between devices with their start and end apart: 10, of which 2 were waited for; matrix products, arithmetic and copies ran while one was open for 16% of the time, Pallas kernels for 0%

profile of v9, /device:TPU:6, one launch (start us, length us, event | category | flops | bytes accessed | tf_op | source)
XLA Modules:
  0.0 274.9 jit_solution(12884047037351689964)
XLA Ops:
  13.1 44.9 %all_to_all.30 = bf16[64,2,1440]{2,1,0:T(2,128)(2,1)S(1)} all-to-all(bf16[64,2,1440]{2,1,0:T(2,128)(2,1)S(1)} %reshape.204), channel_id=1, replica_groups=mesh['rep'=4,'grp'=64,'core'=2] {'grp'}, dimensions={0} | all-to-all | bytes 737280 | tf_op jit(solution)/shard_map/all_to_all | solution.py:58
  60.7 32.0 %all_to_all.31 = bf16[64,2,1440]{2,1,0:T(2,128)(2,1)S(1)} all-to-all(bf16[64,2,1440]{2,1,0:T(2,128)(2,1)S(1)} %reshape.202), channel_id=1, replica_groups=mesh['rep'=4,'grp'=64,'core'=2] {'grp'}, dimensions={0} | all-to-all | bytes 737280 | tf_op jit(solution)/shard_map/all_to_all | solution.py:58
  96.3 6.8 %all-to-all-start.4 = ((bf16[64,2,1440]{2,1,0:T(2,128)(2,1)}), bf16[64,2,1440]{2,1,0:T(2,128)(2,1)S(1)}, u32[]{:S(2)}, u32[]{:S(2)}) async-start(bf16[64,2,1440]{2,1,0:T(2,128)(2,1)} %reshape.200), calls=%async_computation.4 | async-start | bytes 786432 | tf_op jit(solution)/shard_map/all_to_all | solution.py:58
  103.1 1.9 collective-permute-start.2
  105.0 2.4 collective-permute-start.1
  107.4 1.9 collective-permute-start
  114.6 13.9 %all-to-all-done.4 = bf16[64,2,1440]{2,1,0:T(2,128)(2,1)S(1)} async-done(((bf16[64,2,1440]{2,1,0:T(2,128)(2,1)}), bf16[64,2,1440]{2,1,0:T(2,128)(2,1)S(1)}, u32[]{:S(2)}, u32[]{:S(2)}) %all-to-all-start.4) | async-done | bytes 368672 | tf_op jit(solution)/shard_map/all_to_all | solution.py:58
  129.8 3.3 %fusion.8 = f32[256,384]{1,0:T(8,128)S(1)} fusion(bf16[256,1,2880]{2,0,1:T(8,128)(2,1)} %all-gather.10.cloned.1.call-done, bf16[192,2880]{1,0:T(8,128)(2,1)} %collective-permute-done.1, bf16[192,2880]{1,0:T(8,128)(2,1)} %bitcast.4), kind=kOutput, calls=%fused_computation.18 | convolution fusion | flops 570654720 | bytes 4079616 | tf_op jit(solution)/shard_map/dot_general | solution.py:60
  133.1 2.8 %fusion.52 = bf16[256,384]{1,0:T(8,128)(2,1)S(1)} fusion(f32[256,384]{1,0:T(8,128)S(1)} %fusion.8, bf16[256,1,2880]{2,0,1:T(8,128)(2,1)S(1)} %copy-done.8, bf16[192,2880]{1,0:T(8,128)(2,1)} %collective-permute-done, bf16[192,2880]{1,0:T(8,128)(2,1)} %bitcast.3), kind=kOutput, calls=%fused_computation.44 | convolution fusion | flops 571441152 | bytes 4276224 | tf_op jit(solution)/shard_map/dot_general | solution.py:61
  135.9 17.5 %all-gather.1 = bf16[1024,384]{1,0:T(8,128)(2,1)S(1)} all-gather(bf16[256,384]{1,0:T(8,128)(2,1)S(1)} %fusion.52), channel_id=3, replica_groups=mesh['rep'=4,'grp'=64,'core'=2] {'rep'}, dimensions={0}, use_global_device_ids=true | all-gather | bytes 983040 | tf_op jit(solution)/shard_map/all_gather | solution.py:65
  157.4 6.2 %all-to-all-start.1 = ((bf16[4,64,720]{2,0,1:T(4,128)(2,1)}), bf16[4,64,720]{2,0,1:T(4,128)(2,1)S(1)}, u32[]{:S(2)}, u32[]{:S(2)}) async-start(bf16[4,64,720]{2,0,1:T(4,128)(2,1)} %copy.120), calls=%async_computation.1 | async-start | bytes 786432 | tf_op jit(solution)/shard_map/all_to_all | solution.py:70
  163.7 3.1 %fusion.4 = f32[256,384]{1,0:T(8,128)S(1)} fusion(bf16[256,1,2880]{2,0,1:T(8,128)(2,1)} %all-gather.12.cloned.1.call-done, bf16[192,2880]{1,0:T(8,128)(2,1)} %collective-permute-done.1, bf16[192,2880]{1,0:T(8,128)(2,1)} %bitcast.4), kind=kOutput, calls=%fused_computation.14 | convolution fusion | flops 570654720 | bytes 4079616 | tf_op jit(solution)/shard_map/dot_general | solution.py:60
  166.8 2.6 fusion.49
  169.5 13.8 %all-gather.3 = bf16[1024,384]{1,0:T(8,128)(2,1)S(1)} all-gather(bf16[256,384]{1,0:T(8,128)(2,1)S(1)} %fusion.49), channel_id=5, replica_groups=mesh['rep'=4,'grp'=64,'core'=2] {'rep'}, dimensions={0}, use_global_device_ids=true | all-gather | bytes 983040 | tf_op jit(solution)/shard_map/all_gather | solution.py:65
  185.0 1.9 copy.125
  187.0 2.1 copy.126
  189.0 15.3 %all-to-all-start.3 = ((bf16[4,64,720]{2,0,1:T(4,128)(2,1)}), bf16[4,64,720]{2,0,1:T(4,128)(2,1)}, u32[]{:S(2)}, u32[]{:S(2)}) async-start(bf16[4,64,720]{2,0,1:T(4,128)(2,1)} %copy.126), calls=%async_computation.3 | async-start | bytes 786432 | tf_op jit(solution)/shard_map/all_to_all | solution.py:70
  204.4 3.1 %fusion = f32[256,384]{1,0:T(8,128)S(1)} fusion(bf16[256,1,2880]{2,0,1:T(8,128)(2,1)} %all-gather.14.cloned.1.call-done, bf16[192,2880]{1,0:T(8,128)(2,1)} %collective-permute-done.1, bf16[192,2880]{1,0:T(8,128)(2,1)} %bitcast.4), kind=kOutput, calls=%fused_computation.10 | convolution fusion | flops 570654720 | bytes 4079616 | tf_op jit(solution)/shard_map/dot_general | solution.py:60
  207.5 2.6 fusion.46
  210.1 13.3 %all-gather.5 = bf16[1024,384]{1,0:T(8,128)(2,1)S(1)} all-gather(bf16[256,384]{1,0:T(8,128)(2,1)S(1)} %fusion.46), channel_id=7, replica_groups=mesh['rep'=4,'grp'=64,'core'=2] {'rep'}, dimensions={0}, use_global_device_ids=true | all-gather | bytes 983040 | tf_op jit(solution)/shard_map/all_gather | solution.py:65
  227.5 15.1 %all-to-all-start.5 = ((bf16[4,64,720]{2,0,1:T(4,128)(2,1)}), bf16[4,64,720]{2,0,1:T(4,128)(2,1)S(1)}, u32[]{:S(2)}, u32[]{:S(2)}) async-start(bf16[4,64,720]{2,0,1:T(4,128)(2,1)} %copy.132), calls=%async_computation.5 | async-start | bytes 786432 | tf_op jit(solution)/shard_map/all_to_all | solution.py:70
  243.0 18.9 %all-to-all-done.5 = bf16[4,64,720]{2,0,1:T(4,128)(2,1)S(1)} async-done(((bf16[4,64,720]{2,0,1:T(4,128)(2,1)}), bf16[4,64,720]{2,0,1:T(4,128)(2,1)S(1)}, u32[]{:S(2)}, u32[]{:S(2)}) %all-to-all-start.5) | async-done | bytes 368672 | tf_op jit(solution)/shard_map/all_to_all | solution.py:70
  261.8 2.0 pad_maximum_fusion.3
  264.0 2.0 gather_fusion
  (88 shorter events, 31.9 us)
Async XLA Ops:
  6.5 4.2 %copy-start = (bf16[128,2880]{0,1:T(8,128)(2,1)S(1)}, bf16[128,2880]{0,1:T(8,128)(2,1)}, u32[]{:S(2)}) copy-start(bf16[128,2880]{0,1:T(8,128)(2,1)} %param.6) | copy-start | bytes 2211844
  6.5 123.3 %all-gather.10.cloned.1.call-start = ((), (), s32[]{:S(2)}) async-start(), calls=%async_computation.6 | async-start | bytes 1884160 | tf_op jit(solution)/shard_map/all_gather | solution.py:59
  59.4 104.3 %all-gather.12.cloned.1.call-start = ((), (), s32[]{:S(2)}) async-start(), calls=%async_computation.7 | async-start | bytes 1884160 | tf_op jit(solution)/shard_map/all_gather | solution.py:59
  94.1 9.0 %copy-start.2 = (bf16[1,1536,360]{1,2,0:T(8,128)(2,1)S(1)}, bf16[1,1536,360]{1,2,0:T(8,128)(2,1)}, u32[]{:S(2)}) copy-start(bf16[1,1536,360]{1,2,0:T(8,128)(2,1)} %param.11) | copy-start | bytes 3317764
  96.3 32.2 %all-to-all-start.4 = ((bf16[64,2,1440]{2,1,0:T(2,128)(2,1)}), bf16[64,2,1440]{2,1,0:T(2,128)(2,1)S(1)}, u32[]{:S(2)}, u32[]{:S(2)}) async-start(bf16[64,2,1440]{2,1,0:T(2,128)(2,1)} %reshape.200), calls=%async_computation.4 | async-start | bytes 786432 | tf_op jit(solution)/shard_map/all_to_all | solution.py:58
  103.0 101.3 %all-gather.14.cloned.1.call-start = ((), (), s32[]{:S(2)}) async-start(), calls=%async_computation.8 | async-start | bytes 1884160 | tf_op jit(solution)/shard_map/all_gather | solution.py:59
  103.1 7.0 %collective-permute-start.2 = (bf16[1536,360]{0,1:T(8,128)(2,1)S(1)}, bf16[1536,360]{0,1:T(8,128)(2,1)}, u32[]{:S(2)}, u32[]{:S(2)}) collective-permute-start(bf16[1536,360]{0,1:T(8,128)(2,1)S(1)} %bitcast.125), channel_id=1, source_target_pairs={{0,1},{1,0},{2,3},{3,2},{4,5},{5,4},{6,7},{7,6},{8,9},{9,8},{10,11... | collective-permute-start | bytes 3317768 | tf_op jit(solution)/shard_map/ppermute | solution.py:44
  105.0 24.8 %collective-permute-start.1 = (bf16[192,2880]{1,0:T(8,128)(2,1)}, bf16[192,2880]{1,0:T(8,128)(2,1)}, u32[]{:S(2)}, u32[]{:S(2)}) collective-permute-start(bf16[192,2880]{1,0:T(8,128)(2,1)} %bitcast.4), channel_id=1, source_target_pairs={{0,1},{1,0},{2,3},{3,2},{4,5},{5,4},{6,7},{7,6},{8,9},{9,8},{10,11... | collective-permute-start | bytes 3317768 | tf_op jit(solution)/shard_map/ppermute | solution.py:44
  107.4 25.7 %collective-permute-start = (bf16[192,2880]{1,0:T(8,128)(2,1)}, bf16[192,2880]{1,0:T(8,128)(2,1)}, u32[]{:S(2)}, u32[]{:S(2)}) collective-permute-start(bf16[192,2880]{1,0:T(8,128)(2,1)} %bitcast.3), channel_id=1, source_target_pairs={{0,1},{1,0},{2,3},{3,2},{4,5},{5,4},{6,7},{7,6},{8,9},{9,8},{10,11... | collective-permute-start | bytes 3317768 | tf_op jit(solution)/shard_map/ppermute | solution.py:44
  129.8 3.3 %copy-start.8 = (bf16[256,1,2880]{2,0,1:T(8,128)(2,1)S(1)}, bf16[256,1,2880]{2,0,1:T(8,128)(2,1)}, u32[]{:S(2)}) copy-start(bf16[256,1,2880]{2,0,1:T(8,128)(2,1)} %all-gather.10.cloned.1.call-done) | copy-start | bytes 4423684
  133.1 20.3 %copy-start.1 = (bf16[4,2,192,720]{3,2,1,0:T(8,128)(2,1)S(1)}, bf16[4,2,192,720]{3,2,1,0:T(8,128)(2,1)}, u32[]{:S(2)}) copy-start(bf16[4,2,192,720]{3,2,1,0:T(8,128)(2,1)} %copy.117) | copy-start | bytes 6635524
  157.4 31.6 %all-to-all-start.1 = ((bf16[4,64,720]{2,0,1:T(4,128)(2,1)}), bf16[4,64,720]{2,0,1:T(4,128)(2,1)S(1)}, u32[]{:S(2)}, u32[]{:S(2)}) async-start(bf16[4,64,720]{2,0,1:T(4,128)(2,1)} %copy.120), calls=%async_computation.1 | async-start | bytes 786432 | tf_op jit(solution)/shard_map/all_to_all | solution.py:70
  163.7 3.1 %copy-start.7 = (bf16[256,1,2880]{2,0,1:T(8,128)(2,1)S(1)}, bf16[256,1,2880]{2,0,1:T(8,128)(2,1)}, u32[]{:S(2)}) copy-start(bf16[256,1,2880]{2,0,1:T(8,128)(2,1)} %all-gather.12.cloned.1.call-done) | copy-start | bytes 4423684
  189.0 38.5 %all-to-all-start.3 = ((bf16[4,64,720]{2,0,1:T(4,128)(2,1)}), bf16[4,64,720]{2,0,1:T(4,128)(2,1)}, u32[]{:S(2)}, u32[]{:S(2)}) async-start(bf16[4,64,720]{2,0,1:T(4,128)(2,1)} %copy.126), calls=%async_computation.3 | async-start | bytes 786432 | tf_op jit(solution)/shard_map/all_to_all | solution.py:70
  204.4 3.1 %copy-start.9 = (bf16[256,1,2880]{2,0,1:T(8,128)(2,1)S(1)}, bf16[256,1,2880]{2,0,1:T(8,128)(2,1)}, u32[]{:S(2)}) copy-start(bf16[256,1,2880]{2,0,1:T(8,128)(2,1)} %all-gather.14.cloned.1.call-done) | copy-start | bytes 4423684
  225.2 17.5 %copy-start.5 = (s32[128,4]{0,1:T(4,128)S(1)}, s32[128,4]{0,1:T(4,128)}, u32[]{:S(2)}) copy-start(s32[128,4]{0,1:T(4,128)} %param.8) | copy-start | bytes 6148
  225.2 17.7 %copy-start.3 = (s32[512]{0:T(512)S(1)}, s32[512]{0:T(512)}, u32[]{:S(2)}) copy-start(s32[512]{0:T(512)} %get-tuple-element.10) | copy-start | bytes 6148
  225.2 17.7 %copy-start.4 = (s32[512]{0:T(512)S(1)}, s32[512]{0:T(512)}, u32[]{:S(2)}) copy-start(s32[512]{0:T(512)} %get-tuple-element.11) | copy-start | bytes 6148
  225.2 17.7 %copy-start.6 = (pred[512]{0:T(512)(128)(4,1)S(1)}, pred[512]{0:T(512)(128)(4,1)}, u32[]{:S(2)}) copy-start(pred[512]{0:T(512)(128)(4,1)} %get-tuple-element.13) | copy-start | bytes 1540
  227.5 34.4 %all-to-all-start.5 = ((bf16[4,64,720]{2,0,1:T(4,128)(2,1)}), bf16[4,64,720]{2,0,1:T(4,128)(2,1)S(1)}, u32[]{:S(2)}, u32[]{:S(2)}) async-start(bf16[4,64,720]{2,0,1:T(4,128)(2,1)} %copy.132), calls=%async_computation.5 | async-start | bytes 786432 | tf_op jit(solution)/shard_map/all_to_all | solution.py:70
Sparse Core Ops, SparseCore 0:
  59.5 25.8 all-gather.9
  94.2 27.0 all-gather.11
  129.9 29.4 all-gather.13
